TPU v7x, 512 devices: a whole 4x8x8 slice. The times are simulated.
512 devices in a mesh: dp: 16 (over z, core), ctx: 32 (over y, x).
Axes of the slice: x: 4, y: 8, z: 8, core: 2. Of those that a mesh axis runs over, the one named last changes fastest.
Arguments:
- positions: int32 [49152], P('dp'), parts along dimension 0, may hold values from 0 to 24575, as said below
- queries: bfloat16 [147456, 2048], P(('dp', 'ctx')), parts along dimension 0, may hold values from -12 to 12
- keys_values: bfloat16 [147456, 1024], P(('dp', 'ctx')), parts along dimension 0, may hold values from -12 to 12
- router_weight: bfloat16 [147456], P(('dp', 'ctx')), parts along dimension 0, may hold values from 0.25 to 2
Outputs:
- attended: bfloat16 [147456, 2048], P(('dp', 'ctx')), parts along dimension 0
There are 16 independent parts, one for each index of `dp`. A program takes and returns all parts, laid end to end along the dimension named above; each array names one. Nothing has to cross between parts.
Inputs may be any that keep to these rules, and one draw needn't show every extreme that they name: Distinct and increasing. The shard of positions d * 768 to (d + 1) * 768 - 1 holds at most 288 of them, and one shard holds exactly 288; slots of device d's blocks beyond counts[d] hold data that no output reads.
All inputs are finite; a program needn't handle non-finite values.
Results may differ from a plain program's by a relative error of at most 0.0085.
Values may be sent and summed in bfloat16 or wider, within the bound.
No kernel may reach another device: no remote copies, remote signals or barrier semaphores. Data moves between devices by JAX's collectives and lax.ppermute only.
A program may use at most 64 MiB of HBM per device.

v0:
```python
import math

import jax
import jax.numpy as jnp
from jax import lax
from jax.sharding import PartitionSpec as P

QUERY_HEADS = 16
KEY_VALUE_HEADS = 4
HEAD_SIZE = 128
SEL_DEV = 96
TOK_DEV = 768
CAP = 288


large_negative_fill = -1e30


def shard_offsets(positions, devices_ctx):
    bounds = jnp.arange(devices_ctx + 1, dtype=jnp.int32) * TOK_DEV
    return jnp.sum((positions[None, :] < bounds[:, None]).astype(jnp.int32), axis=1)


def pack_forward(arrays, offsets, my_rank, devices_ctx, pair_slots):
    my_start = offsets[my_rank]
    my_count = offsets[my_rank + 1] - my_start
    target = jnp.arange(devices_ctx, dtype=jnp.int32)[:, None]
    slot_index = jnp.arange(pair_slots, dtype=jnp.int32)[None, :]
    global_idx = (my_start // devices_ctx + slot_index) * devices_ctx + target
    local_idx = global_idx - my_start
    usable = ((local_idx >= 0) & (local_idx < my_count)).reshape(-1)
    picked = jnp.clip(local_idx, 0, CAP - 1).reshape(-1)
    result = []
    for member in arrays:
        gathered_rows = jnp.take(member, picked, axis=0)
        mask_shape = usable.reshape(usable.shape + (1,) * (gathered_rows.ndim - 1))
        gathered_rows = jnp.where(mask_shape, gathered_rows, jnp.zeros_like(gathered_rows))
        result.append(gathered_rows.reshape((devices_ctx, pair_slots) + member.shape[1:]))
    return tuple(result)


def unpack_forward(received, offsets, my_rank, devices_ctx, pair_slots):
    slot_ids = jnp.arange(SEL_DEV, dtype=jnp.int32)
    global_idx = slot_ids * devices_ctx + my_rank
    owners = jnp.sum((offsets[None, 1:] <= global_idx[:, None]).astype(jnp.int32), axis=1)
    slot_index = slot_ids - jnp.take(offsets, owners) // devices_ctx
    picked = owners * pair_slots + slot_index
    return tuple(
        (jnp.take(member.reshape((-1,) + member.shape[2:]), picked, axis=0) for member in received)
    )


def pack_return(scaled, offsets, my_rank, devices_ctx, pair_slots):
    starts = offsets[:-1][:, None]
    ends = offsets[1:][:, None]
    slot_index = jnp.arange(pair_slots, dtype=jnp.int32)[None, :]
    local_idx = starts // devices_ctx + slot_index
    global_idx = local_idx * devices_ctx + my_rank
    usable = ((local_idx < SEL_DEV) & (global_idx >= starts) & (global_idx < ends)).reshape(-1)
    picked = jnp.clip(local_idx, 0, SEL_DEV - 1).reshape(-1)
    gathered_rows = jnp.take(scaled, picked, axis=0)
    gathered_rows = jnp.where(usable[:, None], gathered_rows, jnp.zeros_like(gathered_rows))
    return gathered_rows.reshape(devices_ctx, pair_slots, scaled.shape[1])


def unpack_return(received, offsets, my_rank, devices_ctx, pair_slots):
    my_start = offsets[my_rank]
    my_count = offsets[my_rank + 1] - my_start
    slot_ids = jnp.arange(CAP, dtype=jnp.int32)
    global_idx = my_start + slot_ids
    live_slot = slot_ids < my_count
    source = global_idx % devices_ctx
    slot_index = jnp.clip(global_idx // devices_ctx - my_start // devices_ctx, 0, pair_slots - 1)
    flat = received.reshape(-1, received.shape[2])
    gathered_rows = jnp.take(flat, source * pair_slots + slot_index, axis=0)
    return jnp.where(live_slot[:, None], gathered_rows, jnp.zeros_like(gathered_rows))


def block_divisions(rows_total):
    for num_blocks in range(1, rows_total + 1):
        if rows_total % num_blocks == 0 and rows_total // num_blocks <= 512:
            return num_blocks
    return rows_total


def attend(query_row_count, query_index, kv_bal, devices_ctx):
    query_row_total = query_row_count.shape[0]
    group_count = QUERY_HEADS // KEY_VALUE_HEADS
    grouped_heads = query_row_count.reshape(
        query_row_total, KEY_VALUE_HEADS, group_count, HEAD_SIZE
    )
    score_scale = 1.0 / math.sqrt(HEAD_SIZE)

    def update(running, key_block_start, block_start):
        max_run, total_run, accum = running
        key_total_count = key_block_start.shape[0]
        key_rows = block_start + jnp.arange(key_total_count, dtype=jnp.int32)
        key_index = key_rows % SEL_DEV * devices_ctx + key_rows // SEL_DEV
        block_key_rows = key_block_start[:, : KEY_VALUE_HEADS * HEAD_SIZE].reshape(
            key_total_count, KEY_VALUE_HEADS, HEAD_SIZE
        )
        block_value_rows = key_block_start[:, KEY_VALUE_HEADS * HEAD_SIZE :].reshape(
            key_total_count, KEY_VALUE_HEADS, HEAD_SIZE
        )
        scores = (
            jnp.einsum(
                "qkgd,ckd->kgqc", grouped_heads, block_key_rows, preferred_element_type=jnp.float32
            )
            * score_scale
        )
        visible = key_index[None, :] <= query_index[:, None]
        scores = jnp.where(visible, scores, large_negative_fill)
        max_new = jnp.maximum(max_run, jnp.max(scores, axis=-1))
        weights = jnp.where(visible, jnp.exp(scores - max_new[..., None]), 0.0)
        factor = jnp.exp(max_run - max_new)
        total_new = total_run * factor + jnp.sum(weights, axis=-1)
        weighted = jnp.einsum(
            "kgqc,ckd->qkgd",
            weights.astype(jnp.bfloat16),
            block_value_rows,
            preferred_element_type=jnp.float32,
        )
        accum_new = accum * jnp.transpose(factor, (2, 0, 1))[..., None] + weighted
        return (max_new, total_new, accum_new)

    def fold_piece(running, piece_rows, piece_start):
        num_blocks = block_divisions(piece_rows.shape[0])
        if num_blocks == 1:
            return update(running, piece_rows, piece_start)
        block_rows = piece_rows.shape[0] // num_blocks
        blocks = piece_rows.reshape(num_blocks, block_rows, piece_rows.shape[1])

        def scan_step(running_in, inputs_in):
            key_block_start, order_id = inputs_in
            return (update(running_in, key_block_start, piece_start + order_id * block_rows), None)

        running_out, unused = lax.scan(
            scan_step, running, (blocks, jnp.arange(num_blocks, dtype=jnp.int32))
        )
        return running_out

    initial = (
        jnp.full((KEY_VALUE_HEADS, group_count, query_row_total), large_negative_fill, jnp.float32),
        jnp.zeros((KEY_VALUE_HEADS, group_count, query_row_total), jnp.float32),
        jnp.zeros((query_row_total, KEY_VALUE_HEADS, group_count, HEAD_SIZE), jnp.float32),
    )
    max_run, total_run, accum = fold_piece(
        initial, lax.all_gather(kv_bal, "ctx", axis=0, tiled=True), jnp.int32(0)
    )
    result = accum / jnp.transpose(total_run, (2, 0, 1))[..., None]
    return result.reshape(query_row_total, QUERY_HEADS * HEAD_SIZE)


def per_device(positions, queries, keys_values, router_weight):
    devices_ctx = lax.axis_size("ctx")
    my_rank = lax.axis_index("ctx")
    pair_slots = (CAP + devices_ctx - 1) // devices_ctx + 1
    offsets = shard_offsets(positions, devices_ctx)
    packed = pack_forward(
        (queries, keys_values, router_weight), offsets, my_rank, devices_ctx, pair_slots
    )
    moved = (
        lax.all_to_all(packed[0], "ctx", split_axis=0, concat_axis=0, tiled=True),
        lax.all_to_all(packed[1], "ctx", split_axis=0, concat_axis=0, tiled=True),
        lax.all_to_all(packed[2], "ctx", split_axis=0, concat_axis=0, tiled=True),
    )
    query_bal, kv_bal, gate_bal = unpack_forward(moved, offsets, my_rank, devices_ctx, pair_slots)
    query_index = jnp.arange(SEL_DEV, dtype=jnp.int32) * devices_ctx + my_rank
    attended = attend(query_bal, query_index, kv_bal, devices_ctx)
    scaled = (gate_bal.astype(jnp.float32)[:, None] * attended).astype(jnp.bfloat16)
    outgoing = pack_return(scaled, offsets, my_rank, devices_ctx, pair_slots)
    returned = lax.all_to_all(outgoing, "ctx", split_axis=0, concat_axis=0, tiled=True)
    return unpack_return(returned, offsets, my_rank, devices_ctx, pair_slots)


def solution(mesh):
    in_specs = (P("dp"), P(("dp", "ctx"), None), P(("dp", "ctx"), None), P(("dp", "ctx")))
    out_specs = P(("dp", "ctx"), None)
    return jax.shard_map(
        per_device, mesh=mesh, in_specs=in_specs, out_specs=out_specs, check_vma=False
    )
```

profile of v0, /device:TPU:1, one launch (start us, length us, event | category | flops | bytes accessed | tf_op | source)
XLA Modules:
  0.0 317.8 jit_solution(5905198751178517340)
XLA Ops:
  12.8 3.6 %gather_fusion.1 = bf16[320]{0:T(512)(128)(2,1)S(1)} fusion(bf16[288]{0:T(512)(128)(2,1)} %param.9, s32[1024]{0:T(1024)S(1)} %pad_clamp_fusion.3), kind=kCustom, calls=%fused_computation.1 | custom fusion | bytes 2560 | tf_op jit(solution)/shard_map/jit(_take)/gather | solution.py:35
  17.8 10.5 %all-to-all-start = ((bf16[32,1,10]{2,1,0:T(2,128)(2,1)}), bf16[32,1,10]{2,1,0:T(2,128)(2,1)S(1)}, u32[]{:S(2)}, u32[]{:S(2)}) async-start(bf16[32,1,10]{2,1,0:T(2,128)(2,1)} %copy.20), calls=%async_computation | async-start | bytes 32768 | tf_op jit(solution)/shard_map/all_to_all | solution.py:165
  29.0 2.1 gather_fusion.3
  31.3 1.2 select_select_fusion.3
  32.5 4.5 %all-to-all-done = bf16[32,1,10]{2,1,0:T(2,128)(2,1)S(1)} async-done(((bf16[32,1,10]{2,1,0:T(2,128)(2,1)}), bf16[32,1,10]{2,1,0:T(2,128)(2,1)S(1)}, u32[]{:S(2)}, u32[]{:S(2)}) %all-to-all-start) | async-done | bytes 672 | tf_op jit(solution)/shard_map/all_to_all | solution.py:165
  36.9 4.8 %all-to-all-start.1 = ((bf16[32,10,1024]{2,1,0:T(8,128)(2,1)}), bf16[32,10,1024]{2,1,0:T(8,128)(2,1)S(1)}, u32[]{:S(2)}, u32[]{:S(2)}) async-start(bf16[32,10,1024]{2,1,0:T(8,128)(2,1)} %select_select_fusion.3), calls=%async_computation.1 | async-start | bytes 2097152 | tf_op jit(solution)/shard_map/all_to_all | solution.py:164
  42.0 1.2 gather_fusion
  43.4 1.3 gather_fusion.2
  44.7 22.9 %all-to-all-done.1 = bf16[32,10,1024]{2,1,0:T(8,128)(2,1)S(1)} async-done(((bf16[32,10,1024]{2,1,0:T(8,128)(2,1)}), bf16[32,10,1024]{2,1,0:T(8,128)(2,1)S(1)}, u32[]{:S(2)}, u32[]{:S(2)}) %all-to-all-start.1) | async-done | bytes 655392 | tf_op jit(solution)/shard_map/all_to_all | solution.py:164
  69.4 3.0 gather_fusion.5
  72.5 2.3 gather.57
  74.8 1.7 select_select_fusion.1
  76.5 6.8 %all-to-all-start.2 = ((bf16[32,10,2048]{2,1,0:T(8,128)(2,1)}), bf16[32,10,2048]{2,1,0:T(8,128)(2,1)}, u32[]{:S(2)}, u32[]{:S(2)}) async-start(bf16[32,10,2048]{2,1,0:T(8,128)(2,1)} %select_select_fusion.1), calls=%async_computation.2 | async-start | bytes 4194304 | tf_op jit(solution)/shard_map/all_to_all | solution.py:163
  83.6 53.5 %all-to-all-done.2 = bf16[32,10,2048]{2,1,0:T(8,128)(2,1)} async-done(((bf16[32,10,2048]{2,1,0:T(8,128)(2,1)}), bf16[32,10,2048]{2,1,0:T(8,128)(2,1)}, u32[]{:S(2)}, u32[]{:S(2)}) %all-to-all-start.2) | async-done | bytes 1310752 | tf_op jit(solution)/shard_map/all_to_all | solution.py:163
  137.1 2.6 reshape.582
  141.6 33.3 %all-gather.2.cloned.1.call-done = bf16[3072,1024]{1,0:T(8,128)(2,1)} async-done(((bf16[96,1024]{1,0:T(8,128)(2,1)}), bf16[3072,1024]{1,0:T(8,128)(2,1)}) %all-gather.2.cloned.1.call-update) | async-done | bytes 6291472 | tf_op jit(solution)/shard_map/all_gather | solution.py:148
  174.9 64.7 %while.17 = (s32[]{:T(128)}, f32[4,4,96]{2,1,0:T(4,128)S(1)}, f32[4,4,96]{2,1,0:T(4,128)S(1)}, f32[96,4,4,128]{3,0,2,1:T(8,128)}, s32[6]{0:T(128)S(1)}, /*index=...) while((s32[]{:T(128)}, f32[4,4,96]{2,1,0:T(4,128)S(1)}, ...), condition=%wide.region_5.6_spmd.clone, body=%wide.region_2.5_spmd.clone.sunk | while | flops 413532864 | bytes 39490572 | solution.py:137
  176.4 1.3 constant_dynamic-slice_fusion.2
  179.3 2.3 fusion.81
  181.6 2.9 fusion.85
  184.6 1.1 fusion.83
  187.2 1.3 constant_dynamic-slice_fusion.2
  190.1 2.3 fusion.81
  192.4 2.9 fusion.85
  195.4 1.1 fusion.83
  198.0 1.3 constant_dynamic-slice_fusion.2
  200.9 2.3 fusion.81
  203.2 2.9 fusion.85
  206.1 1.1 fusion.83
  208.8 1.3 constant_dynamic-slice_fusion.2
  211.6 2.3 fusion.81
  214.0 2.9 fusion.85
  219.6 1.3 constant_dynamic-slice_fusion.2
  222.4 2.3 fusion.81
  224.8 2.9 fusion.85
  227.7 1.1 fusion.83
  230.4 1.3 constant_dynamic-slice_fusion.2
  233.2 2.3 fusion.81
  235.6 2.9 fusion.85
  239.7 1.4 broadcast_divide_fusion
  242.0 3.0 gather_fusion.7
  245.0 2.3 gather.61
  247.4 1.6 select_select_fusion
  249.0 6.0 %all-to-all-start.3 = ((bf16[32,10,2048]{2,1,0:T(8,128)(2,1)}), bf16[32,10,2048]{2,1,0:T(8,128)(2,1)}, u32[]{:S(2)}, u32[]{:S(2)}) async-start(bf16[32,10,2048]{2,1,0:T(8,128)(2,1)} %select_select_fusion), calls=%async_computation.3 | async-start | bytes 4194304 | tf_op jit(solution)/shard_map/all_to_all | solution.py:172
  256.3 46.6 %all-to-all-done.3 = bf16[32,10,2048]{2,1,0:T(8,128)(2,1)} async-done(((bf16[32,10,2048]{2,1,0:T(8,128)(2,1)}), bf16[32,10,2048]{2,1,0:T(8,128)(2,1)}, u32[]{:S(2)}, u32[]{:S(2)}) %all-to-all-start.3) | async-done | bytes 1310752 | tf_op jit(solution)/shard_map/all_to_all | solution.py:172
  303.0 2.5 reshape.584
  305.5 3.0 gather_fusion.8
  308.5 2.5 select_select_fusion.2
  (155 shorter events, 27.7 us)
Async XLA Ops:
  6.5 62.9 %copy-start = (bf16[288,2048]{1,0:T(8,128)(2,1)S(1)}, bf16[288,2048]{1,0:T(8,128)(2,1)}, u32[]{:S(2)}) copy-start(bf16[288,2048]{1,0:T(8,128)(2,1)} %param.7) | copy-start | bytes 3538948
  6.5 22.4 %copy-start.2 = (bf16[288,1024]{1,0:T(8,128)(2,1)S(1)}, bf16[288,1024]{1,0:T(8,128)(2,1)}, u32[]{:S(2)}) copy-start(bf16[288,1024]{1,0:T(8,128)(2,1)} %param.8) | copy-start | bytes 1769476
  17.8 19.1 %all-to-all-start = ((bf16[32,1,10]{2,1,0:T(2,128)(2,1)}), bf16[32,1,10]{2,1,0:T(2,128)(2,1)S(1)}, u32[]{:S(2)}, u32[]{:S(2)}) async-start(bf16[32,1,10]{2,1,0:T(2,128)(2,1)} %copy.20), calls=%async_computation | async-start | bytes 32768 | tf_op jit(solution)/shard_map/all_to_all | solution.py:165
  36.9 30.7 %all-to-all-start.1 = ((bf16[32,10,1024]{2,1,0:T(8,128)(2,1)}), bf16[32,10,1024]{2,1,0:T(8,128)(2,1)S(1)}, u32[]{:S(2)}, u32[]{:S(2)}) async-start(bf16[32,10,1024]{2,1,0:T(8,128)(2,1)} %select_select_fusion.3), calls=%async_computation.1 | async-start | bytes 2097152 | tf_op jit(solution)/shard_map/all_to_all | solution.py:164
  41.7 133.2 %all-gather.2.cloned.1.call-start = ((), (), s32[]{:S(2)}) async-start(), calls=%async_computation.4 | async-start | bytes 6488064 | tf_op jit(solution)/shard_map/all_gather | solution.py:148
  76.5 60.6 %all-to-all-start.2 = ((bf16[32,10,2048]{2,1,0:T(8,128)(2,1)}), bf16[32,10,2048]{2,1,0:T(8,128)(2,1)}, u32[]{:S(2)}, u32[]{:S(2)}) async-start(bf16[32,10,2048]{2,1,0:T(8,128)(2,1)} %select_select_fusion.1), calls=%async_computation.2 | async-start | bytes 4194304 | tf_op jit(solution)/shard_map/all_to_all | solution.py:163
  178.3 1.0 copy-start.3
  178.4 3.2 %copy-start.4 = (f32[96,4,4,128]{3,0,2,1:T(8,128)S(1)}, f32[96,4,4,128]{3,0,2,1:T(8,128)}, u32[]{:S(2)}) copy-start(f32[96,4,4,128]{3,0,2,1:T(8,128)} %get-tuple-element.274) | copy-start | bytes 2359300 | tf_op jit(solution)/shard_map/while
  181.6 2.9 copy-start.1
  184.6 1.1 copy-start.5
  189.1 1.0 copy-start.3
  189.2 3.2 %copy-start.4 = (f32[96,4,4,128]{3,0,2,1:T(8,128)S(1)}, f32[96,4,4,128]{3,0,2,1:T(8,128)}, u32[]{:S(2)}) copy-start(f32[96,4,4,128]{3,0,2,1:T(8,128)} %get-tuple-element.274) | copy-start | bytes 2359300 | tf_op jit(solution)/shard_map/while
  192.4 2.9 copy-start.1
  195.3 1.1 copy-start.5
  199.9 1.0 copy-start.3
  199.9 3.2 %copy-start.4 = (f32[96,4,4,128]{3,0,2,1:T(8,128)S(1)}, f32[96,4,4,128]{3,0,2,1:T(8,128)}, u32[]{:S(2)}) copy-start(f32[96,4,4,128]{3,0,2,1:T(8,128)} %get-tuple-element.274) | copy-start | bytes 2359300 | tf_op jit(solution)/shard_map/while
  203.2 2.9 copy-start.1
  206.1 1.1 copy-start.5
  210.6 1.0 copy-start.3
  210.7 3.2 %copy-start.4 = (f32[96,4,4,128]{3,0,2,1:T(8,128)S(1)}, f32[96,4,4,128]{3,0,2,1:T(8,128)}, u32[]{:S(2)}) copy-start(f32[96,4,4,128]{3,0,2,1:T(8,128)} %get-tuple-element.274) | copy-start | bytes 2359300 | tf_op jit(solution)/shard_map/while
  214.0 2.9 copy-start.1
  216.9 1.1 copy-start.5
  221.4 1.0 copy-start.3
  221.5 3.2 %copy-start.4 = (f32[96,4,4,128]{3,0,2,1:T(8,128)S(1)}, f32[96,4,4,128]{3,0,2,1:T(8,128)}, u32[]{:S(2)}) copy-start(f32[96,4,4,128]{3,0,2,1:T(8,128)} %get-tuple-element.274) | copy-start | bytes 2359300 | tf_op jit(solution)/shard_map/while
  224.8 2.9 copy-start.1
  227.7 1.1 copy-start.5
  232.2 1.0 copy-start.3
  232.3 3.2 %copy-start.4 = (f32[96,4,4,128]{3,0,2,1:T(8,128)S(1)}, f32[96,4,4,128]{3,0,2,1:T(8,128)}, u32[]{:S(2)}) copy-start(f32[96,4,4,128]{3,0,2,1:T(8,128)} %get-tuple-element.274) | copy-start | bytes 2359300 | tf_op jit(solution)/shard_map/while
  235.6 2.9 copy-start.1
  238.5 1.1 copy-start.5
  249.0 54.0 %all-to-all-start.3 = ((bf16[32,10,2048]{2,1,0:T(8,128)(2,1)}), bf16[32,10,2048]{2,1,0:T(8,128)(2,1)}, u32[]{:S(2)}, u32[]{:S(2)}) async-start(bf16[32,10,2048]{2,1,0:T(8,128)(2,1)} %select_select_fusion), calls=%async_computation.3 | async-start | bytes 4194304 | tf_op jit(solution)/shard_map/all_to_all | solution.py:172
Sparse Core Ops, SparseCore 0:
  69.5 105.3 all-gather.1
where the time goes:
time: 321 us; the launch traced here: 318 us
  waiting for transfers between devices  161 us (50%)
  local copies, waits for them, and re-layouts  52.7 us (16%)
  matrix products  31.3 us (10%)
  starting transfers between devices  28.1 us (9%)
  other arithmetic  22.4 us (7%)
  between operations  17.5 us (5%)
  loops' own time  4.95 us (2%)
    all_to_all x1, waiting for transfers between devices, per_device(): lax.all_to_all(packed[0], 'ctx', split_axis=0, concat_axis=0, tiled=True)  53.5 us
    all_to_all x1, waiting for transfers between devices, per_device(): lax.all_to_all(outgoing, 'ctx', split_axis=0, concat_axis=0, tiled=True)  46.6 us
    all_gather x1, waiting for transfers between devices, attend(): lax.all_gather(kv_bal, 'ctx', axis=0, tiled=True)  33.3 us
    all_to_all x1, waiting for transfers between devices, per_device(): lax.all_to_all(packed[1], 'ctx', split_axis=0, concat_axis=0, tiled=True)  22.9 us
    dot_general x6, matrix products, update(): jnp.einsum('kgqc,ckd->qkgd', weights.astype(jnp.bfloat16), block_value_ro...  17.5 us
    dynamic_slice x18, local copies, waits for them, and re-layouts, fold_piece(): lax.scan(scan_step, running, (blocks, jnp.arange(num_blocks, dtype=jnp.in...  15 us
    dot_general x6, matrix products, update(): jnp.einsum('qkgd,ckd->kgqc', grouped_heads, block_key_rows, preferred_ele...  13.9 us
    gather x6, local copies, waits for them, and re-layouts, pack_forward(): gathered_rows = jnp.take(member, picked, axis=0)  11.4 us
  transfers between devices with their start and end apart: 5, of which 5 were waited for; matrix products, arithmetic and copies ran while one was open for 6% of the time, Pallas kernels for 0%

commit v1 on v0

v1 whole, which is shorter than its diff:
```python
import math

import jax
import jax.numpy as jnp
from jax import lax
from jax.experimental import pallas as pl
from jax.experimental.pallas import tpu as pltpu
from jax.sharding import PartitionSpec as P

QUERY_HEADS = 16
KEY_VALUE_HEADS = 4
HEAD_SIZE = 128
SEL_DEV = 96
TOK_DEV = 768
CAP = 288
KEY_CHUNK = 512


large_negative_fill = -1e30


def shard_offsets(positions, devices_ctx):
    bounds = jnp.arange(devices_ctx + 1, dtype=jnp.int32) * TOK_DEV
    return jnp.sum((positions[None, :] < bounds[:, None]).astype(jnp.int32), axis=1)


def pack_forward(arrays, offsets, my_rank, devices_ctx, pair_slots):
    my_start = offsets[my_rank]
    my_count = offsets[my_rank + 1] - my_start
    target = jnp.arange(devices_ctx, dtype=jnp.int32)[:, None]
    slot_index = jnp.arange(pair_slots, dtype=jnp.int32)[None, :]
    global_idx = (my_start // devices_ctx + slot_index) * devices_ctx + target
    local_idx = global_idx - my_start
    usable = ((local_idx >= 0) & (local_idx < my_count)).reshape(-1)
    picked = jnp.clip(local_idx, 0, CAP - 1).reshape(-1)
    result = []
    for member in arrays:
        gathered_rows = jnp.take(member, picked, axis=0)
        mask_shape = usable.reshape(usable.shape + (1,) * (gathered_rows.ndim - 1))
        gathered_rows = jnp.where(mask_shape, gathered_rows, jnp.zeros_like(gathered_rows))
        result.append(gathered_rows.reshape((devices_ctx, pair_slots) + member.shape[1:]))
    return tuple(result)


def unpack_forward(received, offsets, my_rank, devices_ctx, pair_slots):
    slot_ids = jnp.arange(SEL_DEV, dtype=jnp.int32)
    global_idx = slot_ids * devices_ctx + my_rank
    owners = jnp.sum((offsets[None, 1:] <= global_idx[:, None]).astype(jnp.int32), axis=1)
    slot_index = slot_ids - jnp.take(offsets, owners) // devices_ctx
    picked = owners * pair_slots + slot_index
    return tuple(
        (jnp.take(member.reshape((-1,) + member.shape[2:]), picked, axis=0) for member in received)
    )


def attention_kernel(qidx_ref, kidx_ref, gate_ref, q_ref, k_ref, v_ref, o_ref):
    group_count = QUERY_HEADS // KEY_VALUE_HEADS
    rows = q_ref.shape[0]
    keys = k_ref.shape[0]
    score_scale = 1.0 / math.sqrt(HEAD_SIZE)
    qidx = qidx_ref[...]
    valid = qidx >= 0
    gate = gate_ref[...]
    for g in range(group_count):
        q = q_ref[:, g * HEAD_SIZE : (g + 1) * HEAD_SIZE]
        m_run = jnp.full((rows, 1), large_negative_fill, jnp.float32)
        l_run = jnp.zeros((rows, 1), jnp.float32)
        acc = jnp.zeros((rows, HEAD_SIZE), jnp.float32)
        for c in range(keys // KEY_CHUNK):
            lo = c * KEY_CHUNK
            k = k_ref[lo : lo + KEY_CHUNK, :]
            v = v_ref[lo : lo + KEY_CHUNK, :]
            s = lax.dot_general(
                q, k, (((1,), (1,)), ((), ())), preferred_element_type=jnp.float32
            )
            visible = kidx_ref[:, lo : lo + KEY_CHUNK] <= qidx
            s = jnp.where(visible, s, large_negative_fill)
            m_new = jnp.maximum(m_run, jnp.max(s, axis=-1, keepdims=True))
            p = jnp.exp((s - m_new) * score_scale)
            factor = jnp.exp((m_run - m_new) * score_scale)
            l_run = l_run * factor + jnp.sum(p, axis=-1, keepdims=True)
            acc = acc * factor + jnp.dot(
                p.astype(jnp.bfloat16), v, preferred_element_type=jnp.float32
            )
            m_run = m_new
        out = jnp.where(valid, gate * (acc / l_run), 0.0)
        o_ref[:, g * HEAD_SIZE : (g + 1) * HEAD_SIZE] = out.astype(o_ref.dtype)


def local_attention(qidx, kidx, gate, queries, kv_all):
    rows = queries.shape[0]
    keys = kv_all.shape[0]
    group_width = (QUERY_HEADS // KEY_VALUE_HEADS) * HEAD_SIZE
    return pl.pallas_call(
        attention_kernel,
        grid=(KEY_VALUE_HEADS,),
        in_specs=[
            pl.BlockSpec((rows, 1), lambda h: (0, 0)),
            pl.BlockSpec((1, keys), lambda h: (0, 0)),
            pl.BlockSpec((rows, 1), lambda h: (0, 0)),
            pl.BlockSpec((rows, group_width), lambda h: (0, h)),
            pl.BlockSpec((keys, HEAD_SIZE), lambda h: (0, h)),
            pl.BlockSpec((keys, HEAD_SIZE), lambda h: (0, h + KEY_VALUE_HEADS)),
        ],
        out_specs=pl.BlockSpec((rows, group_width), lambda h: (0, h)),
        out_shape=jax.ShapeDtypeStruct((rows, QUERY_HEADS * HEAD_SIZE), jnp.bfloat16),
        compiler_params=pltpu.CompilerParams(dimension_semantics=("arbitrary",)),
    )(qidx, kidx, gate, queries, kv_all, kv_all)


def per_device(positions, queries, keys_values, router_weight):
    devices_ctx = lax.axis_size("ctx")
    my_rank = lax.axis_index("ctx")
    pair_slots = (CAP + devices_ctx - 1) // devices_ctx + 1
    offsets = shard_offsets(positions, devices_ctx)
    packed = pack_forward((keys_values,), offsets, my_rank, devices_ctx, pair_slots)
    moved = (lax.all_to_all(packed[0], "ctx", split_axis=0, concat_axis=0, tiled=True),)
    (kv_bal,) = unpack_forward(moved, offsets, my_rank, devices_ctx, pair_slots)
    kv_all = lax.all_gather(kv_bal, "ctx", axis=0, tiled=True)
    key_rows = jnp.arange(SEL_DEV * devices_ctx, dtype=jnp.int32)
    kidx = (key_rows % SEL_DEV * devices_ctx + key_rows // SEL_DEV)[None, :]
    my_start = offsets[my_rank]
    my_count = offsets[my_rank + 1] - my_start
    slot_ids = jnp.arange(CAP, dtype=jnp.int32)
    qidx = jnp.where(slot_ids < my_count, my_start + slot_ids, -1)[:, None]
    gate = router_weight.astype(jnp.float32)[:, None]
    return local_attention(qidx, kidx, gate, queries, kv_all)


def solution(mesh):
    in_specs = (P("dp"), P(("dp", "ctx"), None), P(("dp", "ctx"), None), P(("dp", "ctx")))
    out_specs = P(("dp", "ctx"), None)
    return jax.shard_map(
        per_device, mesh=mesh, in_specs=in_specs, out_specs=out_specs, check_vma=False
    )
```

time: 321 us -> 195 us (0.61)
  local copies, waits for them, and re-layouts: 52.7 us -> 6.11 us
  waiting for transfers between devices: 161 us -> 117 us
  Pallas kernels: 0 us -> 37.2 us
  matrix products: 31.3 us -> 0 us
  starting transfers between devices: 28.1 us -> 10.5 us
  other arithmetic: 22.4 us -> 6.39 us
  loops' own time: 4.95 us -> 0 us
    all_to_all x3 -> x0, waiting for transfers between devices: 74 us -> none  [the longest x1 46.6 us: per_device(): lax.all_to_all(outgoing, 'ctx', split_axis=0, concat_axis=0, tiled=True)]
    all_gather x1, waiting for transfers between devices: 33.3 us -> 92.1 us  [per_device(): kv_all = lax.all_gather(kv_bal, 'ctx', axis=0, tiled=True)]
    pallas_call x0 -> x1, Pallas kernels: none -> 37.2 us  [local_attention(): pl.pallas_call(attention_kernel, grid=(KEY_VALUE_HEADS,), in_specs=[pl.Bl...]
    dot_general x12 -> x0, matrix products: 31.3 us -> none  [the longest x6 17.5 us: update(): jnp.einsum('kgqc,ckd->qkgd', weights.astype(jnp.bfloat16), block_value_ro...]
    all_to_all x1, waiting for transfers between devices: 53.5 us -> 24.7 us  [per_device(): lax.all_to_all(packed[0], 'ctx', split_axis=0, concat_axis=0, tiled=True)]
    all_to_all x3 -> x0, starting transfers between devices: 21.3 us -> none  [the longest x1 10.5 us: per_device(): lax.all_to_all(packed[2], 'ctx', split_axis=0, concat_axis=0, tiled=True)]
    dynamic_slice x19 -> x1, local copies, waits for them, and re-layouts: 15.7 us -> 0.62 us  [per_device(): my_count = offsets[my_rank + 1] - my_start]
    gather x6 -> x2, local copies, waits for them, and re-layouts: 11.4 us -> 2.31 us  [pack_forward(): gathered_rows = jnp.take(member, picked, axis=0)]
  transfers between devices with their start and end apart: 5 -> 2, of which waited for: 5 -> 2; matrix products, arithmetic and copies ran while one was open for 6% -> 2% of each run, Pallas kernels for 0% -> 0%
where the time goes in v1:
time: 195 us; the launch traced here: 194 us
  waiting for transfers between devices  117 us (60%)
  Pallas kernels  37.2 us (19%)
  between operations  17.4 us (9%)
  starting transfers between devices  10.5 us (5%)
  other arithmetic  6.39 us (3%)
  local copies, waits for them, and re-layouts  6.11 us (3%)
    all_gather x1, waiting for transfers between devices, per_device(): kv_all = lax.all_gather(kv_bal, 'ctx', axis=0, tiled=True)  92.1 us
    pallas_call x1, Pallas kernels, local_attention(): pl.pallas_call(attention_kernel, grid=(KEY_VALUE_HEADS,), in_specs=[pl.Bl...  37.2 us
    all_to_all x1, waiting for transfers between devices, per_device(): lax.all_to_all(packed[0], 'ctx', split_axis=0, concat_axis=0, tiled=True)  24.7 us
    all_to_all x1, starting transfers between devices, per_device(): lax.all_to_all(packed[0], 'ctx', split_axis=0, concat_axis=0, tiled=True)  10.5 us
  transfers between devices with their start and end apart: 2, of which 2 were waited for; matrix products, arithmetic and copies ran while one was open for 2% of the time, Pallas kernels for 0%

profile of v1, /device:TPU:1, one launch (start us, length us, event | category | flops | bytes accessed | tf_op | source)
XLA Modules:
  0.0 194.4 jit_solution(16046672765308524215)
XLA Ops:
  6.5 0.0 copy-start
  6.5 1.0 convert_reduce_fusion
  7.5 0.6 fusion.10
  12.0 0.6 fusion
  12.7 0.7 fusion.3
  13.3 0.1 min.12
  13.5 0.0 copy-done
  13.5 2.1 %gather_fusion.1 = bf16[320,1024]{1,0:T(8,128)(2,1)S(1)} fusion(bf16[288,1024]{1,0:T(8,128)(2,1)S(1)} %copy-done, s32[1024]{0:T(1024)S(1)} %pad_clamp_fusion.1), kind=kCustom, calls=%fused_computation.1 | custom fusion | bytes 1312000 | tf_op jit(solution)/shard_map/jit(_take)/gather | solution.py:38
  15.6 0.2 gather.18
  15.8 1.2 select_select_fusion
  17.0 10.5 %all-to-all-start = ((bf16[32,10,1024]{2,1,0:T(8,128)(2,1)}), bf16[32,10,1024]{2,1,0:T(8,128)(2,1)S(1)}, u32[]{:S(2)}, u32[]{:S(2)}) async-start(bf16[32,10,1024]{2,1,0:T(8,128)(2,1)} %select_select_fusion), calls=%async_computation | async-start | bytes 2097152 | tf_op jit(solution)/shard_map/all_to_all | solution.py:117
  27.5 0.0 all-gather.2.cloned.1.call-start
  27.5 0.1 slice.3
  27.6 0.1 convert_reduce_fusion.1
  27.7 1.2 gather_fusion
  29.0 24.7 %all-to-all-done = bf16[32,10,1024]{2,1,0:T(8,128)(2,1)S(1)} async-done(((bf16[32,10,1024]{2,1,0:T(8,128)(2,1)}), bf16[32,10,1024]{2,1,0:T(8,128)(2,1)S(1)}, u32[]{:S(2)}, u32[]{:S(2)}) %all-to-all-start) | async-done | bytes 655392 | tf_op jit(solution)/shard_map/all_to_all | solution.py:117
  53.7 0.2 reshape.272
  53.9 0.0 copy-start.1
  53.9 0.8 gather_fusion.2
  54.7 0.8 broadcast_select_fusion
  55.5 0.0 all-gather.2.cloned.1.call-update
  55.5 0.0 copy-done.1
  55.5 0.8 reshape.298.gate_ref
  56.3 1.3 add_select_fusion.qidx_ref
  57.6 0.6 fusion.5.kidx_ref
  58.2 92.1 %all-gather.2.cloned.1.call-done.k_ref.v_ref = bf16[3072,1024]{1,0:T(8,128)(2,1)} async-done(((bf16[96,1024]{1,0:T(8,128)(2,1)}), bf16[3072,1024]{1,0:T(8,128)(2,1)}) %all-gather.2.cloned.1.call-update) | async-done | bytes 6291472 | tf_op jit(solution)/shard_map/all_gather | solution.py:119
  150.3 37.2 %shard_map.46 = bf16[288,2048]{1,0:T(8,128)(2,1)} custom-call(s32[288,1]{1,0:T(8,128)} %add_select_fusion.qidx_ref, s32[1,3072]{1,0:T(1,128)} %fusion.5.kidx_ref, f32[288,1]{1,0:T(8,128)} %reshape.298.gate_ref, bf16[288,2048]{1,0:T(8,128)(2,1)} %q_ref.1, bf16[3072,1024]{1,0:T(8,128)(2,1)} %all-gather.2.cloned.1.call-done.k_ref.v_ref, ...), custom_call_target="tpu_custom_call" | custom-call | tf_op jit(solution)/shard_map/pallas_call | solution.py:94
  (10 shorter events, 0.1 us)
Async XLA Ops:
  6.5 6.9 %copy-start = (bf16[288,1024]{1,0:T(8,128)(2,1)S(1)}, bf16[288,1024]{1,0:T(8,128)(2,1)}, u32[]{:S(2)}) copy-start(bf16[288,1024]{1,0:T(8,128)(2,1)} %param.6) | copy-start | bytes 1769476
  17.0 36.7 %all-to-all-start = ((bf16[32,10,1024]{2,1,0:T(8,128)(2,1)}), bf16[32,10,1024]{2,1,0:T(8,128)(2,1)S(1)}, u32[]{:S(2)}, u32[]{:S(2)}) async-start(bf16[32,10,1024]{2,1,0:T(8,128)(2,1)} %select_select_fusion), calls=%async_computation | async-start | bytes 2097152 | tf_op jit(solution)/shard_map/all_to_all | solution.py:117
  27.5 122.9 %all-gather.2.cloned.1.call-start = ((), (), s32[]{:S(2)}) async-start(), calls=%async_computation.1 | async-start | bytes 6488064 | tf_op jit(solution)/shard_map/all_gather | solution.py:119
  53.9 1.6 copy-start.1
Sparse Core Ops, SparseCore 0:
  55.6 94.6 all-gather.1

commit v2 on v1

--- a/solution.py
+++ b/solution.py
@@ -1,3 +1,4 @@
+import functools
 import math
 
 import jax
@@ -14,6 +15,7 @@
 TOK_DEV = 768
 CAP = 288
 KEY_CHUNK = 512
+GATHER_CHUNKS = 3
 
 
 large_negative_fill = -1e30
@@ -53,19 +55,29 @@
     )
 
 
-def attention_kernel(qidx_ref, kidx_ref, gate_ref, q_ref, k_ref, v_ref, o_ref):
+def attention_kernel(first, last, qidx_ref, kidx_ref, gate_ref, q_ref, k_ref, v_ref, *rest):
     group_count = QUERY_HEADS // KEY_VALUE_HEADS
     rows = q_ref.shape[0]
     keys = k_ref.shape[0]
     score_scale = 1.0 / math.sqrt(HEAD_SIZE)
+    if first:
+        state_in = None
+        state_out = rest
+    else:
+        state_in = rest[:3]
+        state_out = rest[3:]
     qidx = qidx_ref[...]
-    valid = qidx >= 0
-    gate = gate_ref[...]
     for g in range(group_count):
-        q = q_ref[:, g * HEAD_SIZE : (g + 1) * HEAD_SIZE]
-        m_run = jnp.full((rows, 1), large_negative_fill, jnp.float32)
-        l_run = jnp.zeros((rows, 1), jnp.float32)
-        acc = jnp.zeros((rows, HEAD_SIZE), jnp.float32)
+        cols = slice(g * HEAD_SIZE, (g + 1) * HEAD_SIZE)
+        q = q_ref[:, cols]
+        if first:
+            m_run = jnp.full((rows, 1), large_negative_fill, jnp.float32)
+            l_run = jnp.zeros((rows, 1), jnp.float32)
+            acc = jnp.zeros((rows, HEAD_SIZE), jnp.float32)
+        else:
+            acc = state_in[0][:, cols]
+            m_run = state_in[1][0, :, g : g + 1]
+            l_run = state_in[2][0, :, g : g + 1]
         for c in range(keys // KEY_CHUNK):
             lo = c * KEY_CHUNK
             k = k_ref[lo : lo + KEY_CHUNK, :]
@@ -83,29 +95,50 @@
                 p.astype(jnp.bfloat16), v, preferred_element_type=jnp.float32
             )
             m_run = m_new
-        out = jnp.where(valid, gate * (acc / l_run), 0.0)
-        o_ref[:, g * HEAD_SIZE : (g + 1) * HEAD_SIZE] = out.astype(o_ref.dtype)
+        if last:
+            out = jnp.where(qidx >= 0, gate_ref[...] * (acc / l_run), 0.0)
+            state_out[0][:, cols] = out.astype(state_out[0].dtype)
+        else:
+            state_out[0][:, cols] = acc
+            state_out[1][0, :, g : g + 1] = m_run
+            state_out[2][0, :, g : g + 1] = l_run
 
 
-def local_attention(qidx, kidx, gate, queries, kv_all):
+def local_attention(qidx, kidx, gate, queries, kv_part, state, last):
     rows = queries.shape[0]
-    keys = kv_all.shape[0]
-    group_width = (QUERY_HEADS // KEY_VALUE_HEADS) * HEAD_SIZE
+    keys = kv_part.shape[0]
+    group_count = QUERY_HEADS // KEY_VALUE_HEADS
+    group_width = group_count * HEAD_SIZE
+    width = QUERY_HEADS * HEAD_SIZE
+    acc_spec = pl.BlockSpec((rows, group_width), lambda h: (0, h))
+    stat_spec = pl.BlockSpec((1, rows, group_count), lambda h: (h, 0, 0))
+    stat_shape = jax.ShapeDtypeStruct((KEY_VALUE_HEADS, rows, group_count), jnp.float32)
+    in_specs = [
+        pl.BlockSpec((rows, 1), lambda h: (0, 0)),
+        pl.BlockSpec((1, keys), lambda h: (0, 0)),
+        pl.BlockSpec((rows, 1), lambda h: (0, 0)),
+        pl.BlockSpec((rows, group_width), lambda h: (0, h)),
+        pl.BlockSpec((keys, HEAD_SIZE), lambda h: (0, h)),
+        pl.BlockSpec((keys, HEAD_SIZE), lambda h: (0, h + KEY_VALUE_HEADS)),
+    ]
+    operands = [qidx, kidx, gate, queries, kv_part, kv_part]
+    if state is not None:
+        in_specs += [acc_spec, stat_spec, stat_spec]
+        operands += list(state)
+    if last:
+        out_specs = acc_spec
+        out_shape = jax.ShapeDtypeStruct((rows, width), jnp.bfloat16)
+    else:
+        out_specs = (acc_spec, stat_spec, stat_spec)
+        out_shape = (jax.ShapeDtypeStruct((rows, width), jnp.float32), stat_shape, stat_shape)
     return pl.pallas_call(
-        attention_kernel,
+        functools.partial(attention_kernel, state is None, last),
         grid=(KEY_VALUE_HEADS,),
-        in_specs=[
-            pl.BlockSpec((rows, 1), lambda h: (0, 0)),
-            pl.BlockSpec((1, keys), lambda h: (0, 0)),
-            pl.BlockSpec((rows, 1), lambda h: (0, 0)),
-            pl.BlockSpec((rows, group_width), lambda h: (0, h)),
-            pl.BlockSpec((keys, HEAD_SIZE), lambda h: (0, h)),
-            pl.BlockSpec((keys, HEAD_SIZE), lambda h: (0, h + KEY_VALUE_HEADS)),
-        ],
-        out_specs=pl.BlockSpec((rows, group_width), lambda h: (0, h)),
-        out_shape=jax.ShapeDtypeStruct((rows, QUERY_HEADS * HEAD_SIZE), jnp.bfloat16),
+        in_specs=in_specs,
+        out_specs=out_specs,
+        out_shape=out_shape,
         compiler_params=pltpu.CompilerParams(dimension_semantics=("arbitrary",)),
-    )(qidx, kidx, gate, queries, kv_all, kv_all)
+    )(*operands)
 
 
 def per_device(positions, queries, keys_values, router_weight):
@@ -116,15 +149,21 @@
     packed = pack_forward((keys_values,), offsets, my_rank, devices_ctx, pair_slots)
     moved = (lax.all_to_all(packed[0], "ctx", split_axis=0, concat_axis=0, tiled=True),)
     (kv_bal,) = unpack_forward(moved, offsets, my_rank, devices_ctx, pair_slots)
-    kv_all = lax.all_gather(kv_bal, "ctx", axis=0, tiled=True)
-    key_rows = jnp.arange(SEL_DEV * devices_ctx, dtype=jnp.int32)
-    kidx = (key_rows % SEL_DEV * devices_ctx + key_rows // SEL_DEV)[None, :]
     my_start = offsets[my_rank]
     my_count = offsets[my_rank + 1] - my_start
     slot_ids = jnp.arange(CAP, dtype=jnp.int32)
     qidx = jnp.where(slot_ids < my_count, my_start + slot_ids, -1)[:, None]
     gate = router_weight.astype(jnp.float32)[:, None]
-    return local_attention(qidx, kidx, gate, queries, kv_all)
+    chunk_slots = SEL_DEV // GATHER_CHUNKS
+    state = None
+    for c in range(GATHER_CHUNKS):
+        part = kv_bal[c * chunk_slots : (c + 1) * chunk_slots]
+        kv_part = lax.all_gather(part, "ctx", axis=0, tiled=True)
+        key_rows = jnp.arange(chunk_slots * devices_ctx, dtype=jnp.int32)
+        kidx = ((c * chunk_slots + key_rows % chunk_slots) * devices_ctx + key_rows // chunk_slots)[None, :]
+        last = c == GATHER_CHUNKS - 1
+        state = local_attention(qidx, kidx, gate, queries, kv_part, state, last)
+    return state
 
 
 def solution(mesh):

time: 195 us -> 331 us (1.70); the launches traced: 194 us -> 327 us
  waiting for transfers between devices: 117 us -> 235 us
  Pallas kernels: 37.2 us -> 51.3 us
    all_gather x1 -> x3, waiting for transfers between devices: 92.1 us -> 209 us  [per_device(): kv_part = lax.all_gather(part, 'ctx', axis=0, tiled=True)]
    pallas_call x1 -> x3, Pallas kernels: 37.2 us -> 51.3 us  [local_attention(): pl.pallas_call(functools.partial(attention_kernel, state is None, last),...]
  transfers between devices with their start and end apart: 2 -> 4, of which waited for: 2 -> 4; matrix products, arithmetic and copies ran while one was open for 2% -> 2% of each run, Pallas kernels for 0% -> 11%
where the time goes in v2:
time: 331 us; the launch traced here: 327 us
  waiting for transfers between devices  235 us (71%)
  Pallas kernels  51.3 us (15%)
  between operations  16.6 us (5%)
  starting transfers between devices  10.8 us (3%)
  local copies, waits for them, and re-layouts  6.76 us (2%)
  other arithmetic  6.62 us (2%)
    all_gather x3, waiting for transfers between devices, per_device(): kv_part = lax.all_gather(part, 'ctx', axis=0, tiled=True)  209 us
    pallas_call x3, Pallas kernels, local_attention(): pl.pallas_call(functools.partial(attention_kernel, state is None, last),...  51.3 us
    all_to_all x1, waiting for transfers between devices, per_device(): lax.all_to_all(packed[0], 'ctx', split_axis=0, concat_axis=0, tiled=True)  24.7 us
    all_to_all x1, starting transfers between devices, per_device(): lax.all_to_all(packed[0], 'ctx', split_axis=0, concat_axis=0, tiled=True)  10.5 us
  transfers between devices with their start and end apart: 4, of which 4 were waited for; matrix products, arithmetic and copies ran while one was open for 2% of the time, Pallas kernels for 11%

profile of v2, /device:TPU:1, one launch (start us, length us, event | category | flops | bytes accessed | tf_op | source)
XLA Modules:
  0.0 327.0 jit_solution(8586203158632778606)
XLA Ops:
  6.5 0.0 copy-start
  6.5 1.0 convert_reduce_fusion
  7.5 0.6 fusion.9
  10.3 0.6 fusion
  10.9 0.1 min.12
  11.1 0.0 copy-done
  11.1 2.1 gather_fusion.1
  13.2 0.2 gather.18
  14.6 0.6 fusion.3
  15.1 1.2 select_select_fusion
  16.3 10.5 %all-to-all-start = ((bf16[32,10,1024]{2,1,0:T(8,128)(2,1)}), bf16[32,10,1024]{2,1,0:T(8,128)(2,1)S(1)}, u32[]{:S(2)}, u32[]{:S(2)}) async-start(bf16[32,10,1024]{2,1,0:T(8,128)(2,1)} %select_select_fusion), calls=%async_computation | async-start | bytes 2097152 | tf_op jit(solution)/shard_map/all_to_all | solution.py:150
  26.8 0.0 all-gather.8.cloned.1.call-start
  26.9 0.1 slice.12
  27.0 0.1 convert_reduce_fusion.1
  27.1 1.2 gather_fusion
  28.4 0.0 copy-start.1
  28.4 24.7 %all-to-all-done = bf16[32,10,1024]{2,1,0:T(8,128)(2,1)S(1)} async-done(((bf16[32,10,1024]{2,1,0:T(8,128)(2,1)}), bf16[32,10,1024]{2,1,0:T(8,128)(2,1)S(1)}, u32[]{:S(2)}, u32[]{:S(2)}) %all-to-all-start) | async-done | bytes 655392 | tf_op jit(solution)/shard_map/all_to_all | solution.py:150
  53.0 0.2 reshape.295
  53.3 0.8 gather_fusion.2
  54.0 0.1 broadcast_select_fusion
  54.1 0.7 fusion.8
  54.8 0.0 all-gather.8.cloned.1.call-update
  54.8 0.0 all-gather.6.cloned.1.call-start
  54.9 0.7 all-gather.6.cloned.1.call-update
  55.6 0.2 all-gather.4.cloned.1.call-start
  55.8 0.5 all-gather.4.cloned.1.call-update
  56.3 0.0 copy-done.1
  56.3 0.8 reshape.321.gate_ref
  57.1 0.6 multiply_add_fusion.kidx_ref
  57.7 0.6 multiply_add_fusion.1.kidx_ref
  58.3 0.6 multiply_add_fusion.2.kidx_ref
  58.9 1.2 add_select_fusion.qidx_ref
  60.1 75.7 %all-gather.8.cloned.1.call-done.k_ref.v_ref = bf16[1024,1024]{1,0:T(8,128)(2,1)} async-done(((bf16[32,1024]{1,0:T(8,128)(2,1)}), bf16[1024,1024]{1,0:T(8,128)(2,1)}) %all-gather.8.cloned.1.call-update) | async-done | bytes 2097168 | tf_op jit(solution)/shard_map/all_gather | solution.py:161
  135.9 14.2 %shard_map.46 = (f32[288,2048]{1,0:T(8,128)}, f32[4,288,4]{2,1,0:T(8,128)}, f32[4,288,4]{2,1,0:T(8,128)}) custom-call(s32[288,1]{1,0:T(8,128)} %add_select_fusion.qidx_ref, s32[1,1024]{1,0:T(1,128)} %multiply_add_fusion.kidx_ref, f32[288,1]{1,0:T(8,128)} %reshape.321.gate_ref, bf16[288,2048]{1,0:T(8,128)(2,1)} %q_ref.5, ...), custom_call_target="tpu_custom_call" | custom-call | tf_op jit(solution)/shard_map/pallas_call | solution.py:134
  150.0 69.7 %all-gather.6.cloned.1.call-done.k_ref.v_ref = bf16[1024,1024]{1,0:T(8,128)(2,1)} async-done(((bf16[32,1024]{1,0:T(8,128)(2,1)}), bf16[1024,1024]{1,0:T(8,128)(2,1)}) %all-gather.6.cloned.1.call-update) | async-done | bytes 2097168 | tf_op jit(solution)/shard_map/all_gather | solution.py:161
  219.7 20.3 %shard_map.47 = (f32[288,2048]{1,0:T(8,128)}, f32[4,288,4]{2,1,0:T(8,128)}, f32[4,288,4]{2,1,0:T(8,128)}) custom-call(s32[288,1]{1,0:T(8,128)} %add_select_fusion.qidx_ref, s32[1,1024]{1,0:T(1,128)} %multiply_add_fusion.1.kidx_ref, f32[288,1]{1,0:T(8,128)} %reshape.321.gate_ref, bf16[288,2048]{1,0:T(8,128)(2,1)} %q_ref.5, ...), custom_call_target="tpu_custom_call" | custom-call | tf_op jit(solution)/shard_map/pallas_call | solution.py:134
  240.0 63.6 %all-gather.4.cloned.1.call-done.k_ref.v_ref = bf16[1024,1024]{1,0:T(8,128)(2,1)} async-done(((bf16[32,1024]{1,0:T(8,128)(2,1)}), bf16[1024,1024]{1,0:T(8,128)(2,1)}) %all-gather.4.cloned.1.call-update) | async-done | bytes 2097168 | tf_op jit(solution)/shard_map/all_gather | solution.py:161
  303.6 16.9 %shard_map.48 = bf16[288,2048]{1,0:T(8,128)(2,1)} custom-call(s32[288,1]{1,0:T(8,128)} %add_select_fusion.qidx_ref, s32[1,1024]{1,0:T(1,128)} %multiply_add_fusion.2.kidx_ref, f32[288,1]{1,0:T(8,128)} %reshape.321.gate_ref, bf16[288,2048]{1,0:T(8,128)(2,1)} %q_ref.5, bf16[1024,1024]{1,0:T(8,128)(2,1)} %all-gather.4.cloned.1.call-done.k_ref.v_ref, ...), custom_call_target="tpu_custom_call" | custom-call | tf_op jit(solution)/shard_map/pallas_call | solution.py:134
  (10 shorter events, 0.1 us)
Async XLA Ops:
  6.5 4.5 %copy-start = (bf16[288,1024]{1,0:T(8,128)(2,1)S(1)}, bf16[288,1024]{1,0:T(8,128)(2,1)}, u32[]{:S(2)}) copy-start(bf16[288,1024]{1,0:T(8,128)(2,1)} %param.6) | copy-start | bytes 1769476
  16.3 36.7 %all-to-all-start = ((bf16[32,10,1024]{2,1,0:T(8,128)(2,1)}), bf16[32,10,1024]{2,1,0:T(8,128)(2,1)S(1)}, u32[]{:S(2)}, u32[]{:S(2)}) async-start(bf16[32,10,1024]{2,1,0:T(8,128)(2,1)} %select_select_fusion), calls=%async_computation | async-start | bytes 2097152 | tf_op jit(solution)/shard_map/all_to_all | solution.py:150
  26.8 109.0 %all-gather.8.cloned.1.call-start = ((), (), s32[]{:S(2)}) async-start(), calls=%async_computation.3 | async-start | bytes 2162688 | tf_op jit(solution)/shard_map/all_gather | solution.py:161
  28.4 28.0 %copy-start.1 = (bf16[288]{0:T(512)(128)(2,1)S(1)}, bf16[288]{0:T(512)(128)(2,1)}, u32[]{:S(2)}) copy-start(bf16[288]{0:T(512)(128)(2,1)} %param.7) | copy-start | bytes 1732
  54.8 164.9 %all-gather.6.cloned.1.call-start = ((), (), s32[]{:S(2)}) async-start(), calls=%async_computation.2 | async-start | bytes 2162688 | tf_op jit(solution)/shard_map/all_gather | solution.py:161
  55.6 248.0 %all-gather.4.cloned.1.call-start = ((), (), s32[]{:S(2)}) async-start(), calls=%async_computation.1 | async-start | bytes 2162688 | tf_op jit(solution)/shard_map/all_gather | solution.py:161
Sparse Core Ops, SparseCore 0:
  55.0 80.8 all-gather.7
  139.0 80.6 all-gather.5
  222.9 80.6 all-gather.3

commit v3 on v1

--- a/solution.py
+++ b/solution.py
@@ -14,6 +14,7 @@
 TOK_DEV = 768
 CAP = 288
 KEY_CHUNK = 512
+CTX_X = 4
 
 
 large_negative_fill = -1e30
@@ -109,14 +110,16 @@
 
 
 def per_device(positions, queries, keys_values, router_weight):
-    devices_ctx = lax.axis_size("ctx")
-    my_rank = lax.axis_index("ctx")
+    devices_x = lax.axis_size("cx")
+    devices_ctx = lax.axis_size("cy") * devices_x
+    my_rank = lax.axis_index("cy") * devices_x + lax.axis_index("cx")
     pair_slots = (CAP + devices_ctx - 1) // devices_ctx + 1
     offsets = shard_offsets(positions, devices_ctx)
     packed = pack_forward((keys_values,), offsets, my_rank, devices_ctx, pair_slots)
-    moved = (lax.all_to_all(packed[0], "ctx", split_axis=0, concat_axis=0, tiled=True),)
+    moved = (lax.all_to_all(packed[0], ("cy", "cx"), split_axis=0, concat_axis=0, tiled=True),)
     (kv_bal,) = unpack_forward(moved, offsets, my_rank, devices_ctx, pair_slots)
-    kv_all = lax.all_gather(kv_bal, "ctx", axis=0, tiled=True)
+    kv_row = lax.all_gather(kv_bal, "cx", axis=0, tiled=True)
+    kv_all = lax.all_gather(kv_row, "cy", axis=0, tiled=True)
     key_rows = jnp.arange(SEL_DEV * devices_ctx, dtype=jnp.int32)
     kidx = (key_rows % SEL_DEV * devices_ctx + key_rows // SEL_DEV)[None, :]
     my_start = offsets[my_rank]
@@ -128,8 +131,13 @@
 
 
 def solution(mesh):
-    in_specs = (P("dp"), P(("dp", "ctx"), None), P(("dp", "ctx"), None), P(("dp", "ctx")))
-    out_specs = P(("dp", "ctx"), None)
+    devices = mesh.devices
+    split = jax.sharding.Mesh(
+        devices.reshape(devices.shape[0], devices.shape[1] // CTX_X, CTX_X), ("dp", "cy", "cx")
+    )
+    rows = ("dp", "cy", "cx")
+    in_specs = (P("dp"), P(rows, None), P(rows, None), P(rows))
+    out_specs = P(rows, None)
     return jax.shard_map(
-        per_device, mesh=mesh, in_specs=in_specs, out_specs=out_specs, check_vma=False
+        per_device, mesh=split, in_specs=in_specs, out_specs=out_specs, check_vma=False
     )

time: 195 us -> 193 us (0.990)
  waiting for transfers between devices: 117 us -> 102 us
  blocking collectives: 0 us -> 13.8 us
    all_gather x1, waiting for transfers between devices: 92.1 us -> 77.4 us  [per_device(): kv_all = lax.all_gather(kv_row, 'cy', axis=0, tiled=True)]
    all_gather x0 -> x1, blocking collectives: none -> 13.8 us  [per_device(): kv_row = lax.all_gather(kv_bal, 'cx', axis=0, tiled=True)]
where the time goes in v3:
time: 193 us
  waiting for transfers between devices  102 us (53%)
  Pallas kernels  37.2 us (19%)
  between operations  17.5 us (9%)
  blocking collectives  13.8 us (7%)
  starting transfers between devices  10.5 us (5%)
  local copies, waits for them, and re-layouts  6.16 us (3%)
  other arithmetic  5.83 us (3%)
    all_gather x1, waiting for transfers between devices, per_device(): kv_all = lax.all_gather(kv_row, 'cy', axis=0, tiled=True)  77.4 us
    pallas_call x1, Pallas kernels, local_attention(): pl.pallas_call(attention_kernel, grid=(KEY_VALUE_HEADS,), in_specs=[pl.Bl...  37.2 us
    all_to_all x1, waiting for transfers between devices, per_device(): lax.all_to_all(packed[0], ('cy', 'cx'), split_axis=0, concat_axis=0, tile...  24.7 us
    all_gather x1, blocking collectives, per_device(): kv_row = lax.all_gather(kv_bal, 'cx', axis=0, tiled=True)  13.8 us
    all_to_all x1, starting transfers between devices, per_device(): lax.all_to_all(packed[0], ('cy', 'cx'), split_axis=0, concat_axis=0, tile...  10.5 us
  transfers between devices with their start and end apart: 2, of which 2 were waited for; matrix products, arithmetic and copies ran while one was open for 2% of the time, Pallas kernels for 0%

profile of v3, /device:TPU:1, one launch (start us, length us, event | category | flops | bytes accessed | tf_op | source)
XLA Modules:
  0.0 193.1 jit_solution(9671178813399469075)
XLA Ops:
  6.5 0.0 copy-start
  6.5 1.0 convert_reduce_fusion
  7.5 0.7 fusion.10
  12.2 0.7 fusion
  12.9 0.7 fusion.3
  13.6 0.1 min.12
  13.8 0.0 copy-done
  13.8 2.1 %gather_fusion.1 = bf16[320,1024]{1,0:T(8,128)(2,1)S(1)} fusion(bf16[288,1024]{1,0:T(8,128)(2,1)S(1)} %copy-done, s32[1024]{0:T(1024)S(1)} %pad_clamp_fusion.1), kind=kCustom, calls=%fused_computation.1 | custom fusion | bytes 1312000 | tf_op jit(solution)/shard_map/jit(_take)/gather | solution.py:39
  15.9 0.2 gather.18
  16.1 1.2 select_select_fusion
  17.3 10.5 %all-to-all-start = ((bf16[32,10,1024]{2,1,0:T(8,128)(2,1)}), bf16[32,10,1024]{2,1,0:T(8,128)(2,1)S(1)}, u32[]{:S(2)}, u32[]{:S(2)}) async-start(bf16[32,10,1024]{2,1,0:T(8,128)(2,1)} %select_select_fusion), calls=%async_computation | async-start | bytes 2097152 | tf_op jit(solution)/shard_map/all_to_all | solution.py:119
  27.8 0.0 all-gather.2.cloned.1.call-start
  27.8 0.1 slice.3
  27.9 0.1 convert_reduce_fusion.1
  28.0 1.2 gather_fusion
  29.3 24.7 %all-to-all-done = bf16[32,10,1024]{2,1,0:T(8,128)(2,1)S(1)} async-done(((bf16[32,10,1024]{2,1,0:T(8,128)(2,1)}), bf16[32,10,1024]{2,1,0:T(8,128)(2,1)S(1)}, u32[]{:S(2)}, u32[]{:S(2)}) %all-to-all-start) | async-done | bytes 655392 | tf_op jit(solution)/shard_map/all_to_all | solution.py:119
  54.0 0.2 reshape.272
  54.2 0.8 gather_fusion.2
  55.0 0.0 copy-start.1
  55.0 0.1 broadcast_select_fusion
  55.1 13.8 %all_gather.6 = bf16[384,1024]{1,0:T(8,128)(2,1)} all-gather(bf16[96,1024]{1,0:T(8,128)(2,1)S(1)} %broadcast_select_fusion), channel_id=1, replica_groups=mesh['dp'=16,'cy'=8,'cx'=4] {'cx'}, dimensions={0}, use_global_device_ids=true | all-gather | bytes 983040 | tf_op jit(solution)/shard_map/all_gather | solution.py:121
  68.9 0.0 all-gather.2.cloned.1.call-update
  69.0 0.0 copy-done.1
  69.0 0.8 reshape.298.gate_ref
  69.8 1.4 add_select_fusion.qidx_ref
  71.1 0.6 fusion.5.kidx_ref
  71.8 77.4 %all-gather.2.cloned.1.call-done.k_ref.v_ref = bf16[3072,1024]{1,0:T(8,128)(2,1)} async-done(((bf16[384,1024]{1,0:T(8,128)(2,1)}), bf16[3072,1024]{1,0:T(8,128)(2,1)}) %all-gather.2.cloned.1.call-update) | async-done | bytes 6291472 | tf_op jit(solution)/shard_map/all_gather | solution.py:122
  149.1 37.2 %shard_map.46 = bf16[288,2048]{1,0:T(8,128)(2,1)} custom-call(s32[288,1]{1,0:T(8,128)} %add_select_fusion.qidx_ref, s32[1,3072]{1,0:T(1,128)} %fusion.5.kidx_ref, f32[288,1]{1,0:T(8,128)} %reshape.298.gate_ref, bf16[288,2048]{1,0:T(8,128)(2,1)} %q_ref.1, bf16[3072,1024]{1,0:T(8,128)(2,1)} %all-gather.2.cloned.1.call-done.k_ref.v_ref, ...), custom_call_target="tpu_custom_call" | custom-call | tf_op jit(solution)/shard_map/pallas_call | solution.py:95
  (10 shorter events, 0.1 us)
Async XLA Ops:
  6.5 7.2 %copy-start = (bf16[288,1024]{1,0:T(8,128)(2,1)S(1)}, bf16[288,1024]{1,0:T(8,128)(2,1)}, u32[]{:S(2)}) copy-start(bf16[288,1024]{1,0:T(8,128)(2,1)} %param.6) | copy-start | bytes 1769476
  17.3 36.7 %all-to-all-start = ((bf16[32,10,1024]{2,1,0:T(8,128)(2,1)}), bf16[32,10,1024]{2,1,0:T(8,128)(2,1)S(1)}, u32[]{:S(2)}, u32[]{:S(2)}) async-start(bf16[32,10,1024]{2,1,0:T(8,128)(2,1)} %select_select_fusion), calls=%async_computation | async-start | bytes 2097152 | tf_op jit(solution)/shard_map/all_to_all | solution.py:119
  27.8 121.3 %all-gather.2.cloned.1.call-start = ((), (), s32[]{:S(2)}) async-start(), calls=%async_computation.1 | async-start | bytes 7077888 | tf_op jit(solution)/shard_map/all_gather | solution.py:122
  55.0 14.0 %copy-start.1 = (bf16[288]{0:T(512)(128)(2,1)S(1)}, bf16[288]{0:T(512)(128)(2,1)}, u32[]{:S(2)}) copy-start(bf16[288]{0:T(512)(128)(2,1)} %param.7) | copy-start | bytes 1732
Sparse Core Ops, SparseCore 0:
  69.1 79.9 all-gather.1

commit v4 on v2

--- a/solution.py
+++ b/solution.py
@@ -15,7 +15,7 @@
 TOK_DEV = 768
 CAP = 288
 KEY_CHUNK = 512
-GATHER_CHUNKS = 3
+CTX_X = 4
 
 
 large_negative_fill = -1e30
@@ -55,11 +55,12 @@
     )
 
 
-def attention_kernel(first, last, qidx_ref, kidx_ref, gate_ref, q_ref, k_ref, v_ref, *rest):
+def attention_kernel(first, last, n_kv, qidx_ref, kidx_ref, gate_ref, q_ref, *rest):
     group_count = QUERY_HEADS // KEY_VALUE_HEADS
     rows = q_ref.shape[0]
-    keys = k_ref.shape[0]
     score_scale = 1.0 / math.sqrt(HEAD_SIZE)
+    kv_refs = rest[: 2 * n_kv]
+    rest = rest[2 * n_kv :]
     if first:
         state_in = None
         state_out = rest
@@ -78,14 +79,16 @@
             acc = state_in[0][:, cols]
             m_run = state_in[1][0, :, g : g + 1]
             l_run = state_in[2][0, :, g : g + 1]
-        for c in range(keys // KEY_CHUNK):
-            lo = c * KEY_CHUNK
-            k = k_ref[lo : lo + KEY_CHUNK, :]
-            v = v_ref[lo : lo + KEY_CHUNK, :]
+        base = 0
+        for i in range(n_kv):
+            k = kv_refs[2 * i][...]
+            v = kv_refs[2 * i + 1][...]
+            keys = k.shape[0]
             s = lax.dot_general(
                 q, k, (((1,), (1,)), ((), ())), preferred_element_type=jnp.float32
             )
-            visible = kidx_ref[:, lo : lo + KEY_CHUNK] <= qidx
+            visible = kidx_ref[:, base : base + keys] <= qidx
+            base += keys
             s = jnp.where(visible, s, large_negative_fill)
             m_new = jnp.maximum(m_run, jnp.max(s, axis=-1, keepdims=True))
             p = jnp.exp((s - m_new) * score_scale)
@@ -104,9 +107,9 @@
             state_out[2][0, :, g : g + 1] = l_run
 
 
-def local_attention(qidx, kidx, gate, queries, kv_part, state, last):
+def local_attention(qidx, kidx, gate, queries, kv_parts, state, last):
     rows = queries.shape[0]
-    keys = kv_part.shape[0]
+    keys = kidx.shape[1]
     group_count = QUERY_HEADS // KEY_VALUE_HEADS
     group_width = group_count * HEAD_SIZE
     width = QUERY_HEADS * HEAD_SIZE
@@ -118,10 +121,15 @@
         pl.BlockSpec((1, keys), lambda h: (0, 0)),
         pl.BlockSpec((rows, 1), lambda h: (0, 0)),
         pl.BlockSpec((rows, group_width), lambda h: (0, h)),
-        pl.BlockSpec((keys, HEAD_SIZE), lambda h: (0, h)),
-        pl.BlockSpec((keys, HEAD_SIZE), lambda h: (0, h + KEY_VALUE_HEADS)),
     ]
-    operands = [qidx, kidx, gate, queries, kv_part, kv_part]
+    operands = [qidx, kidx, gate, queries]
+    for part in kv_parts:
+        part_rows = part.shape[0]
+        in_specs += [
+            pl.BlockSpec((part_rows, HEAD_SIZE), lambda h: (0, h)),
+            pl.BlockSpec((part_rows, HEAD_SIZE), lambda h: (0, h + KEY_VALUE_HEADS)),
+        ]
+        operands += [part, part]
     if state is not None:
         in_specs += [acc_spec, stat_spec, stat_spec]
         operands += list(state)
@@ -132,7 +140,7 @@
         out_specs = (acc_spec, stat_spec, stat_spec)
         out_shape = (jax.ShapeDtypeStruct((rows, width), jnp.float32), stat_shape, stat_shape)
     return pl.pallas_call(
-        functools.partial(attention_kernel, state is None, last),
+        functools.partial(attention_kernel, state is None, last, len(kv_parts)),
         grid=(KEY_VALUE_HEADS,),
         in_specs=in_specs,
         out_specs=out_specs,
@@ -141,34 +149,77 @@
     )(*operands)
 
 
+def group_key_index(y_row, row_lo, row_count, devices_x, devices_ctx):
+    rows = row_lo + jnp.arange(row_count, dtype=jnp.int32)
+    source = y_row * devices_x + rows // SEL_DEV
+    return rows % SEL_DEV * devices_ctx + source
+
+
 def per_device(positions, queries, keys_values, router_weight):
-    devices_ctx = lax.axis_size("ctx")
-    my_rank = lax.axis_index("ctx")
+    devices_x = lax.axis_size("cx")
+    devices_ctx = lax.axis_size("cy") * devices_x
+    my_rank = lax.axis_index("cy") * devices_x + lax.axis_index("cx")
     pair_slots = (CAP + devices_ctx - 1) // devices_ctx + 1
     offsets = shard_offsets(positions, devices_ctx)
     packed = pack_forward((keys_values,), offsets, my_rank, devices_ctx, pair_slots)
-    moved = (lax.all_to_all(packed[0], "ctx", split_axis=0, concat_axis=0, tiled=True),)
+    moved = (lax.all_to_all(packed[0], ("cy", "cx"), split_axis=0, concat_axis=0, tiled=True),)
     (kv_bal,) = unpack_forward(moved, offsets, my_rank, devices_ctx, pair_slots)
+    kv_row = lax.all_gather(kv_bal, "cx", axis=0, tiled=True)
     my_start = offsets[my_rank]
     my_count = offsets[my_rank + 1] - my_start
     slot_ids = jnp.arange(CAP, dtype=jnp.int32)
     qidx = jnp.where(slot_ids < my_count, my_start + slot_ids, -1)[:, None]
     gate = router_weight.astype(jnp.float32)[:, None]
-    chunk_slots = SEL_DEV // GATHER_CHUNKS
-    state = None
-    for c in range(GATHER_CHUNKS):
-        part = kv_bal[c * chunk_slots : (c + 1) * chunk_slots]
-        kv_part = lax.all_gather(part, "ctx", axis=0, tiled=True)
-        key_rows = jnp.arange(chunk_slots * devices_ctx, dtype=jnp.int32)
-        kidx = ((c * chunk_slots + key_rows % chunk_slots) * devices_ctx + key_rows // chunk_slots)[None, :]
-        last = c == GATHER_CHUNKS - 1
-        state = local_attention(qidx, kidx, gate, queries, kv_part, state, last)
-    return state
+    devices_y = devices_ctx // devices_x
+    my_y = lax.axis_index("cy")
+    group_rows = kv_row.shape[0]
+    half = group_rows // 2
+    fwd = [(i, (i + 1) % devices_y) for i in range(devices_y)]
+    bwd = [(i, (i - 1) % devices_y) for i in range(devices_y)]
+
+    def kidx_of(pieces):
+        return jnp.concatenate(
+            [group_key_index(y, lo, n, devices_x, devices_ctx) for y, lo, n in pieces]
+        )[None, :]
+
+    state = local_attention(
+        qidx, kidx_of([(my_y, 0, group_rows)]), gate, queries, [kv_row], None, False
+    )
+    ahead = lax.ppermute(kv_row, "cy", fwd)
+    behind = lax.ppermute(kv_row, "cy", bwd)
+    steps = devices_y // 2
+
+    def ring_step(step, carry):
+        ahead, behind, state = carry
+        ahead_next = lax.ppermute(ahead, "cy", fwd)
+        behind_next = lax.ppermute(behind, "cy", bwd)
+        y_a = (my_y - step) % devices_y
+        y_b = (my_y + step) % devices_y
+        kidx = kidx_of([(y_a, 0, group_rows), (y_b, 0, group_rows)])
+        state = local_attention(qidx, kidx, gate, queries, [ahead, behind], state, False)
+        return ahead_next, behind_next, state
+
+    ahead, behind, state = lax.fori_loop(1, steps - 1, ring_step, (ahead, behind, state))
+    step = steps - 1
+    last_a = lax.ppermute(ahead[:half], "cy", fwd)
+    last_b = lax.ppermute(behind[half:], "cy", bwd)
+    y_a = (my_y - step) % devices_y
+    y_b = (my_y + step) % devices_y
+    kidx = kidx_of([(y_a, 0, group_rows), (y_b, 0, group_rows)])
+    state = local_attention(qidx, kidx, gate, queries, [ahead, behind], state, False)
+    y_far = (my_y + steps) % devices_y
+    kidx = kidx_of([(y_far, 0, half), (y_far, half, group_rows - half)])
+    return local_attention(qidx, kidx, gate, queries, [last_a, last_b], state, True)
 
 
 def solution(mesh):
-    in_specs = (P("dp"), P(("dp", "ctx"), None), P(("dp", "ctx"), None), P(("dp", "ctx")))
-    out_specs = P(("dp", "ctx"), None)
+    devices = mesh.devices
+    split = jax.sharding.Mesh(
+        devices.reshape(devices.shape[0], devices.shape[1] // CTX_X, CTX_X), ("dp", "cy", "cx")
+    )
+    rows = ("dp", "cy", "cx")
+    in_specs = (P("dp"), P(rows, None), P(rows, None), P(rows))
+    out_specs = P(rows, None)
     return jax.shard_map(
-        per_device, mesh=mesh, in_specs=in_specs, out_specs=out_specs, check_vma=False
-    )
+        per_device, mesh=split, in_specs=in_specs, out_specs=out_specs, check_vma=False
+    )

time: 331 us -> 210 us (0.63)
  the two profiles are of different devices: /device:TPU:1 before, /device:TPU:386 now
where the time goes in v4:
time: 210 us; the launch traced here: 209 us
  Pallas kernels  88 us (42%)
  starting transfers between devices  39.2 us (19%)
  waiting for transfers between devices  29.7 us (14%)
  local copies, waits for them, and re-layouts  25.5 us (12%)
  blocking collectives  13.6 us (6%)
  other arithmetic  8.43 us (4%)
  between operations  4.13 us (2%)
    pallas_call x5, Pallas kernels, local_attention(): pl.pallas_call(functools.partial(attention_kernel, state is None, last, l...  88 us
    all_to_all x1, waiting for transfers between devices, per_device(): lax.all_to_all(packed[0], ('cy', 'cx'), split_axis=0, concat_axis=0, tile...  26.6 us
    while x26, local copies, waits for them, and re-layouts  14.8 us
    all_gather x1, blocking collectives, per_device(): kv_row = lax.all_gather(kv_bal, 'cx', axis=0, tiled=True)  13.6 us
    ppermute x2, starting transfers between devices, ring_step(): behind_next = lax.ppermute(behind, 'cy', bwd)  10.5 us
    all_to_all x1, starting transfers between devices, per_device(): lax.all_to_all(packed[0], ('cy', 'cx'), split_axis=0, concat_axis=0, tile...  10.2 us
    ppermute x1, starting transfers between devices, per_device(): last_b = lax.ppermute(behind[half:], 'cy', bwd)  5.31 us
    ppermute x1, starting transfers between devices, per_device(): behind = lax.ppermute(kv_row, 'cy', bwd)  4.58 us
  transfers between devices with their start and end apart: 9, of which 3 were waited for; matrix products, arithmetic and copies ran while one was open for 11% of the time, Pallas kernels for 33%

profile of v4, /device:TPU:386, one launch (start us, length us, event | category | flops | bytes accessed | tf_op | source)
XLA Modules:
  0.0 208.7 jit_solution(13188260372698250240)
XLA Ops:
  0.0 1.0 convert_reduce_fusion
  1.0 0.6 fusion.30
  4.2 0.6 fusion.8
  5.0 2.1 %gather_fusion.1 = bf16[320,1024]{1,0:T(8,128)(2,1)S(1)} fusion(bf16[288,1024]{1,0:T(8,128)(2,1)S(1)} %copy-done, s32[1024]{0:T(1024)S(1)} %pad_clamp_fusion.1), kind=kCustom, calls=%fused_computation.1 | custom fusion | bytes 1312000 | tf_op jit(solution)/shard_map/jit(_take)/gather | solution.py:40
  8.6 0.7 fusion.11
  9.2 1.2 select_select_fusion
  10.4 10.2 %all-to-all-start = ((bf16[32,10,1024]{2,1,0:T(8,128)(2,1)}), bf16[32,10,1024]{2,1,0:T(8,128)(2,1)S(1)}, u32[]{:S(2)}, u32[]{:S(2)}) async-start(bf16[32,10,1024]{2,1,0:T(8,128)(2,1)} %select_select_fusion), calls=%async_computation | async-start | bytes 2097152 | tf_op jit(solution)/shard_map/all_to_all | solution.py:165
  20.9 1.2 gather_fusion
  22.2 26.6 %all-to-all-done = bf16[32,10,1024]{2,1,0:T(8,128)(2,1)S(1)} async-done(((bf16[32,10,1024]{2,1,0:T(8,128)(2,1)}), bf16[32,10,1024]{2,1,0:T(8,128)(2,1)S(1)}, u32[]{:S(2)}, u32[]{:S(2)}) %all-to-all-start) | async-done | bytes 655392 | tf_op jit(solution)/shard_map/all_to_all | solution.py:165
  49.0 0.8 gather_fusion.2
  49.9 13.6 %all_gather.3.rest_0_.rest_1_ = bf16[384,1024]{1,0:T(8,128)(2,1)S(1)} all-gather(bf16[96,1024]{1,0:T(8,128)(2,1)S(1)} %broadcast_select_fusion), channel_id=1, replica_groups=mesh['dp'=16,'cy'=8,'cx'=4] {'cx'}, dimensions={0}, use_global_device_ids=true | all-gather | bytes 983040 | tf_op jit(solution)/shard_map/all_gather | solution.py:167
  63.4 2.5 %collective-permute-start.2 = (bf16[384,1024]{1,0:T(8,128)(2,1)S(1)}, bf16[384,1024]{1,0:T(8,128)(2,1)}, u32[]{:S(2)}, u32[]{:S(2)}) collective-permute-start(bf16[384,1024]{1,0:T(8,128)(2,1)S(1)} %all_gather.3.rest_0_.rest_1_), channel_id=1, source_target_pairs={{0,4},{4,8},{8,12},{12,16},{16,20},{20,24},{24,28},{28,0},{1,5},{5... | collective-permute-start | bytes 2359304 | tf_op jit(solution)/shard_map/ppermute | solution.py:188
  65.9 4.6 %collective-permute-start.3 = (bf16[384,1024]{1,0:T(8,128)(2,1)S(1)}, bf16[384,1024]{1,0:T(8,128)(2,1)}, u32[]{:S(2)}, u32[]{:S(2)}) collective-permute-start(bf16[384,1024]{1,0:T(8,128)(2,1)S(1)} %all_gather.3.rest_0_.rest_1_), channel_id=1, source_target_pairs={{0,28},{4,0},{8,4},{12,8},{16,12},{20,16},{24,20},{28,24},{1,29},{... | collective-permute-start | bytes 2359304 | tf_op jit(solution)/shard_map/ppermute | solution.py:189
  70.6 0.6 fusion.20.kidx_ref
  71.3 1.3 add_select_fusion.3.qidx_ref
  72.6 7.9 %shard_map.46 = (f32[288,2048]{1,0:T(8,128)}, f32[4,288,4]{2,1,0:T(8,128)}, f32[4,288,4]{2,1,0:T(8,128)}) custom-call(s32[288,1]{1,0:T(8,128)} %add_select_fusion.3.qidx_ref, s32[1,384]{1,0:T(1,128)} %fusion.20.kidx_ref, f32[288,1]{1,0:T(8,128)S(1)} %reshape.301.gate_ref, bf16[288,2048]{1,0:T(8,128)(2,1)S(1)} %copy-done.3, bf16[384,1024]{1,0:T(8,128)(2,1)} %copy-done.6, ...), custom_call_target="tpu_custom_call" | custom-call | tf_op jit(solution)/shard_map/pallas_call | solution.py:142
  80.4 2.1 %collective-permute-done.2 = bf16[384,1024]{1,0:T(8,128)(2,1)} collective-permute-done((bf16[384,1024]{1,0:T(8,128)(2,1)S(1)}, bf16[384,1024]{1,0:T(8,128)(2,1)}, u32[]{:S(2)}, u32[]{:S(2)}) %collective-permute-start.2) | collective-permute-done | bytes 786464 | tf_op jit(solution)/shard_map/ppermute | solution.py:188
  82.5 1.1 collective-permute-done.3
  83.6 73.7 %while.25 = (s32[]{:T(128)}, bf16[384,1024]{1,0:T(8,128)(2,1)}, bf16[384,1024]{1,0:T(8,128)(2,1)}, f32[288,2048]{1,0:T(8,128)}, f32[4,288,4]{2,1,0:T(8,128)}, /*...) while((s32[]{:T(128)}, bf16[384,1024]{1,0:T(8,128)(2,1)}, ...), condition=%wide.region_3.4_spmd.clone, body=%wide.region_2.3_spmd.clone.sunk | while | flops 8188 | bytes 20685552 | solution.py:202
  83.6 1.1 copy.20.rest_0_.rest_1_
  84.7 2.2 %collective-permute-start = (bf16[384,1024]{1,0:T(8,128)(2,1)S(1)}, bf16[384,1024]{1,0:T(8,128)(2,1)}, u32[]{:S(2)}, u32[]{:S(2)}) collective-permute-start(bf16[384,1024]{1,0:T(8,128)(2,1)S(1)} %copy.20.rest_0_.rest_1_), channel_id=1, source_target_pairs={{0,4},{4,8},{8,12},{12,16},{16,20},{20,24},{24,28},{28,0},{1,5},{5... | collective-permute-start | bytes 2359304 | tf_op jit(solution)/shard_map/while/body/eval_jaxpr/ppermute | solution.py:194
  87.0 1.1 copy.21.rest_2_.rest_3_
  88.1 5.4 %collective-permute-start.1 = (bf16[384,1024]{1,0:T(8,128)(2,1)S(1)}, bf16[384,1024]{1,0:T(8,128)(2,1)}, u32[]{:S(2)}, u32[]{:S(2)}) collective-permute-start(bf16[384,1024]{1,0:T(8,128)(2,1)S(1)} %copy.21.rest_2_.rest_3_), channel_id=1, source_target_pairs={{0,28},{4,0},{8,4},{12,8},{16,12},{20,16},{24,20},{28,24},{1,29},{... | collective-permute-start | bytes 2359304 | tf_op jit(solution)/shard_map/while/body/eval_jaxpr/ppermute | solution.py:195
  93.6 0.6 broadcast_in_dim.97.kidx_ref
  94.2 3.4 %copy.34.rest_4_ = f32[288,2048]{1,0:T(8,128)} copy(f32[288,2048]{1,0:T(8,128)} %get-tuple-element.485) | data formatting | bytes 4718592 | tf_op jit(solution)/shard_map/while
  97.6 0.9 copy.35.rest_5_
  98.5 0.8 copy.36.rest_6_
  99.3 1.3 add_select_fusion.7.qidx_ref
  100.6 20.1 %eval_jaxpr.9 = (f32[288,2048]{1,0:T(8,128)}, f32[4,288,4]{2,1,0:T(8,128)}, f32[4,288,4]{2,1,0:T(8,128)}) custom-call(s32[288,1]{1,0:T(8,128)} %add_select_fusion.7.qidx_ref, s32[1,768]{1,0:T(1,128)} %broadcast_in_dim.97.kidx_ref, f32[288,1]{1,0:T(8,128)S(1)} %get-tuple-element.505.gate_ref, bf16[288,2048]{1,0:T(8,128)(2,1)S(1)} %get-tuple-element.506.q_ref, ...), custom_call_target="tpu_custom_call" | custom-call | tf_op jit(solution)/shard_map/while/body/eval_jaxpr/pallas_call | solution.py:142
  120.7 1.1 copy.20.rest_0_.rest_1_
  121.9 1.9 collective-permute-start
  123.8 1.1 copy.21.rest_2_.rest_3_
  124.9 5.1 %collective-permute-start.1 = (bf16[384,1024]{1,0:T(8,128)(2,1)S(1)}, bf16[384,1024]{1,0:T(8,128)(2,1)}, u32[]{:S(2)}, u32[]{:S(2)}) collective-permute-start(bf16[384,1024]{1,0:T(8,128)(2,1)S(1)} %copy.21.rest_2_.rest_3_), channel_id=1, source_target_pairs={{0,28},{4,0},{8,4},{12,8},{16,12},{20,16},{24,20},{28,24},{1,29},{... | collective-permute-start | bytes 2359304 | tf_op jit(solution)/shard_map/while/body/eval_jaxpr/ppermute | solution.py:195
  130.1 0.6 broadcast_in_dim.97.kidx_ref
  130.7 3.4 %copy.34.rest_4_ = f32[288,2048]{1,0:T(8,128)} copy(f32[288,2048]{1,0:T(8,128)} %get-tuple-element.485) | data formatting | bytes 4718592 | tf_op jit(solution)/shard_map/while
  134.2 0.9 copy.35.rest_5_
  135.0 0.8 copy.36.rest_6_
  135.8 1.3 add_select_fusion.7.qidx_ref
  137.1 20.1 %eval_jaxpr.9 = (f32[288,2048]{1,0:T(8,128)}, f32[4,288,4]{2,1,0:T(8,128)}, f32[4,288,4]{2,1,0:T(8,128)}) custom-call(s32[288,1]{1,0:T(8,128)} %add_select_fusion.7.qidx_ref, s32[1,768]{1,0:T(1,128)} %broadcast_in_dim.97.kidx_ref, f32[288,1]{1,0:T(8,128)S(1)} %get-tuple-element.505.gate_ref, bf16[288,2048]{1,0:T(8,128)(2,1)S(1)} %get-tuple-element.506.q_ref, ...), custom_call_target="tpu_custom_call" | custom-call | tf_op jit(solution)/shard_map/while/body/eval_jaxpr/pallas_call | solution.py:142
  157.3 1.0 slice.10
  158.3 1.9 collective-permute-start.4
  160.2 1.0 slice.11
  161.3 5.3 %collective-permute-start.5 = (bf16[192,1024]{1,0:T(8,128)(2,1)S(1)}, bf16[192,1024]{1,0:T(8,128)(2,1)S(1)}, u32[]{:S(2)}, u32[]{:S(2)}) collective-permute-start(bf16[192,1024]{1,0:T(8,128)(2,1)S(1)} %slice.11), channel_id=1, source_target_pairs={{0,28},{4,0},{8,4},{12,8},{16,12},{20,16},{24,20},{28,24},{1,29},{... | collective-permute-start | bytes 1179656 | tf_op jit(solution)/shard_map/ppermute | solution.py:205
  166.6 0.6 broadcast_in_dim.77.kidx_ref
  167.3 0.6 broadcast_in_dim.66.kidx_ref
  167.9 20.1 %shard_map.47 = (f32[288,2048]{1,0:T(8,128)}, f32[4,288,4]{2,1,0:T(8,128)}, f32[4,288,4]{2,1,0:T(8,128)}) custom-call(s32[288,1]{1,0:T(8,128)} %add_select_fusion.3.qidx_ref, s32[1,768]{1,0:T(1,128)} %broadcast_in_dim.77.kidx_ref, f32[288,1]{1,0:T(8,128)S(1)} %get-tuple-element.517, bf16[288,2048]{1,0:T(8,128)(2,1)S(1)} %get-tuple-element.516, ...), custom_call_target="tpu_custom_call" | custom-call | tf_op jit(solution)/shard_map/pallas_call | solution.py:142
  188.0 0.7 copy-done.7
  188.9 19.8 %shard_map.48 = bf16[288,2048]{1,0:T(8,128)(2,1)} custom-call(s32[288,1]{1,0:T(8,128)} %add_select_fusion.3.qidx_ref, s32[1,384]{1,0:T(1,128)} %broadcast_in_dim.66.kidx_ref, f32[288,1]{1,0:T(8,128)S(1)} %get-tuple-element.517, bf16[288,2048]{1,0:T(8,128)(2,1)S(1)} %get-tuple-element.516, bf16[192,1024]{1,0:T(8,128)(2,1)} %copy-done.7, ...), custom_call_target="tpu_custom_call" | custom-call | tf_op jit(solution)/shard_map/pallas_call | solution.py:142
  (58 shorter events, 1.3 us)
Async XLA Ops:
  0.0 5.0 %copy-start = (bf16[288,1024]{1,0:T(8,128)(2,1)S(1)}, bf16[288,1024]{1,0:T(8,128)(2,1)}, u32[]{:S(2)}) copy-start(bf16[288,1024]{1,0:T(8,128)(2,1)} %param.8) | copy-start | bytes 1769476
  10.4 38.3 %all-to-all-start = ((bf16[32,10,1024]{2,1,0:T(8,128)(2,1)}), bf16[32,10,1024]{2,1,0:T(8,128)(2,1)S(1)}, u32[]{:S(2)}, u32[]{:S(2)}) async-start(bf16[32,10,1024]{2,1,0:T(8,128)(2,1)} %select_select_fusion), calls=%async_computation | async-start | bytes 2097152 | tf_op jit(solution)/shard_map/all_to_all | solution.py:165
  22.2 48.3 %copy-start.9 = (bf16[288]{0:T(512)(128)(2,1)S(1)}, bf16[288]{0:T(512)(128)(2,1)}, u32[]{:S(2)}) copy-start(bf16[288]{0:T(512)(128)(2,1)} %param.9) | copy-start | bytes 1732
  22.2 50.4 %copy-start.3 = (bf16[288,2048]{1,0:T(8,128)(2,1)S(1)}, bf16[288,2048]{1,0:T(8,128)(2,1)}, u32[]{:S(2)}) copy-start(bf16[288,2048]{1,0:T(8,128)(2,1)} %q_ref.5) | copy-start | bytes 3538948
  63.4 9.1 %copy-start.6 = (bf16[384,1024]{1,0:T(8,128)(2,1)}, bf16[384,1024]{1,0:T(8,128)(2,1)S(1)}, u32[]{:S(2)}) copy-start(bf16[384,1024]{1,0:T(8,128)(2,1)S(1)} %all_gather.3.rest_0_.rest_1_) | copy-start | bytes 2359300
  63.4 19.1 %collective-permute-start.2 = (bf16[384,1024]{1,0:T(8,128)(2,1)S(1)}, bf16[384,1024]{1,0:T(8,128)(2,1)}, u32[]{:S(2)}, u32[]{:S(2)}) collective-permute-start(bf16[384,1024]{1,0:T(8,128)(2,1)S(1)} %all_gather.3.rest_0_.rest_1_), channel_id=1, source_target_pairs={{0,4},{4,8},{8,12},{12,16},{16,20},{20,24},{24,28},{28,0},{1,5},{5... | collective-permute-start | bytes 2359304 | tf_op jit(solution)/shard_map/ppermute | solution.py:188
  65.9 17.7 %collective-permute-start.3 = (bf16[384,1024]{1,0:T(8,128)(2,1)S(1)}, bf16[384,1024]{1,0:T(8,128)(2,1)}, u32[]{:S(2)}, u32[]{:S(2)}) collective-permute-start(bf16[384,1024]{1,0:T(8,128)(2,1)S(1)} %all_gather.3.rest_0_.rest_1_), channel_id=1, source_target_pairs={{0,28},{4,0},{8,4},{12,8},{16,12},{20,16},{24,20},{28,24},{1,29},{... | collective-permute-start | bytes 2359304 | tf_op jit(solution)/shard_map/ppermute | solution.py:189
  84.7 12.9 %copy-start.1 = (bf16[384,1024]{1,0:T(8,128)(2,1)}, bf16[384,1024]{1,0:T(8,128)(2,1)S(1)}, u32[]{:S(2)}) copy-start(bf16[384,1024]{1,0:T(8,128)(2,1)S(1)} %copy.20.rest_0_.rest_1_) | copy-start | bytes 2359300 | tf_op jit(solution)/shard_map/while
  84.7 36.0 %collective-permute-start = (bf16[384,1024]{1,0:T(8,128)(2,1)S(1)}, bf16[384,1024]{1,0:T(8,128)(2,1)}, u32[]{:S(2)}, u32[]{:S(2)}) collective-permute-start(bf16[384,1024]{1,0:T(8,128)(2,1)S(1)} %copy.20.rest_0_.rest_1_), channel_id=1, source_target_pairs={{0,4},{4,8},{8,12},{12,16},{16,20},{20,24},{24,28},{28,0},{1,5},{5... | collective-permute-start | bytes 2359304 | tf_op jit(solution)/shard_map/while/body/eval_jaxpr/ppermute | solution.py:194
  88.1 9.5 %copy-start.2 = (bf16[384,1024]{1,0:T(8,128)(2,1)}, bf16[384,1024]{1,0:T(8,128)(2,1)S(1)}, u32[]{:S(2)}) copy-start(bf16[384,1024]{1,0:T(8,128)(2,1)S(1)} %copy.21.rest_2_.rest_3_) | copy-start | bytes 2359300 | tf_op jit(solution)/shard_map/while
  88.1 32.6 %collective-permute-start.1 = (bf16[384,1024]{1,0:T(8,128)(2,1)S(1)}, bf16[384,1024]{1,0:T(8,128)(2,1)}, u32[]{:S(2)}, u32[]{:S(2)}) collective-permute-start(bf16[384,1024]{1,0:T(8,128)(2,1)S(1)} %copy.21.rest_2_.rest_3_), channel_id=1, source_target_pairs={{0,28},{4,0},{8,4},{12,8},{16,12},{20,16},{24,20},{28,24},{1,29},{... | collective-permute-start | bytes 2359304 | tf_op jit(solution)/shard_map/while/body/eval_jaxpr/ppermute | solution.py:195
  94.2 3.4 %copy-start.4 = (f32[4,288,4]{2,1,0:T(8,128)S(1)}, f32[4,288,4]{2,1,0:T(8,128)}, u32[]{:S(2)}) copy-start(f32[4,288,4]{2,1,0:T(8,128)} %get-tuple-element.486) | copy-start | bytes 55300 | tf_op jit(solution)/shard_map/while
  94.2 4.3 %copy-start.5 = (f32[4,288,4]{2,1,0:T(8,128)S(1)}, f32[4,288,4]{2,1,0:T(8,128)}, u32[]{:S(2)}) copy-start(f32[4,288,4]{2,1,0:T(8,128)} %get-tuple-element.487) | copy-start | bytes 55300 | tf_op jit(solution)/shard_map/while
  121.9 12.3 %copy-start.1 = (bf16[384,1024]{1,0:T(8,128)(2,1)}, bf16[384,1024]{1,0:T(8,128)(2,1)S(1)}, u32[]{:S(2)}) copy-start(bf16[384,1024]{1,0:T(8,128)(2,1)S(1)} %copy.20.rest_0_.rest_1_) | copy-start | bytes 2359300 | tf_op jit(solution)/shard_map/while
  121.9 35.4 %collective-permute-start = (bf16[384,1024]{1,0:T(8,128)(2,1)S(1)}, bf16[384,1024]{1,0:T(8,128)(2,1)}, u32[]{:S(2)}, u32[]{:S(2)}) collective-permute-start(bf16[384,1024]{1,0:T(8,128)(2,1)S(1)} %copy.20.rest_0_.rest_1_), channel_id=1, source_target_pairs={{0,4},{4,8},{8,12},{12,16},{16,20},{20,24},{24,28},{28,0},{1,5},{5... | collective-permute-start | bytes 2359304 | tf_op jit(solution)/shard_map/while/body/eval_jaxpr/ppermute | solution.py:194
  124.9 9.2 %copy-start.2 = (bf16[384,1024]{1,0:T(8,128)(2,1)}, bf16[384,1024]{1,0:T(8,128)(2,1)S(1)}, u32[]{:S(2)}) copy-start(bf16[384,1024]{1,0:T(8,128)(2,1)S(1)} %copy.21.rest_2_.rest_3_) | copy-start | bytes 2359300 | tf_op jit(solution)/shard_map/while
  124.9 32.3 %collective-permute-start.1 = (bf16[384,1024]{1,0:T(8,128)(2,1)S(1)}, bf16[384,1024]{1,0:T(8,128)(2,1)}, u32[]{:S(2)}, u32[]{:S(2)}) collective-permute-start(bf16[384,1024]{1,0:T(8,128)(2,1)S(1)} %copy.21.rest_2_.rest_3_), channel_id=1, source_target_pairs={{0,28},{4,0},{8,4},{12,8},{16,12},{20,16},{24,20},{28,24},{1,29},{... | collective-permute-start | bytes 2359304 | tf_op jit(solution)/shard_map/while/body/eval_jaxpr/ppermute | solution.py:195
  130.7 3.4 %copy-start.4 = (f32[4,288,4]{2,1,0:T(8,128)S(1)}, f32[4,288,4]{2,1,0:T(8,128)}, u32[]{:S(2)}) copy-start(f32[4,288,4]{2,1,0:T(8,128)} %get-tuple-element.486) | copy-start | bytes 55300 | tf_op jit(solution)/shard_map/while
  130.7 4.3 %copy-start.5 = (f32[4,288,4]{2,1,0:T(8,128)S(1)}, f32[4,288,4]{2,1,0:T(8,128)}, u32[]{:S(2)}) copy-start(f32[4,288,4]{2,1,0:T(8,128)} %get-tuple-element.487) | copy-start | bytes 55300 | tf_op jit(solution)/shard_map/while
  158.3 29.7 %collective-permute-start.4 = (bf16[192,1024]{1,0:T(8,128)(2,1)S(1)}, bf16[192,1024]{1,0:T(8,128)(2,1)S(1)}, u32[]{:S(2)}, u32[]{:S(2)}) collective-permute-start(bf16[192,1024]{1,0:T(8,128)(2,1)S(1)} %slice.10), channel_id=1, source_target_pairs={{0,4},{4,8},{8,12},{12,16},{16,20},{20,24},{24,28},{28,0},{1,5},{5... | collective-permute-start | bytes 1179656 | tf_op jit(solution)/shard_map/ppermute | solution.py:204
  161.3 26.7 %collective-permute-start.5 = (bf16[192,1024]{1,0:T(8,128)(2,1)S(1)}, bf16[192,1024]{1,0:T(8,128)(2,1)S(1)}, u32[]{:S(2)}, u32[]{:S(2)}) collective-permute-start(bf16[192,1024]{1,0:T(8,128)(2,1)S(1)} %slice.11), channel_id=1, source_target_pairs={{0,28},{4,0},{8,4},{12,8},{16,12},{20,16},{24,20},{28,24},{1,29},{... | collective-permute-start | bytes 1179656 | tf_op jit(solution)/shard_map/ppermute | solution.py:205
  188.0 0.8 copy-start.7
  188.0 0.9 copy-start.8

commit v5 on v4

--- a/solution.py
+++ b/solution.py
@@ -182,34 +182,55 @@
             [group_key_index(y, lo, n, devices_x, devices_ctx) for y, lo, n in pieces]
         )[None, :]
 
-    state = local_attention(
+    first = local_attention(
         qidx, kidx_of([(my_y, 0, group_rows)]), gate, queries, [kv_row], None, False
     )
     ahead = lax.ppermute(kv_row, "cy", fwd)
     behind = lax.ppermute(kv_row, "cy", bwd)
     steps = devices_y // 2
 
-    def ring_step(step, carry):
-        ahead, behind, state = carry
+    def ring_step(carry, step):
+        ahead, behind = carry
         ahead_next = lax.ppermute(ahead, "cy", fwd)
         behind_next = lax.ppermute(behind, "cy", bwd)
         y_a = (my_y - step) % devices_y
         y_b = (my_y + step) % devices_y
         kidx = kidx_of([(y_a, 0, group_rows), (y_b, 0, group_rows)])
-        state = local_attention(qidx, kidx, gate, queries, [ahead, behind], state, False)
-        return ahead_next, behind_next, state
-
-    ahead, behind, state = lax.fori_loop(1, steps - 1, ring_step, (ahead, behind, state))
+        part = local_attention(qidx, kidx, gate, queries, [ahead, behind], None, False)
+        return (ahead_next, behind_next), part
+
+    (ahead, behind), looped = lax.scan(
+        ring_step, (ahead, behind), jnp.arange(1, steps - 1, dtype=jnp.int32)
+    )
     step = steps - 1
     last_a = lax.ppermute(ahead[:half], "cy", fwd)
     last_b = lax.ppermute(behind[half:], "cy", bwd)
     y_a = (my_y - step) % devices_y
     y_b = (my_y + step) % devices_y
     kidx = kidx_of([(y_a, 0, group_rows), (y_b, 0, group_rows)])
-    state = local_attention(qidx, kidx, gate, queries, [ahead, behind], state, False)
+    third = local_attention(qidx, kidx, gate, queries, [ahead, behind], None, False)
     y_far = (my_y + steps) % devices_y
     kidx = kidx_of([(y_far, 0, half), (y_far, half, group_rows - half)])
-    return local_attention(qidx, kidx, gate, queries, [last_a, last_b], state, True)
+    fourth = local_attention(qidx, kidx, gate, queries, [last_a, last_b], None, False)
+    parts = [first, third, fourth]
+    acc_all = jnp.concatenate([looped[0]] + [p[0][None] for p in parts])
+    m_all = jnp.concatenate([looped[1]] + [p[1][None] for p in parts])
+    l_all = jnp.concatenate([looped[2]] + [p[2][None] for p in parts])
+    return combine(acc_all, m_all, l_all, qidx, gate)
+
+
+def combine(acc_all, m_all, l_all, qidx, gate):
+    count, rows = acc_all.shape[0], acc_all.shape[1]
+    score_scale = 1.0 / math.sqrt(HEAD_SIZE)
+    m_heads = jnp.transpose(m_all, (0, 2, 1, 3)).reshape(count, rows, QUERY_HEADS)
+    l_heads = jnp.transpose(l_all, (0, 2, 1, 3)).reshape(count, rows, QUERY_HEADS)
+    m_top = jnp.max(m_heads, axis=0)
+    weight = jnp.exp((m_heads - m_top[None]) * score_scale)
+    total = jnp.sum(l_heads * weight, axis=0)
+    acc = acc_all.reshape(count, rows, QUERY_HEADS, HEAD_SIZE)
+    acc = jnp.sum(acc * weight[..., None], axis=0)
+    mixed = (acc / total[..., None]).reshape(rows, QUERY_HEADS * HEAD_SIZE)
+    return jnp.where(qidx >= 0, gate * mixed, 0.0).astype(jnp.bfloat16)
 
 
 def solution(mesh):

time: 210 us -> 233 us (1.11)
  the two profiles are of different devices: /device:TPU:386 before, /device:TPU:258 now
where the time goes in v5:
time: 233 us; the launch traced here: 231 us
  local copies, waits for them, and re-layouts  78.5 us (34%)
  waiting for transfers between devices  39.8 us (17%)
  starting transfers between devices  36.2 us (16%)
  Pallas kernels  35.5 us (15%)
  other arithmetic  20.7 us (9%)
  blocking collectives  13.6 us (6%)
  between operations  4.48 us (2%)
  loops' own time  2.45 us (1%)
    pallas_call x3, Pallas kernels, local_attention(): pl.pallas_call(functools.partial(attention_kernel, state is None, last, l...  35.5 us
    all_to_all x1, waiting for transfers between devices, per_device(): lax.all_to_all(packed[0], ('cy', 'cx'), split_axis=0, concat_axis=0, tile...  26.6 us
    pallas_call x2, local copies, waits for them, and re-layouts, local_attention(): pl.pallas_call(functools.partial(attention_kernel, state is None, last, l...  26.4 us
    unnamed x28, local copies, waits for them, and re-layouts  17.9 us
    all_gather x1, blocking collectives, per_device(): kv_row = lax.all_gather(kv_bal, 'cx', axis=0, tiled=True)  13.6 us
    all_to_all x1, starting transfers between devices, per_device(): lax.all_to_all(packed[0], ('cy', 'cx'), split_axis=0, concat_axis=0, tile...  10.3 us
    ppermute x1, waiting for transfers between devices, per_device(): behind = lax.ppermute(kv_row, 'cy', bwd)  10 us
    ppermute x2, starting transfers between devices, ring_step(): behind_next = lax.ppermute(behind, 'cy', bwd)  9.73 us
  transfers between devices with their start and end apart: 9, of which 3 were waited for; matrix products, arithmetic and copies ran while one was open for 28% of the time, Pallas kernels for 9%

profile of v5, /device:TPU:258, one launch (start us, length us, event | category | flops | bytes accessed | tf_op | source)
XLA Modules:
  0.0 231.1 jit_solution(7722408841183236700)
XLA Ops:
  0.0 1.0 convert_reduce_fusion
  7.4 2.1 gather_fusion.1
  9.7 1.2 select_select_fusion
  10.9 10.3 %all-to-all-start = ((bf16[32,10,1024]{2,1,0:T(8,128)(2,1)}), bf16[32,10,1024]{2,1,0:T(8,128)(2,1)S(1)}, u32[]{:S(2)}, u32[]{:S(2)}) async-start(bf16[32,10,1024]{2,1,0:T(8,128)(2,1)} %select_select_fusion), calls=%async_computation | async-start | bytes 2097152 | tf_op jit(solution)/shard_map/all_to_all | solution.py:165
  21.4 1.2 gather_fusion
  22.7 26.6 %all-to-all-done = bf16[32,10,1024]{2,1,0:T(8,128)(2,1)S(1)} async-done(((bf16[32,10,1024]{2,1,0:T(8,128)(2,1)}), bf16[32,10,1024]{2,1,0:T(8,128)(2,1)S(1)}, u32[]{:S(2)}, u32[]{:S(2)}) %all-to-all-start) | async-done | bytes 655392 | tf_op jit(solution)/shard_map/all_to_all | solution.py:165
  50.3 13.6 %all_gather.3.rest_0_.rest_1_ = bf16[384,1024]{1,0:T(8,128)(2,1)S(1)} all-gather(bf16[96,1024]{1,0:T(8,128)(2,1)S(1)} %broadcast_select_fusion), channel_id=1, replica_groups=mesh['dp'=16,'cy'=8,'cx'=4] {'cx'}, dimensions={0}, use_global_device_ids=true | all-gather | bytes 983040 | tf_op jit(solution)/shard_map/all_gather | solution.py:167
  63.9 1.9 collective-permute-start.3
  65.8 3.9 %collective-permute-start.2 = (bf16[384,1024]{1,0:T(8,128)(2,1)S(1)}, bf16[384,1024]{1,0:T(8,128)(2,1)}, u32[]{:S(2)}, u32[]{:S(2)}) collective-permute-start(bf16[384,1024]{1,0:T(8,128)(2,1)S(1)} %all_gather.3.rest_0_.rest_1_), channel_id=1, source_target_pairs={{0,4},{4,8},{8,12},{12,16},{16,20},{20,24},{24,28},{28,0},{1,5},{5... | collective-permute-start | bytes 2359304 | tf_op jit(solution)/shard_map/ppermute | solution.py:188
  71.7 10.0 %collective-permute-done.3 = bf16[384,1024]{1,0:T(8,128)(2,1)} collective-permute-done((bf16[384,1024]{1,0:T(8,128)(2,1)S(1)}, bf16[384,1024]{1,0:T(8,128)(2,1)}, u32[]{:S(2)}, u32[]{:S(2)}) %collective-permute-start.3) | collective-permute-done | bytes 786464 | tf_op jit(solution)/shard_map/ppermute | solution.py:189
  81.8 3.1 %collective-permute-done.2 = bf16[384,1024]{1,0:T(8,128)(2,1)} collective-permute-done((bf16[384,1024]{1,0:T(8,128)(2,1)S(1)}, bf16[384,1024]{1,0:T(8,128)(2,1)}, u32[]{:S(2)}, u32[]{:S(2)}) %collective-permute-start.2) | collective-permute-done | bytes 786464 | tf_op jit(solution)/shard_map/ppermute | solution.py:188
  84.9 57.9 %while.22 = (s32[]{:T(128)}, bf16[384,1024]{1,0:T(8,128)(2,1)}, bf16[384,1024]{1,0:T(8,128)(2,1)}, f32[2,288,2048]{2,1,0:T(8,128)}, f32[2,4,288,4]{2,3,1,0:T(4,1...) while((s32[]{:T(128)}, bf16[384,1024]{1,0:T(8,128)(2,1)}, ...), condition=%wide.region_3.4_spmd.clone, body=%wide.region_2.3_spmd.clone.sunk | while | flops 13180 | bytes 16069411 | solution.py:202
  84.9 1.1 copy.79
  86.1 2.4 %collective-permute-start = (bf16[384,1024]{1,0:T(8,128)(2,1)S(1)}, bf16[384,1024]{1,0:T(8,128)(2,1)}, u32[]{:S(2)}, u32[]{:S(2)}) collective-permute-start(bf16[384,1024]{1,0:T(8,128)(2,1)S(1)} %copy.79), channel_id=1, source_target_pairs={{0,4},{4,8},{8,12},{12,16},{16,20},{20,24},{24,28},{28,0},{1,5},{5... | collective-permute-start | bytes 2359304 | tf_op jit(solution)/shard_map/while/body/eval_jaxpr/ppermute | solution.py:194
  88.5 1.1 copy.80
  89.6 4.6 %collective-permute-start.1 = (bf16[384,1024]{1,0:T(8,128)(2,1)S(1)}, bf16[384,1024]{1,0:T(8,128)(2,1)}, u32[]{:S(2)}, u32[]{:S(2)}) collective-permute-start(bf16[384,1024]{1,0:T(8,128)(2,1)S(1)} %copy.80), channel_id=1, source_target_pairs={{0,28},{4,0},{8,4},{12,8},{16,12},{20,16},{24,20},{28,24},{1,29},{... | collective-permute-start | bytes 2359304 | tf_op jit(solution)/shard_map/while/body/eval_jaxpr/ppermute | solution.py:195
  94.3 1.2 dynamic_slice.22
  97.4 13.2 %eval_jaxpr.6 = (f32[2,288,2048]{2,1,0:T(8,128)}, f32[4,288,4]{2,1,0:T(8,128)}, f32[4,288,4]{2,1,0:T(8,128)}) fusion(f32[2,288,2048]{2,1,0:T(8,128)} %get-tuple-element.417, s32[]{:T(128)S(6)} %copy.78, s32[288,1]{1,0:T(8,128)S(1)} %add_select_fusion.7, s32[1,768]{1,0:T(1,128)S(1)} %broadcast_in_dim.174, f32[288,1]{1,0:T(8,128)} %get-tuple-element.439, ...), kind=kCustom, calls=%fused_computation.4.clone.1 | custom fusion | bytes 6443140 | tf_op jit(solution)/shard_map/while/body/eval_jaxpr/pallas_call | solution.py:142
  110.6 1.3 copy.67
  111.9 1.3 copy.68
  113.9 1.1 copy.79
  115.0 1.9 collective-permute-start
  116.9 1.1 copy.80
  118.1 5.1 %collective-permute-start.1 = (bf16[384,1024]{1,0:T(8,128)(2,1)S(1)}, bf16[384,1024]{1,0:T(8,128)(2,1)}, u32[]{:S(2)}, u32[]{:S(2)}) collective-permute-start(bf16[384,1024]{1,0:T(8,128)(2,1)S(1)} %copy.80), channel_id=1, source_target_pairs={{0,28},{4,0},{8,4},{12,8},{16,12},{20,16},{24,20},{28,24},{1,29},{... | collective-permute-start | bytes 2359304 | tf_op jit(solution)/shard_map/while/body/eval_jaxpr/ppermute | solution.py:195
  123.2 1.2 dynamic_slice.22
  126.4 13.2 %eval_jaxpr.6 = (f32[2,288,2048]{2,1,0:T(8,128)}, f32[4,288,4]{2,1,0:T(8,128)}, f32[4,288,4]{2,1,0:T(8,128)}) fusion(f32[2,288,2048]{2,1,0:T(8,128)} %get-tuple-element.417, s32[]{:T(128)S(6)} %copy.78, s32[288,1]{1,0:T(8,128)S(1)} %add_select_fusion.7, s32[1,768]{1,0:T(1,128)S(1)} %broadcast_in_dim.174, f32[288,1]{1,0:T(8,128)} %get-tuple-element.439, ...), kind=kCustom, calls=%fused_computation.4.clone.1 | custom fusion | bytes 6443140 | tf_op jit(solution)/shard_map/while/body/eval_jaxpr/pallas_call | solution.py:142
  139.6 1.3 copy.67
  140.9 1.3 copy.68
  142.8 1.8 slice.10
  144.6 1.8 slice.11
  146.4 1.9 collective-permute-start.5
  148.3 4.1 %collective-permute-start.4 = (bf16[192,1024]{1,0:T(8,128)(2,1)}, bf16[192,1024]{1,0:T(8,128)(2,1)S(1)}, u32[]{:S(2)}, u32[]{:S(2)}) collective-permute-start(bf16[192,1024]{1,0:T(8,128)(2,1)} %slice.10), channel_id=1, source_target_pairs={{0,4},{4,8},{8,12},{12,16},{16,20},{20,24},{24,28},{28,0},{1,5},{5... | collective-permute-start | bytes 1179656 | tf_op jit(solution)/shard_map/ppermute | solution.py:206
  155.6 1.4 add_select_fusion.3.qidx_ref
  157.0 7.9 %shard_map.46 = (f32[288,2048]{1,0:T(8,128)}, f32[4,288,4]{2,1,0:T(8,128)}, f32[4,288,4]{2,1,0:T(8,128)}) custom-call(s32[288,1]{1,0:T(8,128)} %add_select_fusion.3.qidx_ref, s32[1,384]{1,0:T(1,128)} %fusion.25.kidx_ref, f32[288,1]{1,0:T(8,128)} %get-tuple-element.451, bf16[288,2048]{1,0:T(8,128)(2,1)S(1)} %get-tuple-element.450, ...), custom_call_target="tpu_custom_call" | custom-call | tf_op jit(solution)/shard_map/pallas_call | solution.py:142
  164.9 3.6 %copy.60 = f32[36,8,16,128]{3,2,1,0:T(8,128)} copy(f32[36,8,16,128]{3,1,2,0:T(8,128)} %bitcast.85) | data formatting | bytes 4718592
  168.5 1.9 copy.37
  171.2 5.6 %copy.59 = f32[72,8,16,128]{3,2,1,0:T(8,128)} copy(f32[72,8,16,128]{3,1,2,0:T(8,128)} %bitcast.82) | data formatting | bytes 9437184
  176.8 13.1 %shard_map.47 = (f32[288,2048]{1,0:T(8,128)}, f32[4,288,4]{2,1,0:T(8,128)}, f32[4,288,4]{2,1,0:T(8,128)}) custom-call(s32[288,1]{1,0:T(8,128)} %add_select_fusion.3.qidx_ref, s32[1,768]{1,0:T(1,128)} %broadcast_in_dim.140.kidx_ref, f32[288,1]{1,0:T(8,128)S(1)} %copy-done.2, bf16[288,2048]{1,0:T(8,128)(2,1)S(1)} %get-tuple-element.450, ...), custom_call_target="tpu_custom_call" | custom-call | tf_op jit(solution)/shard_map/pallas_call | solution.py:142
  189.9 3.6 %copy.61 = f32[36,8,16,128]{3,2,1,0:T(8,128)} copy(f32[36,8,16,128]{3,1,2,0:T(8,128)} %bitcast.84) | data formatting | bytes 4718592
  193.6 1.9 copy.38
  197.9 14.4 %shard_map.48 = (f32[288,2048]{1,0:T(8,128)}, f32[4,288,4]{2,1,0:T(8,128)}, f32[4,288,4]{2,1,0:T(8,128)}) custom-call(s32[288,1]{1,0:T(8,128)} %add_select_fusion.3.qidx_ref, s32[1,384]{1,0:T(1,128)} %broadcast_in_dim.141.kidx_ref, f32[288,1]{1,0:T(8,128)S(1)} %copy-done.2, bf16[288,2048]{1,0:T(8,128)(2,1)S(1)} %get-tuple-element.450, ...), custom_call_target="tpu_custom_call" | custom-call | tf_op jit(solution)/shard_map/pallas_call | solution.py:142
  212.3 3.7 %copy.62 = f32[36,8,16,128]{3,2,1,0:T(8,128)} copy(f32[36,8,16,128]{3,1,2,0:T(8,128)} %bitcast.83) | data formatting | bytes 4718592
  216.0 2.1 copy.39
  218.9 0.9 fusion.39
  219.9 0.9 fusion.12
  221.0 1.1 copy.42
  222.1 6.3 %fusion.8 = f32[288,16,128]{2,1,0:T(8,128)S(1)} fusion(f32[1,288,16,128]{3,2,1,0:T(8,128)} %bitcast.81, f32[1,288,16,128]{3,2,1,0:T(8,128)} %bitcast.80, f32[1,288,16,128]{3,2,1,0:T(8,128)S(1)} %bitcast.79, f32[2,288,16,128]{3,2,1,0:T(8,128)} %bitcast.77, f32[5,288,16]{2,1,0:T(8,128)} %copy.42), kind=kLoop, calls=%fused_computation.24 | loop fusion | flops 14155776 | bytes 14247936 | tf_op jit(solution)/shard_map/reduce_sum | solution.py:231
  229.3 1.8 fusion.10
  (85 shorter events, 16.7 us)
Async XLA Ops:
  0.0 7.4 %copy-start = (bf16[288,1024]{1,0:T(8,128)(2,1)S(1)}, bf16[288,1024]{1,0:T(8,128)(2,1)}, u32[]{:S(2)}) copy-start(bf16[288,1024]{1,0:T(8,128)(2,1)} %param.8) | copy-start | bytes 1769476
  10.9 38.3 %all-to-all-start = ((bf16[32,10,1024]{2,1,0:T(8,128)(2,1)}), bf16[32,10,1024]{2,1,0:T(8,128)(2,1)S(1)}, u32[]{:S(2)}, u32[]{:S(2)}) async-start(bf16[32,10,1024]{2,1,0:T(8,128)(2,1)} %select_select_fusion), calls=%async_computation | async-start | bytes 2097152 | tf_op jit(solution)/shard_map/all_to_all | solution.py:165
  22.7 47.2 %copy-start.11 = (bf16[288]{0:T(512)(128)(2,1)S(1)}, bf16[288]{0:T(512)(128)(2,1)}, u32[]{:S(2)}) copy-start(bf16[288]{0:T(512)(128)(2,1)} %param.9) | copy-start | bytes 1732
  22.7 62.3 %copy-start.1 = (bf16[288,2048]{1,0:T(8,128)(2,1)S(1)}, bf16[288,2048]{1,0:T(8,128)(2,1)}, u32[]{:S(2)}) copy-start(bf16[288,2048]{1,0:T(8,128)(2,1)} %q_ref.5) | copy-start | bytes 3538948
  63.9 21.0 %copy-start.4 = (bf16[384,1024]{1,0:T(8,128)(2,1)}, bf16[384,1024]{1,0:T(8,128)(2,1)S(1)}, u32[]{:S(2)}) copy-start(bf16[384,1024]{1,0:T(8,128)(2,1)S(1)} %all_gather.3.rest_0_.rest_1_) | copy-start | bytes 2359300
  63.9 17.9 %collective-permute-start.3 = (bf16[384,1024]{1,0:T(8,128)(2,1)S(1)}, bf16[384,1024]{1,0:T(8,128)(2,1)}, u32[]{:S(2)}, u32[]{:S(2)}) collective-permute-start(bf16[384,1024]{1,0:T(8,128)(2,1)S(1)} %all_gather.3.rest_0_.rest_1_), channel_id=1, source_target_pairs={{0,28},{4,0},{8,4},{12,8},{16,12},{20,16},{24,20},{28,24},{1,29},{... | collective-permute-start | bytes 2359304 | tf_op jit(solution)/shard_map/ppermute | solution.py:189
  65.8 19.1 %collective-permute-start.2 = (bf16[384,1024]{1,0:T(8,128)(2,1)S(1)}, bf16[384,1024]{1,0:T(8,128)(2,1)}, u32[]{:S(2)}, u32[]{:S(2)}) collective-permute-start(bf16[384,1024]{1,0:T(8,128)(2,1)S(1)} %all_gather.3.rest_0_.rest_1_), channel_id=1, source_target_pairs={{0,4},{4,8},{8,12},{12,16},{16,20},{20,24},{24,28},{28,0},{1,5},{5... | collective-permute-start | bytes 2359304 | tf_op jit(solution)/shard_map/ppermute | solution.py:188
  86.1 27.8 %collective-permute-start = (bf16[384,1024]{1,0:T(8,128)(2,1)S(1)}, bf16[384,1024]{1,0:T(8,128)(2,1)}, u32[]{:S(2)}, u32[]{:S(2)}) collective-permute-start(bf16[384,1024]{1,0:T(8,128)(2,1)S(1)} %copy.79), channel_id=1, source_target_pairs={{0,4},{4,8},{8,12},{12,16},{16,20},{20,24},{24,28},{28,0},{1,5},{5... | collective-permute-start | bytes 2359304 | tf_op jit(solution)/shard_map/while/body/eval_jaxpr/ppermute | solution.py:194
  89.6 24.3 %collective-permute-start.1 = (bf16[384,1024]{1,0:T(8,128)(2,1)S(1)}, bf16[384,1024]{1,0:T(8,128)(2,1)}, u32[]{:S(2)}, u32[]{:S(2)}) collective-permute-start(bf16[384,1024]{1,0:T(8,128)(2,1)S(1)} %copy.80), channel_id=1, source_target_pairs={{0,28},{4,0},{8,4},{12,8},{16,12},{20,16},{24,20},{28,24},{1,29},{... | collective-permute-start | bytes 2359304 | tf_op jit(solution)/shard_map/while/body/eval_jaxpr/ppermute | solution.py:195
  115.0 27.8 %collective-permute-start = (bf16[384,1024]{1,0:T(8,128)(2,1)S(1)}, bf16[384,1024]{1,0:T(8,128)(2,1)}, u32[]{:S(2)}, u32[]{:S(2)}) collective-permute-start(bf16[384,1024]{1,0:T(8,128)(2,1)S(1)} %copy.79), channel_id=1, source_target_pairs={{0,4},{4,8},{8,12},{12,16},{16,20},{20,24},{24,28},{28,0},{1,5},{5... | collective-permute-start | bytes 2359304 | tf_op jit(solution)/shard_map/while/body/eval_jaxpr/ppermute | solution.py:194
  118.1 24.8 %collective-permute-start.1 = (bf16[384,1024]{1,0:T(8,128)(2,1)S(1)}, bf16[384,1024]{1,0:T(8,128)(2,1)}, u32[]{:S(2)}, u32[]{:S(2)}) collective-permute-start(bf16[384,1024]{1,0:T(8,128)(2,1)S(1)} %copy.80), channel_id=1, source_target_pairs={{0,28},{4,0},{8,4},{12,8},{16,12},{20,16},{24,20},{28,24},{1,29},{... | collective-permute-start | bytes 2359304 | tf_op jit(solution)/shard_map/while/body/eval_jaxpr/ppermute | solution.py:195
  142.8 22.0 %copy-start.10 = (f32[2,4,288,4]{2,3,1,0:T(4,128)}, f32[2,4,288,4]{2,3,1,0:T(4,128)S(1)}, u32[]{:S(2)}) copy-start(f32[2,4,288,4]{2,3,1,0:T(4,128)S(1)} %get-tuple-element.201) | copy-start | bytes 110596
  146.4 49.9 %collective-permute-start.5 = (bf16[192,1024]{1,0:T(8,128)(2,1)}, bf16[192,1024]{1,0:T(8,128)(2,1)S(1)}, u32[]{:S(2)}, u32[]{:S(2)}) collective-permute-start(bf16[192,1024]{1,0:T(8,128)(2,1)} %slice.11), channel_id=1, source_target_pairs={{0,28},{4,0},{8,4},{12,8},{16,12},{20,16},{24,20},{28,24},{1,29},{... | collective-permute-start | bytes 1179656 | tf_op jit(solution)/shard_map/ppermute | solution.py:207
  148.3 48.0 %collective-permute-start.4 = (bf16[192,1024]{1,0:T(8,128)(2,1)}, bf16[192,1024]{1,0:T(8,128)(2,1)S(1)}, u32[]{:S(2)}, u32[]{:S(2)}) collective-permute-start(bf16[192,1024]{1,0:T(8,128)(2,1)} %slice.10), channel_id=1, source_target_pairs={{0,4},{4,8},{8,12},{12,16},{16,20},{20,24},{24,28},{28,0},{1,5},{5... | collective-permute-start | bytes 1179656 | tf_op jit(solution)/shard_map/ppermute | solution.py:206
  164.9 5.5 %copy-start.9 = (f32[4,288,4]{2,1,0:T(8,128)S(1)}, f32[4,288,4]{2,1,0:T(8,128)}, u32[]{:S(2)}) copy-start(f32[4,288,4]{2,1,0:T(8,128)} %get-tuple-element.202) | copy-start | bytes 55300
  171.2 5.6 %copy-start.2 = (f32[288,1]{1,0:T(8,128)S(1)}, f32[288,1]{1,0:T(8,128)}, u32[]{:S(2)}) copy-start(f32[288,1]{1,0:T(8,128)} %get-tuple-element.451) | copy-start | bytes 3460
  189.9 5.6 %copy-start.8 = (f32[4,288,4]{2,1,0:T(8,128)S(1)}, f32[4,288,4]{2,1,0:T(8,128)}, u32[]{:S(2)}) copy-start(f32[4,288,4]{2,1,0:T(8,128)} %get-tuple-element.203) | copy-start | bytes 55300
  196.4 0.8 copy-start.5
  197.1 0.7 copy-start.6
  212.3 5.7 %copy-start.7 = (f32[4,288,4]{2,1,0:T(8,128)S(1)}, f32[4,288,4]{2,1,0:T(8,128)}, u32[]{:S(2)}) copy-start(f32[4,288,4]{2,1,0:T(8,128)} %get-tuple-element.204) | copy-start | bytes 55300
  216.0 6.2 %copy-start.3 = (f32[36,8,16,128]{3,2,1,0:T(8,128)S(1)}, f32[36,8,16,128]{3,2,1,0:T(8,128)}, u32[]{:S(2)}) copy-start(f32[36,8,16,128]{3,2,1,0:T(8,128)} %copy.60) | copy-start | bytes 7077892

commit v6 on v3

--- a/solution.py
+++ b/solution.py
@@ -13,7 +13,8 @@
 SEL_DEV = 96
 TOK_DEV = 768
 CAP = 288
-KEY_CHUNK = 512
+KEY_TILE = 256
+ROW_TILE = 96
 CTX_X = 4
 
 
@@ -57,47 +58,56 @@
 def attention_kernel(qidx_ref, kidx_ref, gate_ref, q_ref, k_ref, v_ref, o_ref):
     group_count = QUERY_HEADS // KEY_VALUE_HEADS
     rows = q_ref.shape[0]
-    keys = k_ref.shape[0]
+    tiles = kidx_ref.shape[0]
     score_scale = 1.0 / math.sqrt(HEAD_SIZE)
-    qidx = qidx_ref[...]
-    valid = qidx >= 0
-    gate = gate_ref[...]
-    for g in range(group_count):
-        q = q_ref[:, g * HEAD_SIZE : (g + 1) * HEAD_SIZE]
-        m_run = jnp.full((rows, 1), large_negative_fill, jnp.float32)
-        l_run = jnp.zeros((rows, 1), jnp.float32)
-        acc = jnp.zeros((rows, HEAD_SIZE), jnp.float32)
-        for c in range(keys // KEY_CHUNK):
-            lo = c * KEY_CHUNK
-            k = k_ref[lo : lo + KEY_CHUNK, :]
-            v = v_ref[lo : lo + KEY_CHUNK, :]
-            s = lax.dot_general(
-                q, k, (((1,), (1,)), ((), ())), preferred_element_type=jnp.float32
+    for r in range(rows // ROW_TILE):
+        row_sel = slice(r * ROW_TILE, (r + 1) * ROW_TILE)
+        qidx = qidx_ref[row_sel, :]
+        for g in range(group_count):
+            cols = slice(g * HEAD_SIZE, (g + 1) * HEAD_SIZE)
+            q = q_ref[row_sel, cols]
+
+            def body(c, carry):
+                m_run, l_run, acc = carry
+                lo = pl.multiple_of(c * KEY_TILE, KEY_TILE)
+                k = k_ref[pl.ds(lo, KEY_TILE), :]
+                v = v_ref[pl.ds(lo, KEY_TILE), :]
+                s = lax.dot_general(
+                    q, k, (((1,), (1,)), ((), ())), preferred_element_type=jnp.float32
+                )
+                visible = kidx_ref[c] <= qidx
+                s = jnp.where(visible, s, large_negative_fill)
+                m_new = jnp.maximum(m_run, jnp.max(s, axis=-1, keepdims=True))
+                p = jnp.exp((s - m_new) * score_scale)
+                factor = jnp.exp((m_run - m_new) * score_scale)
+                l_run = l_run * factor + jnp.sum(p, axis=-1, keepdims=True)
+                acc = acc * factor + jnp.dot(
+                    p.astype(jnp.bfloat16), v, preferred_element_type=jnp.float32
+                )
+                return m_new, l_run, acc
+
+            init = (
+                jnp.full((ROW_TILE, 1), large_negative_fill, jnp.float32),
+                jnp.zeros((ROW_TILE, 1), jnp.float32),
+                jnp.zeros((ROW_TILE, HEAD_SIZE), jnp.float32),
             )
-            visible = kidx_ref[:, lo : lo + KEY_CHUNK] <= qidx
-            s = jnp.where(visible, s, large_negative_fill)
-            m_new = jnp.maximum(m_run, jnp.max(s, axis=-1, keepdims=True))
-            p = jnp.exp((s - m_new) * score_scale)
-            factor = jnp.exp((m_run - m_new) * score_scale)
-            l_run = l_run * factor + jnp.sum(p, axis=-1, keepdims=True)
-            acc = acc * factor + jnp.dot(
-                p.astype(jnp.bfloat16), v, preferred_element_type=jnp.float32
-            )
-            m_run = m_new
-        out = jnp.where(valid, gate * (acc / l_run), 0.0)
-        o_ref[:, g * HEAD_SIZE : (g + 1) * HEAD_SIZE] = out.astype(o_ref.dtype)
+            m_run, l_run, acc = lax.fori_loop(0, tiles, body, init, unroll=2)
+            out = jnp.where(qidx >= 0, gate_ref[row_sel, :] * (acc / l_run), 0.0)
+            o_ref[row_sel, cols] = out.astype(o_ref.dtype)
 
 
 def local_attention(qidx, kidx, gate, queries, kv_all):
     rows = queries.shape[0]
     keys = kv_all.shape[0]
+    tiles = keys // KEY_TILE
     group_width = (QUERY_HEADS // KEY_VALUE_HEADS) * HEAD_SIZE
+    kidx_tiles = kidx.reshape(tiles, 1, KEY_TILE)
     return pl.pallas_call(
         attention_kernel,
         grid=(KEY_VALUE_HEADS,),
         in_specs=[
             pl.BlockSpec((rows, 1), lambda h: (0, 0)),
-            pl.BlockSpec((1, keys), lambda h: (0, 0)),
+            pl.BlockSpec((tiles, 1, KEY_TILE), lambda h: (0, 0, 0)),
             pl.BlockSpec((rows, 1), lambda h: (0, 0)),
             pl.BlockSpec((rows, group_width), lambda h: (0, h)),
             pl.BlockSpec((keys, HEAD_SIZE), lambda h: (0, h)),
@@ -106,7 +116,7 @@
         out_specs=pl.BlockSpec((rows, group_width), lambda h: (0, h)),
         out_shape=jax.ShapeDtypeStruct((rows, QUERY_HEADS * HEAD_SIZE), jnp.bfloat16),
         compiler_params=pltpu.CompilerParams(dimension_semantics=("arbitrary",)),
-    )(qidx, kidx, gate, queries, kv_all, kv_all)
+    )(qidx, kidx_tiles, gate, queries, kv_all, kv_all)
 
 
 def per_device(positions, queries, keys_values, router_weight):

time: 193 us -> 342 us (1.77)
  Pallas kernels: 37.2 us -> 186 us
    pallas_call x1, Pallas kernels: 37.2 us -> 186 us  [local_attention(): pl.pallas_call(attention_kernel, grid=(KEY_VALUE_HEADS,), in_specs=[pl.Bl...]
  transfers between devices with their start and end apart: 2 -> 2, of which waited for: 2 -> 2; matrix products, arithmetic and copies ran while one was open for 2% -> 1% of each run, Pallas kernels for 0% -> 0%
where the time goes in v6:
time: 342 us
  Pallas kernels  186 us (54%)
  waiting for transfers between devices  102 us (30%)
  between operations  17.4 us (5%)
  blocking collectives  13.8 us (4%)
  starting transfers between devices  10.5 us (3%)
  local copies, waits for them, and re-layouts  6.16 us (2%)
  other arithmetic  5.72 us (2%)
    pallas_call x1, Pallas kernels, local_attention(): pl.pallas_call(attention_kernel, grid=(KEY_VALUE_HEADS,), in_specs=[pl.Bl...  186 us
    all_gather x1, waiting for transfers between devices, per_device(): kv_all = lax.all_gather(kv_row, 'cy', axis=0, tiled=True)  77.4 us
    all_to_all x1, waiting for transfers between devices, per_device(): lax.all_to_all(packed[0], ('cy', 'cx'), split_axis=0, concat_axis=0, tile...  24.7 us
    all_gather x1, blocking collectives, per_device(): kv_row = lax.all_gather(kv_bal, 'cx', axis=0, tiled=True)  13.8 us
    all_to_all x1, starting transfers between devices, per_device(): lax.all_to_all(packed[0], ('cy', 'cx'), split_axis=0, concat_axis=0, tile...  10.5 us
  transfers between devices with their start and end apart: 2, of which 2 were waited for; matrix products, arithmetic and copies ran while one was open for 1% of the time, Pallas kernels for 0%

profile of v6, /device:TPU:1, one launch (start us, length us, event | category | flops | bytes accessed | tf_op | source)
XLA Modules:
  0.0 342.0 jit_solution(4108334391952640683)
XLA Ops:
  6.5 0.0 copy-start
  6.5 1.0 convert_reduce_fusion
  7.5 0.7 fusion.10
  12.1 0.6 fusion
  12.7 0.7 fusion.3
  13.4 0.1 min.12
  13.5 0.0 copy-done
  13.5 2.1 gather_fusion.1
  15.6 0.2 gather.18
  15.8 1.2 select_select_fusion
  17.0 10.5 %all-to-all-start = ((bf16[32,10,1024]{2,1,0:T(8,128)(2,1)}), bf16[32,10,1024]{2,1,0:T(8,128)(2,1)S(1)}, u32[]{:S(2)}, u32[]{:S(2)}) async-start(bf16[32,10,1024]{2,1,0:T(8,128)(2,1)} %select_select_fusion), calls=%async_computation | async-start | bytes 2097152 | tf_op jit(solution)/shard_map/all_to_all | solution.py:129
  27.5 0.0 all-gather.2.cloned.1.call-start
  27.6 0.1 slice.3
  27.7 0.1 convert_reduce_fusion.1
  27.8 1.2 gather_fusion
  29.1 24.7 %all-to-all-done = bf16[32,10,1024]{2,1,0:T(8,128)(2,1)S(1)} async-done(((bf16[32,10,1024]{2,1,0:T(8,128)(2,1)}), bf16[32,10,1024]{2,1,0:T(8,128)(2,1)S(1)}, u32[]{:S(2)}, u32[]{:S(2)}) %all-to-all-start) | async-done | bytes 655392 | tf_op jit(solution)/shard_map/all_to_all | solution.py:129
  53.7 0.2 reshape.278
  54.0 0.8 gather_fusion.2
  54.8 0.0 copy-start.1
  54.8 0.1 broadcast_select_fusion
  54.9 13.8 %all_gather.6 = bf16[384,1024]{1,0:T(8,128)(2,1)} all-gather(bf16[96,1024]{1,0:T(8,128)(2,1)S(1)} %broadcast_select_fusion), channel_id=1, replica_groups=mesh['dp'=16,'cy'=8,'cx'=4] {'cx'}, dimensions={0}, use_global_device_ids=true | all-gather | bytes 983040 | tf_op jit(solution)/shard_map/all_gather | solution.py:131
  68.7 0.0 all-gather.2.cloned.1.call-update
  68.7 0.0 copy-done.1
  68.7 0.8 reshape.304.gate_ref
  69.5 0.6 fusion.5.kidx_ref
  70.2 1.3 add_select_fusion.qidx_ref
  71.5 77.4 %all-gather.2.cloned.1.call-done.k_ref.v_ref = bf16[3072,1024]{1,0:T(8,128)(2,1)} async-done(((bf16[384,1024]{1,0:T(8,128)(2,1)}), bf16[3072,1024]{1,0:T(8,128)(2,1)}) %all-gather.2.cloned.1.call-update) | async-done | bytes 6291472 | tf_op jit(solution)/shard_map/all_gather | solution.py:132
  148.9 186.3 %shard_map.46 = bf16[288,2048]{1,0:T(8,128)(2,1)} custom-call(s32[288,1]{1,0:T(8,128)} %add_select_fusion.qidx_ref, s32[12,1,256]{2,1,0:T(1,128)} %fusion.5.kidx_ref, f32[288,1]{1,0:T(8,128)} %reshape.304.gate_ref, bf16[288,2048]{1,0:T(8,128)(2,1)} %q_ref.1, bf16[3072,1024]{1,0:T(8,128)(2,1)} %all-gather.2.cloned.1.call-done.k_ref.v_ref, ...), custom_call_target="tpu_custom_call" | custom-call | tf_op jit(solution)/shard_map/pallas_call | solution.py:105
  (10 shorter events, 0.1 us)
Async XLA Ops:
  6.5 7.0 %copy-start = (bf16[288,1024]{1,0:T(8,128)(2,1)S(1)}, bf16[288,1024]{1,0:T(8,128)(2,1)}, u32[]{:S(2)}) copy-start(bf16[288,1024]{1,0:T(8,128)(2,1)} %param.6) | copy-start | bytes 1769476
  17.0 36.7 %all-to-all-start = ((bf16[32,10,1024]{2,1,0:T(8,128)(2,1)}), bf16[32,10,1024]{2,1,0:T(8,128)(2,1)S(1)}, u32[]{:S(2)}, u32[]{:S(2)}) async-start(bf16[32,10,1024]{2,1,0:T(8,128)(2,1)} %select_select_fusion), calls=%async_computation | async-start | bytes 2097152 | tf_op jit(solution)/shard_map/all_to_all | solution.py:129
  27.5 121.3 %all-gather.2.cloned.1.call-start = ((), (), s32[]{:S(2)}) async-start(), calls=%async_computation.1 | async-start | bytes 7077888 | tf_op jit(solution)/shard_map/all_gather | solution.py:132
  54.8 14.0 %copy-start.1 = (bf16[288]{0:T(512)(128)(2,1)S(1)}, bf16[288]{0:T(512)(128)(2,1)}, u32[]{:S(2)}) copy-start(bf16[288]{0:T(512)(128)(2,1)} %param.7) | copy-start | bytes 1732
Sparse Core Ops, SparseCore 0:
  68.8 79.9 all-gather.1

commit v7 on v3

--- a/solution.py
+++ b/solution.py
@@ -13,7 +13,7 @@
 SEL_DEV = 96
 TOK_DEV = 768
 CAP = 288
-KEY_CHUNK = 512
+KEY_CHUNK = 3072
 CTX_X = 4
 
 

time: 193 us -> 184 us (0.953)
  Pallas kernels: 37.2 us -> 28.1 us
    pallas_call x1, Pallas kernels: 37.2 us -> 28.1 us  [local_attention(): pl.pallas_call(attention_kernel, grid=(KEY_VALUE_HEADS,), in_specs=[pl.Bl...]
where the time goes in v7:
time: 184 us
  waiting for transfers between devices  102 us (55%)
  Pallas kernels  28.1 us (15%)
  between operations  17.5 us (10%)
  blocking collectives  13.8 us (8%)
  starting transfers between devices  10.5 us (6%)
  local copies, waits for them, and re-layouts  6.16 us (3%)
  other arithmetic  5.83 us (3%)
    all_gather x1, waiting for transfers between devices, per_device(): kv_all = lax.all_gather(kv_row, 'cy', axis=0, tiled=True)  77.4 us
    pallas_call x1, Pallas kernels, local_attention(): pl.pallas_call(attention_kernel, grid=(KEY_VALUE_HEADS,), in_specs=[pl.Bl...  28.1 us
    all_to_all x1, waiting for transfers between devices, per_device(): lax.all_to_all(packed[0], ('cy', 'cx'), split_axis=0, concat_axis=0, tile...  24.7 us
    all_gather x1, blocking collectives, per_device(): kv_row = lax.all_gather(kv_bal, 'cx', axis=0, tiled=True)  13.8 us
    all_to_all x1, starting transfers between devices, per_device(): lax.all_to_all(packed[0], ('cy', 'cx'), split_axis=0, concat_axis=0, tile...  10.5 us
  transfers between devices with their start and end apart: 2, of which 2 were waited for; matrix products, arithmetic and copies ran while one was open for 2% of the time, Pallas kernels for 0%

profile of v7, /device:TPU:1, one launch (start us, length us, event | category | flops | bytes accessed | tf_op | source)
XLA Modules:
  0.0 184.1 jit_solution(9763991781411347887)
XLA Ops:
  6.5 0.0 copy-start
  6.5 1.0 convert_reduce_fusion
  7.5 0.7 fusion.10
  12.2 0.7 fusion
  12.9 0.7 fusion.3
  13.6 0.1 min.12
  13.8 0.0 copy-done
  13.8 2.1 %gather_fusion.1 = bf16[320,1024]{1,0:T(8,128)(2,1)S(1)} fusion(bf16[288,1024]{1,0:T(8,128)(2,1)S(1)} %copy-done, s32[1024]{0:T(1024)S(1)} %pad_clamp_fusion.1), kind=kCustom, calls=%fused_computation.1 | custom fusion | bytes 1312000 | tf_op jit(solution)/shard_map/jit(_take)/gather | solution.py:39
  15.9 0.2 gather.18
  16.1 1.2 select_select_fusion
  17.3 10.5 %all-to-all-start = ((bf16[32,10,1024]{2,1,0:T(8,128)(2,1)}), bf16[32,10,1024]{2,1,0:T(8,128)(2,1)S(1)}, u32[]{:S(2)}, u32[]{:S(2)}) async-start(bf16[32,10,1024]{2,1,0:T(8,128)(2,1)} %select_select_fusion), calls=%async_computation | async-start | bytes 2097152 | tf_op jit(solution)/shard_map/all_to_all | solution.py:119
  27.8 0.0 all-gather.2.cloned.1.call-start
  27.8 0.1 slice.3
  27.9 0.1 convert_reduce_fusion.1
  28.0 1.2 gather_fusion
  29.3 24.7 %all-to-all-done = bf16[32,10,1024]{2,1,0:T(8,128)(2,1)S(1)} async-done(((bf16[32,10,1024]{2,1,0:T(8,128)(2,1)}), bf16[32,10,1024]{2,1,0:T(8,128)(2,1)S(1)}, u32[]{:S(2)}, u32[]{:S(2)}) %all-to-all-start) | async-done | bytes 655392 | tf_op jit(solution)/shard_map/all_to_all | solution.py:119
  54.0 0.2 reshape.272
  54.2 0.8 gather_fusion.2
  55.0 0.0 copy-start.1
  55.0 0.1 broadcast_select_fusion
  55.1 13.8 %all_gather.6 = bf16[384,1024]{1,0:T(8,128)(2,1)} all-gather(bf16[96,1024]{1,0:T(8,128)(2,1)S(1)} %broadcast_select_fusion), channel_id=1, replica_groups=mesh['dp'=16,'cy'=8,'cx'=4] {'cx'}, dimensions={0}, use_global_device_ids=true | all-gather | bytes 983040 | tf_op jit(solution)/shard_map/all_gather | solution.py:121
  68.9 0.0 all-gather.2.cloned.1.call-update
  69.0 0.0 copy-done.1
  69.0 0.8 reshape.298.gate_ref
  69.8 1.4 add_select_fusion.qidx_ref
  71.1 0.6 fusion.5.kidx_ref
  71.8 77.4 %all-gather.2.cloned.1.call-done.k_ref.v_ref = bf16[3072,1024]{1,0:T(8,128)(2,1)} async-done(((bf16[384,1024]{1,0:T(8,128)(2,1)}), bf16[3072,1024]{1,0:T(8,128)(2,1)}) %all-gather.2.cloned.1.call-update) | async-done | bytes 6291472 | tf_op jit(solution)/shard_map/all_gather | solution.py:122
  149.1 28.1 %shard_map.46 = bf16[288,2048]{1,0:T(8,128)(2,1)} custom-call(s32[288,1]{1,0:T(8,128)} %add_select_fusion.qidx_ref, s32[1,3072]{1,0:T(1,128)} %fusion.5.kidx_ref, f32[288,1]{1,0:T(8,128)} %reshape.298.gate_ref, bf16[288,2048]{1,0:T(8,128)(2,1)} %q_ref.1, bf16[3072,1024]{1,0:T(8,128)(2,1)} %all-gather.2.cloned.1.call-done.k_ref.v_ref, ...), custom_call_target="tpu_custom_call" | custom-call | tf_op jit(solution)/shard_map/pallas_call | solution.py:95
  (10 shorter events, 0.1 us)
Async XLA Ops:
  6.5 7.2 %copy-start = (bf16[288,1024]{1,0:T(8,128)(2,1)S(1)}, bf16[288,1024]{1,0:T(8,128)(2,1)}, u32[]{:S(2)}) copy-start(bf16[288,1024]{1,0:T(8,128)(2,1)} %param.6) | copy-start | bytes 1769476
  17.3 36.7 %all-to-all-start = ((bf16[32,10,1024]{2,1,0:T(8,128)(2,1)}), bf16[32,10,1024]{2,1,0:T(8,128)(2,1)S(1)}, u32[]{:S(2)}, u32[]{:S(2)}) async-start(bf16[32,10,1024]{2,1,0:T(8,128)(2,1)} %select_select_fusion), calls=%async_computation | async-start | bytes 2097152 | tf_op jit(solution)/shard_map/all_to_all | solution.py:119
  27.8 121.3 %all-gather.2.cloned.1.call-start = ((), (), s32[]{:S(2)}) async-start(), calls=%async_computation.1 | async-start | bytes 7077888 | tf_op jit(solution)/shard_map/all_gather | solution.py:122
  55.0 14.0 %copy-start.1 = (bf16[288]{0:T(512)(128)(2,1)S(1)}, bf16[288]{0:T(512)(128)(2,1)}, u32[]{:S(2)}) copy-start(bf16[288]{0:T(512)(128)(2,1)} %param.7) | copy-start | bytes 1732
Sparse Core Ops, SparseCore 0:
  69.1 79.9 all-gather.1

commit v8 on v7

--- a/solution.py
+++ b/solution.py
@@ -119,15 +119,42 @@
     moved = (lax.all_to_all(packed[0], ("cy", "cx"), split_axis=0, concat_axis=0, tiled=True),)
     (kv_bal,) = unpack_forward(moved, offsets, my_rank, devices_ctx, pair_slots)
     kv_row = lax.all_gather(kv_bal, "cx", axis=0, tiled=True)
-    kv_all = lax.all_gather(kv_row, "cy", axis=0, tiled=True)
-    key_rows = jnp.arange(SEL_DEV * devices_ctx, dtype=jnp.int32)
-    kidx = (key_rows % SEL_DEV * devices_ctx + key_rows // SEL_DEV)[None, :]
+    devices_y = devices_ctx // devices_x
+    my_y = lax.axis_index("cy")
+    group_rows = kv_row.shape[0]
+    half = group_rows // 2
+    fwd = [(i, (i + 1) % devices_y) for i in range(devices_y)]
+    bwd = [(i, (i - 1) % devices_y) for i in range(devices_y)]
+    parts = [kv_row]
+    pieces = [(my_y, 0, group_rows)]
+    ahead = kv_row
+    behind = kv_row
+    steps = devices_y // 2
+    for step in range(1, steps):
+        ahead = lax.ppermute(ahead, "cy", fwd)
+        behind = lax.ppermute(behind, "cy", bwd)
+        parts += [ahead, behind]
+        pieces += [((my_y - step) % devices_y, 0, group_rows), ((my_y + step) % devices_y, 0, group_rows)]
+    parts.append(lax.ppermute(ahead[:half], "cy", fwd))
+    parts.append(lax.ppermute(behind[half:], "cy", bwd))
+    y_far = (my_y + steps) % devices_y
+    pieces += [(y_far, 0, half), (y_far, half, group_rows - half)]
+    kv_all = jnp.concatenate(parts, axis=0)
+    kidx = jnp.concatenate(
+        [group_key_index(y, lo, n, devices_x, devices_ctx) for y, lo, n in pieces]
+    )[None, :]
     my_start = offsets[my_rank]
     my_count = offsets[my_rank + 1] - my_start
     slot_ids = jnp.arange(CAP, dtype=jnp.int32)
     qidx = jnp.where(slot_ids < my_count, my_start + slot_ids, -1)[:, None]
     gate = router_weight.astype(jnp.float32)[:, None]
     return local_attention(qidx, kidx, gate, queries, kv_all)
+
+
+def group_key_index(y_row, row_lo, row_count, devices_x, devices_ctx):
+    rows = row_lo + jnp.arange(row_count, dtype=jnp.int32)
+    source = y_row * devices_x + rows // SEL_DEV
+    return rows % SEL_DEV * devices_ctx + source
 
 
 def solution(mesh):

time: 184 us -> 161 us (0.88)
  the two profiles are of different devices: /device:TPU:1 before, /device:TPU:474 now
where the time goes in v8:
time: 161 us; the launch traced here: 160 us
  waiting for transfers between devices  52.6 us (33%)
  starting transfers between devices  36.4 us (23%)
  Pallas kernels  28.1 us (17%)
  local copies, waits for them, and re-layouts  19.6 us (12%)
  blocking collectives  14.4 us (9%)
  other arithmetic  5.14 us (3%)
  between operations  4.22 us (3%)
    pallas_call x1, Pallas kernels, local_attention(): pl.pallas_call(attention_kernel, grid=(KEY_VALUE_HEADS,), in_specs=[pl.Bl...  28.1 us
    ppermute x3, waiting for transfers between devices, per_device(): ahead = lax.ppermute(ahead, 'cy', fwd)  24.4 us
    all_to_all x1, waiting for transfers between devices, per_device(): lax.all_to_all(packed[0], ('cy', 'cx'), split_axis=0, concat_axis=0, tile...  24 us
    all_gather x1, blocking collectives, per_device(): kv_row = lax.all_gather(kv_bal, 'cx', axis=0, tiled=True)  14.4 us
    unnamed x16, local copies, waits for them, and re-layouts  11.9 us
    ppermute x3, starting transfers between devices, per_device(): ahead = lax.ppermute(ahead, 'cy', fwd)  11.2 us
    all_to_all x1, starting transfers between devices, per_device(): lax.all_to_all(packed[0], ('cy', 'cx'), split_axis=0, concat_axis=0, tile...  9.91 us
    ppermute x3, starting transfers between devices, per_device(): behind = lax.ppermute(behind, 'cy', bwd)  7.96 us
  transfers between devices with their start and end apart: 9, of which 5 were waited for; matrix products, arithmetic and copies ran while one was open for 10% of the time, Pallas kernels for 0%

profile of v8, /device:TPU:474, one launch (start us, length us, event | category | flops | bytes accessed | tf_op | source)
XLA Modules:
  0.0 160.4 jit_solution(640844440689084434)
XLA Ops:
  0.0 0.0 copy-start
  0.0 1.0 convert_reduce_fusion
  1.0 0.6 fusion.19
  3.5 0.1 slice.9
  4.3 0.6 fusion
  4.9 0.1 min.12
  5.1 0.1 convert_reduce_fusion.1
  5.2 2.1 %gather_fusion.1 = bf16[320,1024]{1,0:T(8,128)(2,1)S(1)} fusion(bf16[288,1024]{1,0:T(8,128)(2,1)S(1)} %copy-done, s32[1024]{0:T(1024)S(1)} %get-tuple-element.17), kind=kCustom, calls=%fused_computation.1 | custom fusion | bytes 1312000 | tf_op jit(solution)/shard_map/jit(_take)/gather | solution.py:39
  7.3 0.0 copy-start.3
  7.3 0.2 gather.18
  8.8 0.7 fusion.3
  9.5 1.2 select_select_fusion
  10.7 9.9 %all-to-all-start = ((bf16[32,10,1024]{2,1,0:T(8,128)(2,1)}), bf16[32,10,1024]{2,1,0:T(8,128)(2,1)S(1)}, u32[]{:S(2)}, u32[]{:S(2)}) async-start(bf16[32,10,1024]{2,1,0:T(8,128)(2,1)} %select_select_fusion), calls=%async_computation | async-start | bytes 2097152 | tf_op jit(solution)/shard_map/all_to_all | solution.py:119
  20.6 1.2 gather_fusion
  21.9 24.0 %all-to-all-done = bf16[32,10,1024]{2,1,0:T(8,128)(2,1)S(1)} async-done(((bf16[32,10,1024]{2,1,0:T(8,128)(2,1)}), bf16[32,10,1024]{2,1,0:T(8,128)(2,1)S(1)}, u32[]{:S(2)}, u32[]{:S(2)}) %all-to-all-start) | async-done | bytes 655392 | tf_op jit(solution)/shard_map/all_to_all | solution.py:119
  45.9 0.2 reshape.220
  46.1 0.8 gather_fusion.2
  46.9 0.1 broadcast_select_fusion
  47.0 14.4 %all_gather.3 = bf16[384,1024]{1,0:T(8,128)(2,1)S(1)} all-gather(bf16[96,1024]{1,0:T(8,128)(2,1)S(1)} %broadcast_select_fusion), channel_id=1, replica_groups=mesh['dp'=16,'cy'=8,'cx'=4] {'cx'}, dimensions={0}, use_global_device_ids=true | all-gather | bytes 983040 | tf_op jit(solution)/shard_map/all_gather | solution.py:121
  61.4 1.9 %collective-permute-start = (bf16[384,1024]{1,0:T(8,128)(2,1)S(1)}, bf16[384,1024]{1,0:T(8,128)(2,1)S(1)}, u32[]{:S(2)}, u32[]{:S(2)}) collective-permute-start(bf16[384,1024]{1,0:T(8,128)(2,1)S(1)} %all_gather.3), channel_id=1, source_target_pairs={{0,4},{4,8},{8,12},{12,16},{16,20},{20,24},{24,28},{28,0},{1,5},{5... | collective-permute-start | bytes 2359304 | tf_op jit(solution)/shard_map/ppermute | solution.py:134
  63.3 3.9 %collective-permute-start.1 = (bf16[384,1024]{1,0:T(8,128)(2,1)S(1)}, bf16[384,1024]{1,0:T(8,128)(2,1)S(1)}, u32[]{:S(2)}, u32[]{:S(2)}) collective-permute-start(bf16[384,1024]{1,0:T(8,128)(2,1)S(1)} %all_gather.3), channel_id=1, source_target_pairs={{0,28},{4,0},{8,4},{12,8},{16,12},{20,16},{24,20},{28,24},{1,29},{... | collective-permute-start | bytes 2359304 | tf_op jit(solution)/shard_map/ppermute | solution.py:135
  67.2 12.2 %collective-permute-done = bf16[384,1024]{1,0:T(8,128)(2,1)S(1)} collective-permute-done((bf16[384,1024]{1,0:T(8,128)(2,1)S(1)}, bf16[384,1024]{1,0:T(8,128)(2,1)S(1)}, u32[]{:S(2)}, u32[]{:S(2)}) %collective-permute-start) | collective-permute-done | bytes 786464 | tf_op jit(solution)/shard_map/ppermute | solution.py:134
  79.4 3.7 %collective-permute-start.2 = (bf16[384,1024]{1,0:T(8,128)(2,1)S(1)}, bf16[384,1024]{1,0:T(8,128)(2,1)}, u32[]{:S(2)}, u32[]{:S(2)}) collective-permute-start(bf16[384,1024]{1,0:T(8,128)(2,1)S(1)} %collective-permute-done), channel_id=1, source_target_pairs={{0,4},{4,8},{8,12},{12,16},{16,20},{20,24},{24,28},{28,0},{1,5},{5... | collective-permute-start | bytes 2359304 | tf_op jit(solution)/shard_map/ppermute | solution.py:134
  83.1 0.0 collective-permute-done.1
  83.2 2.1 %collective-permute-start.3 = (bf16[384,1024]{1,0:T(8,128)(2,1)S(1)}, bf16[384,1024]{1,0:T(8,128)(2,1)}, u32[]{:S(2)}, u32[]{:S(2)}) collective-permute-start(bf16[384,1024]{1,0:T(8,128)(2,1)S(1)} %collective-permute-done.1), channel_id=1, source_target_pairs={{0,28},{4,0},{8,4},{12,8},{16,12},{20,16},{24,20},{28,24},{1,29},{... | collective-permute-start | bytes 2359304 | tf_op jit(solution)/shard_map/ppermute | solution.py:135
  85.4 11.3 %collective-permute-done.2 = bf16[384,1024]{1,0:T(8,128)(2,1)} collective-permute-done((bf16[384,1024]{1,0:T(8,128)(2,1)S(1)}, bf16[384,1024]{1,0:T(8,128)(2,1)}, u32[]{:S(2)}, u32[]{:S(2)}) %collective-permute-start.2) | collective-permute-done | bytes 786464 | tf_op jit(solution)/shard_map/ppermute | solution.py:134
  96.7 5.5 %collective-permute-start.4 = (bf16[384,1024]{1,0:T(8,128)(2,1)}, bf16[384,1024]{1,0:T(8,128)(2,1)S(1)}, u32[]{:S(2)}, u32[]{:S(2)}) collective-permute-start(bf16[384,1024]{1,0:T(8,128)(2,1)} %collective-permute-done.2), channel_id=1, source_target_pairs={{0,4},{4,8},{8,12},{12,16},{16,20},{20,24},{24,28},{28,0},{1,5},{5... | collective-permute-start | bytes 2359304 | tf_op jit(solution)/shard_map/ppermute | solution.py:134
  102.2 0.0 collective-permute-done.3
  102.3 1.9 %collective-permute-start.5 = (bf16[384,1024]{1,0:T(8,128)(2,1)}, bf16[384,1024]{1,0:T(8,128)(2,1)S(1)}, u32[]{:S(2)}, u32[]{:S(2)}) collective-permute-start(bf16[384,1024]{1,0:T(8,128)(2,1)} %collective-permute-done.3), channel_id=1, source_target_pairs={{0,28},{4,0},{8,4},{12,8},{16,12},{20,16},{24,20},{28,24},{1,29},{... | collective-permute-start | bytes 2359304 | tf_op jit(solution)/shard_map/ppermute | solution.py:135
  104.2 0.8 reshape.246.gate_ref
  105.0 0.7 concatenate.6
  105.7 1.3 add_select_fusion.qidx_ref
  107.0 0.9 constant_dynamic-update-slice_fusion.8
  108.0 2.1 %constant_dynamic-update-slice_fusion.7 = bf16[3072,1024]{1,0:T(8,128)(2,1)} fusion(bf16[3072,1024]{1,0:T(8,128)(2,1)} %constant_dynamic-update-slice_fusion.8, bf16[384,1024]{1,0:T(8,128)(2,1)} %copy-done.1), kind=kLoop, calls=%fused_computation.16 | loop fusion | bytes 1572864
  110.0 2.1 %constant_dynamic-update-slice_fusion.6 = bf16[3072,1024]{1,0:T(8,128)(2,1)} fusion(bf16[3072,1024]{1,0:T(8,128)(2,1)} %constant_dynamic-update-slice_fusion.7, bf16[384,1024]{1,0:T(8,128)(2,1)} %copy-done.2), kind=kLoop, calls=%fused_computation.15 | loop fusion | bytes 1572864
  112.1 2.1 %constant_dynamic-update-slice_fusion.5 = bf16[3072,1024]{1,0:T(8,128)(2,1)} fusion(bf16[3072,1024]{1,0:T(8,128)(2,1)} %constant_dynamic-update-slice_fusion.6, bf16[384,1024]{1,0:T(8,128)(2,1)} %collective-permute-done.2), kind=kLoop, calls=%fused_computation.14 | loop fusion | bytes 1572864
  114.2 0.9 collective-permute-done.4
  115.1 5.5 %collective-permute-start.6 = (bf16[192,1024]{1,0:T(8,128)(2,1)S(1)}, bf16[192,1024]{1,0:T(8,128)(2,1)S(1)}, u32[]{:S(2)}, u32[]{:S(2)}) collective-permute-start(bf16[192,1024]{1,0:T(8,128)(2,1)S(1)} %slice.18), channel_id=1, source_target_pairs={{0,4},{4,8},{8,12},{12,16},{16,20},{20,24},{24,28},{28,0},{1,5},{5... | collective-permute-start | bytes 1179656 | tf_op jit(solution)/shard_map/ppermute | solution.py:138
  120.6 0.0 collective-permute-done.5
  120.7 1.9 %collective-permute-start.7 = (bf16[192,1024]{1,0:T(8,128)(2,1)S(1)}, bf16[192,1024]{1,0:T(8,128)(2,1)S(1)}, u32[]{:S(2)}, u32[]{:S(2)}) collective-permute-start(bf16[192,1024]{1,0:T(8,128)(2,1)S(1)} %slice.19), channel_id=1, source_target_pairs={{0,28},{4,0},{8,4},{12,8},{16,12},{20,16},{24,20},{28,24},{1,29},{... | collective-permute-start | bytes 1179656 | tf_op jit(solution)/shard_map/ppermute | solution.py:139
  122.6 2.1 %constant_dynamic-update-slice_fusion.4 = bf16[3072,1024]{1,0:T(8,128)(2,1)} fusion(bf16[3072,1024]{1,0:T(8,128)(2,1)} %constant_dynamic-update-slice_fusion.5, bf16[384,1024]{1,0:T(8,128)(2,1)} %collective-permute-done.3), kind=kLoop, calls=%fused_computation.13 | loop fusion | bytes 1572864
  124.7 0.9 constant_dynamic-update-slice_fusion.3
  125.6 1.0 constant_dynamic-update-slice_fusion.2
  126.6 0.0 collective-permute-done.6
  126.6 0.8 constant_dynamic-update-slice_fusion.1
  127.4 4.2 %collective-permute-done.7 = bf16[192,1024]{1,0:T(8,128)(2,1)S(1)} collective-permute-done((bf16[192,1024]{1,0:T(8,128)(2,1)S(1)}, bf16[192,1024]{1,0:T(8,128)(2,1)S(1)}, u32[]{:S(2)}, u32[]{:S(2)}) %collective-permute-start.7) | collective-permute-done | bytes 393248 | tf_op jit(solution)/shard_map/ppermute | solution.py:139
  131.6 0.8 constant_dynamic-update-slice_fusion.k_ref.v_ref
  132.3 28.1 %shard_map.46 = bf16[288,2048]{1,0:T(8,128)(2,1)} custom-call(s32[288,1]{1,0:T(8,128)} %add_select_fusion.qidx_ref, s32[1,3072]{1,0:T(1,128)} %bitcast.22, f32[288,1]{1,0:T(8,128)} %reshape.246.gate_ref, bf16[288,2048]{1,0:T(8,128)(2,1)} %q_ref.1, bf16[3072,1024]{1,0:T(8,128)(2,1)} %constant_dynamic-update-slice_fusion.k_ref.v_ref, ...), custom_call_target="tpu_custom_call" | custom-call | tf_op jit(solution)/shard_map/pallas_call | solution.py:95
  (22 shorter events, 0.2 us)
Async XLA Ops:
  0.0 5.2 %copy-start = (bf16[288,1024]{1,0:T(8,128)(2,1)S(1)}, bf16[288,1024]{1,0:T(8,128)(2,1)}, u32[]{:S(2)}) copy-start(bf16[288,1024]{1,0:T(8,128)(2,1)} %param.6) | copy-start | bytes 1769476
  7.3 96.9 %copy-start.3 = (bf16[288]{0:T(512)(128)(2,1)S(1)}, bf16[288]{0:T(512)(128)(2,1)}, u32[]{:S(2)}) copy-start(bf16[288]{0:T(512)(128)(2,1)} %param.7) | copy-start | bytes 1732
  10.7 35.2 %all-to-all-start = ((bf16[32,10,1024]{2,1,0:T(8,128)(2,1)}), bf16[32,10,1024]{2,1,0:T(8,128)(2,1)S(1)}, u32[]{:S(2)}, u32[]{:S(2)}) async-start(bf16[32,10,1024]{2,1,0:T(8,128)(2,1)} %select_select_fusion), calls=%async_computation | async-start | bytes 2097152 | tf_op jit(solution)/shard_map/all_to_all | solution.py:119
  61.4 18.0 %collective-permute-start = (bf16[384,1024]{1,0:T(8,128)(2,1)S(1)}, bf16[384,1024]{1,0:T(8,128)(2,1)S(1)}, u32[]{:S(2)}, u32[]{:S(2)}) collective-permute-start(bf16[384,1024]{1,0:T(8,128)(2,1)S(1)} %all_gather.3), channel_id=1, source_target_pairs={{0,4},{4,8},{8,12},{12,16},{16,20},{20,24},{24,28},{28,0},{1,5},{5... | collective-permute-start | bytes 2359304 | tf_op jit(solution)/shard_map/ppermute | solution.py:134
  63.3 19.9 %collective-permute-start.1 = (bf16[384,1024]{1,0:T(8,128)(2,1)S(1)}, bf16[384,1024]{1,0:T(8,128)(2,1)S(1)}, u32[]{:S(2)}, u32[]{:S(2)}) collective-permute-start(bf16[384,1024]{1,0:T(8,128)(2,1)S(1)} %all_gather.3), channel_id=1, source_target_pairs={{0,28},{4,0},{8,4},{12,8},{16,12},{20,16},{24,20},{28,24},{1,29},{... | collective-permute-start | bytes 2359304 | tf_op jit(solution)/shard_map/ppermute | solution.py:135
  79.4 6.0 %copy-start.1 = (bf16[384,1024]{1,0:T(8,128)(2,1)}, bf16[384,1024]{1,0:T(8,128)(2,1)S(1)}, u32[]{:S(2)}) copy-start(bf16[384,1024]{1,0:T(8,128)(2,1)S(1)} %collective-permute-done) | copy-start | bytes 2359300
  79.4 17.3 %collective-permute-start.2 = (bf16[384,1024]{1,0:T(8,128)(2,1)S(1)}, bf16[384,1024]{1,0:T(8,128)(2,1)}, u32[]{:S(2)}, u32[]{:S(2)}) collective-permute-start(bf16[384,1024]{1,0:T(8,128)(2,1)S(1)} %collective-permute-done), channel_id=1, source_target_pairs={{0,4},{4,8},{8,12},{12,16},{16,20},{20,24},{24,28},{28,0},{1,5},{5... | collective-permute-start | bytes 2359304 | tf_op jit(solution)/shard_map/ppermute | solution.py:134
  83.1 19.1 %copy-start.2 = (bf16[384,1024]{1,0:T(8,128)(2,1)}, bf16[384,1024]{1,0:T(8,128)(2,1)S(1)}, u32[]{:S(2)}) copy-start(bf16[384,1024]{1,0:T(8,128)(2,1)S(1)} %collective-permute-done.1) | copy-start | bytes 2359300
  83.2 19.1 %collective-permute-start.3 = (bf16[384,1024]{1,0:T(8,128)(2,1)S(1)}, bf16[384,1024]{1,0:T(8,128)(2,1)}, u32[]{:S(2)}, u32[]{:S(2)}) collective-permute-start(bf16[384,1024]{1,0:T(8,128)(2,1)S(1)} %collective-permute-done.1), channel_id=1, source_target_pairs={{0,28},{4,0},{8,4},{12,8},{16,12},{20,16},{24,20},{28,24},{1,29},{... | collective-permute-start | bytes 2359304 | tf_op jit(solution)/shard_map/ppermute | solution.py:135
  96.7 18.4 %collective-permute-start.4 = (bf16[384,1024]{1,0:T(8,128)(2,1)}, bf16[384,1024]{1,0:T(8,128)(2,1)S(1)}, u32[]{:S(2)}, u32[]{:S(2)}) collective-permute-start(bf16[384,1024]{1,0:T(8,128)(2,1)} %collective-permute-done.2), channel_id=1, source_target_pairs={{0,4},{4,8},{8,12},{12,16},{16,20},{20,24},{24,28},{28,0},{1,5},{5... | collective-permute-start | bytes 2359304 | tf_op jit(solution)/shard_map/ppermute | solution.py:134
  102.3 18.4 %collective-permute-start.5 = (bf16[384,1024]{1,0:T(8,128)(2,1)}, bf16[384,1024]{1,0:T(8,128)(2,1)S(1)}, u32[]{:S(2)}, u32[]{:S(2)}) collective-permute-start(bf16[384,1024]{1,0:T(8,128)(2,1)} %collective-permute-done.3), channel_id=1, source_target_pairs={{0,28},{4,0},{8,4},{12,8},{16,12},{20,16},{24,20},{28,24},{1,29},{... | collective-permute-start | bytes 2359304 | tf_op jit(solution)/shard_map/ppermute | solution.py:135
  115.1 11.5 %collective-permute-start.6 = (bf16[192,1024]{1,0:T(8,128)(2,1)S(1)}, bf16[192,1024]{1,0:T(8,128)(2,1)S(1)}, u32[]{:S(2)}, u32[]{:S(2)}) collective-permute-start(bf16[192,1024]{1,0:T(8,128)(2,1)S(1)} %slice.18), channel_id=1, source_target_pairs={{0,4},{4,8},{8,12},{12,16},{16,20},{20,24},{24,28},{28,0},{1,5},{5... | collective-permute-start | bytes 1179656 | tf_op jit(solution)/shard_map/ppermute | solution.py:138
  120.7 10.9 %collective-permute-start.7 = (bf16[192,1024]{1,0:T(8,128)(2,1)S(1)}, bf16[192,1024]{1,0:T(8,128)(2,1)S(1)}, u32[]{:S(2)}, u32[]{:S(2)}) collective-permute-start(bf16[192,1024]{1,0:T(8,128)(2,1)S(1)} %slice.19), channel_id=1, source_target_pairs={{0,28},{4,0},{8,4},{12,8},{16,12},{20,16},{24,20},{28,24},{1,29},{... | collective-permute-start | bytes 1179656 | tf_op jit(solution)/shard_map/ppermute | solution.py:139

commit v9 on v8

--- a/solution.py
+++ b/solution.py
@@ -118,15 +118,40 @@
     packed = pack_forward((keys_values,), offsets, my_rank, devices_ctx, pair_slots)
     moved = (lax.all_to_all(packed[0], ("cy", "cx"), split_axis=0, concat_axis=0, tiled=True),)
     (kv_bal,) = unpack_forward(moved, offsets, my_rank, devices_ctx, pair_slots)
-    kv_row = lax.all_gather(kv_bal, "cx", axis=0, tiled=True)
+    my_x = lax.axis_index("cx")
     devices_y = devices_ctx // devices_x
     my_y = lax.axis_index("cy")
+    slots = kv_bal.shape[0]
+    slot_half = slots // 2
+    x_fwd = [(i, (i + 1) % devices_x) for i in range(devices_x)]
+    x_bwd = [(i, (i - 1) % devices_x) for i in range(devices_x)]
+    from_left = lax.ppermute(kv_bal, "cx", x_fwd)
+    from_right = lax.ppermute(kv_bal, "cx", x_bwd)
+    far_a = lax.ppermute(from_left[:slot_half], "cx", x_fwd)
+    far_b = lax.ppermute(from_right[slot_half:], "cx", x_bwd)
+    kv_row = jnp.concatenate([kv_bal, from_left, from_right, far_a, far_b], axis=0)
+    x_blocks = [
+        (my_x, 0, slots),
+        ((my_x - 1) % devices_x, 0, slots),
+        ((my_x + 1) % devices_x, 0, slots),
+        ((my_x + 2) % devices_x, 0, slot_half),
+        ((my_x + 2) % devices_x, slot_half, slots - slot_half),
+    ]
+
+    def row_key_index(y_row):
+        return jnp.concatenate(
+            [
+                (lo + jnp.arange(n, dtype=jnp.int32)) * devices_ctx + y_row * devices_x + x
+                for x, lo, n in x_blocks
+            ]
+        )
+
     group_rows = kv_row.shape[0]
     half = group_rows // 2
     fwd = [(i, (i + 1) % devices_y) for i in range(devices_y)]
     bwd = [(i, (i - 1) % devices_y) for i in range(devices_y)]
     parts = [kv_row]
-    pieces = [(my_y, 0, group_rows)]
+    keys = [row_key_index(my_y)]
     ahead = kv_row
     behind = kv_row
     steps = devices_y // 2
@@ -134,27 +159,19 @@
         ahead = lax.ppermute(ahead, "cy", fwd)
         behind = lax.ppermute(behind, "cy", bwd)
         parts += [ahead, behind]
-        pieces += [((my_y - step) % devices_y, 0, group_rows), ((my_y + step) % devices_y, 0, group_rows)]
+        keys += [row_key_index((my_y - step) % devices_y), row_key_index((my_y + step) % devices_y)]
     parts.append(lax.ppermute(ahead[:half], "cy", fwd))
     parts.append(lax.ppermute(behind[half:], "cy", bwd))
-    y_far = (my_y + steps) % devices_y
-    pieces += [(y_far, 0, half), (y_far, half, group_rows - half)]
+    far_keys = row_key_index((my_y + steps) % devices_y)
+    keys += [far_keys[:half], far_keys[half:]]
     kv_all = jnp.concatenate(parts, axis=0)
-    kidx = jnp.concatenate(
-        [group_key_index(y, lo, n, devices_x, devices_ctx) for y, lo, n in pieces]
-    )[None, :]
+    kidx = jnp.concatenate(keys)[None, :]
     my_start = offsets[my_rank]
     my_count = offsets[my_rank + 1] - my_start
     slot_ids = jnp.arange(CAP, dtype=jnp.int32)
     qidx = jnp.where(slot_ids < my_count, my_start + slot_ids, -1)[:, None]
     gate = router_weight.astype(jnp.float32)[:, None]
     return local_attention(qidx, kidx, gate, queries, kv_all)
-
-
-def group_key_index(y_row, row_lo, row_count, devices_x, devices_ctx):
-    rows = row_lo + jnp.arange(row_count, dtype=jnp.int32)
-    source = y_row * devices_x + rows // SEL_DEV
-    return rows % SEL_DEV * devices_ctx + source
 
 
 def solution(mesh):

time: 161 us -> 166 us (1.031)
  the two profiles are of different devices: /device:TPU:474 before, /device:TPU:376 now
where the time goes in v9:
time: 166 us; the launch traced here: 165 us
  waiting for transfers between devices  58.6 us (35%)
  starting transfers between devices  47.9 us (29%)
  Pallas kernels  28.1 us (17%)
  local copies, waits for them, and re-layouts  20.9 us (13%)
  other arithmetic  5.2 us (3%)
  between operations  4.43 us (3%)
    ppermute x3, waiting for transfers between devices, per_device(): ahead = lax.ppermute(ahead, 'cy', fwd)  29.7 us
    pallas_call x1, Pallas kernels, local_attention(): pl.pallas_call(attention_kernel, grid=(KEY_VALUE_HEADS,), in_specs=[pl.Bl...  28.1 us
    all_to_all x1, waiting for transfers between devices, per_device(): lax.all_to_all(packed[0], ('cy', 'cx'), split_axis=0, concat_axis=0, tile...  24.2 us
    unnamed x17, local copies, waits for them, and re-layouts  12.6 us
    ppermute x3, starting transfers between devices, per_device(): ahead = lax.ppermute(ahead, 'cy', fwd)  12.5 us
    all_to_all x1, starting transfers between devices, per_device(): lax.all_to_all(packed[0], ('cy', 'cx'), split_axis=0, concat_axis=0, tile...  9.55 us
    ppermute x3, starting transfers between devices, per_device(): behind = lax.ppermute(behind, 'cy', bwd)  5.92 us
    ppermute x1, starting transfers between devices, per_device(): far_b = lax.ppermute(from_right[slot_half:], 'cx', x_bwd)  5.13 us
  transfers between devices with their start and end apart: 13, of which 7 were waited for; matrix products, arithmetic and copies ran while one was open for 10% of the time, Pallas kernels for 0%

profile of v9, /device:TPU:376, one launch (start us, length us, event | category | flops | bytes accessed | tf_op | source)
XLA Modules:
  0.0 165.2 jit_solution(12074709967464953097)
XLA Ops:
  0.0 1.0 convert_reduce_fusion
  1.0 0.6 fusion.17
  4.3 0.6 fusion
  4.9 0.1 min.12
  5.2 2.1 %gather_fusion.1 = bf16[320,1024]{1,0:T(8,128)(2,1)S(1)} fusion(bf16[288,1024]{1,0:T(8,128)(2,1)S(1)} %copy-done, s32[1024]{0:T(1024)S(1)} %get-tuple-element.59), kind=kCustom, calls=%fused_computation.1 | custom fusion | bytes 1312000 | tf_op jit(solution)/shard_map/jit(_take)/gather | solution.py:39
  7.3 0.2 gather.18
  8.8 0.7 fusion.3
  9.4 1.2 select_select_fusion
  10.6 9.6 %all-to-all-start = ((bf16[32,10,1024]{2,1,0:T(8,128)(2,1)}), bf16[32,10,1024]{2,1,0:T(8,128)(2,1)S(1)}, u32[]{:S(2)}, u32[]{:S(2)}) async-start(bf16[32,10,1024]{2,1,0:T(8,128)(2,1)} %select_select_fusion), calls=%async_computation | async-start | bytes 2097152 | tf_op jit(solution)/shard_map/all_to_all | solution.py:119
  20.3 1.2 gather_fusion
  21.6 24.2 %all-to-all-done = bf16[32,10,1024]{2,1,0:T(8,128)(2,1)S(1)} async-done(((bf16[32,10,1024]{2,1,0:T(8,128)(2,1)}), bf16[32,10,1024]{2,1,0:T(8,128)(2,1)S(1)}, u32[]{:S(2)}, u32[]{:S(2)}) %all-to-all-start) | async-done | bytes 655392 | tf_op jit(solution)/shard_map/all_to_all | solution.py:119
  45.8 0.2 reshape.220
  46.0 0.8 gather_fusion.2
  46.8 0.1 constant_dynamic-update-slice_fusion.4
  46.9 1.9 %collective-permute-start = (bf16[96,1024]{1,0:T(8,128)(2,1)S(1)}, bf16[96,1024]{1,0:T(8,128)(2,1)S(1)}, u32[]{:S(2)}, u32[]{:S(2)}) collective-permute-start(bf16[96,1024]{1,0:T(8,128)(2,1)S(1)} %get-tuple-element.6), channel_id=1, source_target_pairs={{0,1},{1,2},{2,3},{3,0},{4,5},{5,6},{6,7},{7,4},{8,9},{9,10},{10,1... | collective-permute-start | bytes 589832 | tf_op jit(solution)/shard_map/ppermute | solution.py:128
  48.8 5.1 %collective-permute-start.1 = (bf16[96,1024]{1,0:T(8,128)(2,1)S(1)}, bf16[96,1024]{1,0:T(8,128)(2,1)S(1)}, u32[]{:S(2)}, u32[]{:S(2)}) collective-permute-start(bf16[96,1024]{1,0:T(8,128)(2,1)S(1)} %get-tuple-element.6), channel_id=1, source_target_pairs={{0,3},{1,0},{2,1},{3,2},{4,7},{5,4},{6,5},{7,6},{8,11},{9,8},{10,9... | collective-permute-start | bytes 589832 | tf_op jit(solution)/shard_map/ppermute | solution.py:129
  54.0 0.7 constant_dynamic-update-slice_fusion.17
  54.6 1.0 collective-permute-done
  55.7 1.9 %collective-permute-start.2 = (bf16[48,1024]{1,0:T(8,128)(2,1)S(1)}, bf16[48,1024]{1,0:T(8,128)(2,1)S(1)}, u32[]{:S(2)}, u32[]{:S(2)}) collective-permute-start(bf16[48,1024]{1,0:T(8,128)(2,1)S(1)} %slice.30), channel_id=1, source_target_pairs={{0,1},{1,2},{2,3},{3,0},{4,5},{5,6},{6,7},{7,4},{8,9},{9,10},{10,1... | collective-permute-start | bytes 294920 | tf_op jit(solution)/shard_map/ppermute | solution.py:130
  57.6 5.1 %collective-permute-start.3 = (bf16[48,1024]{1,0:T(8,128)(2,1)S(1)}, bf16[48,1024]{1,0:T(8,128)(2,1)S(1)}, u32[]{:S(2)}, u32[]{:S(2)}) collective-permute-start(bf16[48,1024]{1,0:T(8,128)(2,1)S(1)} %slice.31), channel_id=1, source_target_pairs={{0,3},{1,0},{2,1},{3,2},{4,7},{5,4},{6,5},{7,6},{8,11},{9,8},{10,9... | collective-permute-start | bytes 294920 | tf_op jit(solution)/shard_map/ppermute | solution.py:131
  62.8 0.7 constant_dynamic-update-slice_fusion.3
  63.5 0.7 constant_dynamic-update-slice_fusion.2
  64.2 0.7 constant_dynamic-update-slice_fusion.1
  65.0 0.6 constant_dynamic-update-slice_fusion
  65.6 4.6 %collective-permute-start.4 = (bf16[384,1024]{1,0:T(8,128)(2,1)S(1)}, bf16[384,1024]{1,0:T(8,128)(2,1)S(1)}, u32[]{:S(2)}, u32[]{:S(2)}) collective-permute-start(bf16[384,1024]{1,0:T(8,128)(2,1)S(1)} %get-tuple-element.11), channel_id=1, source_target_pairs={{0,4},{4,8},{8,12},{12,16},{16,20},{20,24},{24,28},{28,0},{1,5},{5... | collective-permute-start | bytes 2359304 | tf_op jit(solution)/shard_map/ppermute | solution.py:159
  70.2 1.9 %collective-permute-start.5 = (bf16[384,1024]{1,0:T(8,128)(2,1)S(1)}, bf16[384,1024]{1,0:T(8,128)(2,1)S(1)}, u32[]{:S(2)}, u32[]{:S(2)}) collective-permute-start(bf16[384,1024]{1,0:T(8,128)(2,1)S(1)} %get-tuple-element.11), channel_id=1, source_target_pairs={{0,28},{4,0},{8,4},{12,8},{16,12},{20,16},{24,20},{28,24},{1,29},{... | collective-permute-start | bytes 2359304 | tf_op jit(solution)/shard_map/ppermute | solution.py:160
  72.2 12.9 %collective-permute-done.4 = bf16[384,1024]{1,0:T(8,128)(2,1)S(1)} collective-permute-done((bf16[384,1024]{1,0:T(8,128)(2,1)S(1)}, bf16[384,1024]{1,0:T(8,128)(2,1)S(1)}, u32[]{:S(2)}, u32[]{:S(2)}) %collective-permute-start.4) | collective-permute-done | bytes 786464 | tf_op jit(solution)/shard_map/ppermute | solution.py:159
  85.1 4.2 %collective-permute-start.6 = (bf16[384,1024]{1,0:T(8,128)(2,1)S(1)}, bf16[384,1024]{1,0:T(8,128)(2,1)}, u32[]{:S(2)}, u32[]{:S(2)}) collective-permute-start(bf16[384,1024]{1,0:T(8,128)(2,1)S(1)} %collective-permute-done.4), channel_id=1, source_target_pairs={{0,4},{4,8},{8,12},{12,16},{16,20},{20,24},{24,28},{28,0},{1,5},{5... | collective-permute-start | bytes 2359304 | tf_op jit(solution)/shard_map/ppermute | solution.py:159
  89.3 1.9 %collective-permute-start.7 = (bf16[384,1024]{1,0:T(8,128)(2,1)S(1)}, bf16[384,1024]{1,0:T(8,128)(2,1)}, u32[]{:S(2)}, u32[]{:S(2)}) collective-permute-start(bf16[384,1024]{1,0:T(8,128)(2,1)S(1)} %collective-permute-done.5), channel_id=1, source_target_pairs={{0,28},{4,0},{8,4},{12,8},{16,12},{20,16},{24,20},{28,24},{1,29},{... | collective-permute-start | bytes 2359304 | tf_op jit(solution)/shard_map/ppermute | solution.py:160
  91.4 12.5 %collective-permute-done.6 = bf16[384,1024]{1,0:T(8,128)(2,1)} collective-permute-done((bf16[384,1024]{1,0:T(8,128)(2,1)S(1)}, bf16[384,1024]{1,0:T(8,128)(2,1)}, u32[]{:S(2)}, u32[]{:S(2)}) %collective-permute-start.6) | collective-permute-done | bytes 786464 | tf_op jit(solution)/shard_map/ppermute | solution.py:159
  103.9 3.7 %collective-permute-start.8 = (bf16[384,1024]{1,0:T(8,128)(2,1)}, bf16[384,1024]{1,0:T(8,128)(2,1)S(1)}, u32[]{:S(2)}, u32[]{:S(2)}) collective-permute-start(bf16[384,1024]{1,0:T(8,128)(2,1)} %collective-permute-done.6), channel_id=1, source_target_pairs={{0,4},{4,8},{8,12},{12,16},{16,20},{20,24},{24,28},{28,0},{1,5},{5... | collective-permute-start | bytes 2359304 | tf_op jit(solution)/shard_map/ppermute | solution.py:159
  107.7 2.1 %collective-permute-start.9 = (bf16[384,1024]{1,0:T(8,128)(2,1)}, bf16[384,1024]{1,0:T(8,128)(2,1)S(1)}, u32[]{:S(2)}, u32[]{:S(2)}) collective-permute-start(bf16[384,1024]{1,0:T(8,128)(2,1)} %collective-permute-done.7), channel_id=1, source_target_pairs={{0,28},{4,0},{8,4},{12,8},{16,12},{20,16},{24,20},{28,24},{1,29},{... | collective-permute-start | bytes 2359304 | tf_op jit(solution)/shard_map/ppermute | solution.py:160
  109.8 0.8 reshape.246.gate_ref
  110.6 0.7 concatenate.14
  111.3 1.3 add_select_fusion.qidx_ref
  112.6 0.9 constant_dynamic-update-slice_fusion.12
  113.5 2.1 %constant_dynamic-update-slice_fusion.11 = bf16[3072,1024]{1,0:T(8,128)(2,1)} fusion(bf16[3072,1024]{1,0:T(8,128)(2,1)} %constant_dynamic-update-slice_fusion.12, bf16[384,1024]{1,0:T(8,128)(2,1)} %copy-done.1), kind=kLoop, calls=%fused_computation.20 | loop fusion | bytes 1572864
  115.6 2.1 %constant_dynamic-update-slice_fusion.10 = bf16[3072,1024]{1,0:T(8,128)(2,1)} fusion(bf16[3072,1024]{1,0:T(8,128)(2,1)} %constant_dynamic-update-slice_fusion.11, bf16[384,1024]{1,0:T(8,128)(2,1)} %collective-permute-done.6), kind=kLoop, calls=%fused_computation.19 | loop fusion | bytes 1572864
  117.7 4.3 %collective-permute-done.8 = bf16[384,1024]{1,0:T(8,128)(2,1)S(1)} collective-permute-done((bf16[384,1024]{1,0:T(8,128)(2,1)}, bf16[384,1024]{1,0:T(8,128)(2,1)S(1)}, u32[]{:S(2)}, u32[]{:S(2)}) %collective-permute-start.8) | collective-permute-done | bytes 786464 | tf_op jit(solution)/shard_map/ppermute | solution.py:159
  122.0 3.4 %collective-permute-start.10 = (bf16[192,1024]{1,0:T(8,128)(2,1)S(1)}, bf16[192,1024]{1,0:T(8,128)(2,1)S(1)}, u32[]{:S(2)}, u32[]{:S(2)}) collective-permute-start(bf16[192,1024]{1,0:T(8,128)(2,1)S(1)} %slice.32), channel_id=1, source_target_pairs={{0,4},{4,8},{8,12},{12,16},{16,20},{20,24},{24,28},{28,0},{1,5},{5... | collective-permute-start | bytes 1179656 | tf_op jit(solution)/shard_map/ppermute | solution.py:163
  125.4 2.4 %collective-permute-start.11 = (bf16[192,1024]{1,0:T(8,128)(2,1)S(1)}, bf16[192,1024]{1,0:T(8,128)(2,1)S(1)}, u32[]{:S(2)}, u32[]{:S(2)}) collective-permute-start(bf16[192,1024]{1,0:T(8,128)(2,1)S(1)} %slice.33), channel_id=1, source_target_pairs={{0,28},{4,0},{8,4},{12,8},{16,12},{20,16},{24,20},{28,24},{1,29},{... | collective-permute-start | bytes 1179656 | tf_op jit(solution)/shard_map/ppermute | solution.py:164
  127.9 2.1 %constant_dynamic-update-slice_fusion.9 = bf16[3072,1024]{1,0:T(8,128)(2,1)} fusion(bf16[3072,1024]{1,0:T(8,128)(2,1)} %constant_dynamic-update-slice_fusion.10, bf16[384,1024]{1,0:T(8,128)(2,1)} %collective-permute-done.7), kind=kLoop, calls=%fused_computation.18 | loop fusion | bytes 1572864
  129.9 0.9 constant_dynamic-update-slice_fusion.8
  130.9 1.0 constant_dynamic-update-slice_fusion.7
  131.8 0.8 constant_dynamic-update-slice_fusion.6
  132.6 3.7 %collective-permute-done.11 = bf16[192,1024]{1,0:T(8,128)(2,1)S(1)} collective-permute-done((bf16[192,1024]{1,0:T(8,128)(2,1)S(1)}, bf16[192,1024]{1,0:T(8,128)(2,1)S(1)}, u32[]{:S(2)}, u32[]{:S(2)}) %collective-permute-start.11) | collective-permute-done | bytes 393248 | tf_op jit(solution)/shard_map/ppermute | solution.py:164
  136.3 0.8 constant_dynamic-update-slice_fusion.5.k_ref.v_ref
  137.1 28.1 %shard_map.46 = bf16[288,2048]{1,0:T(8,128)(2,1)} custom-call(s32[288,1]{1,0:T(8,128)} %add_select_fusion.qidx_ref, s32[1,3072]{1,0:T(1,128)} %bitcast.22, f32[288,1]{1,0:T(8,128)} %reshape.246.gate_ref, bf16[288,2048]{1,0:T(8,128)(2,1)} %q_ref.1, bf16[3072,1024]{1,0:T(8,128)(2,1)} %constant_dynamic-update-slice_fusion.5.k_ref.v_ref, ...), custom_call_target="tpu_custom_call" | custom-call | tf_op jit(solution)/shard_map/pallas_call | solution.py:95
  (48 shorter events, 0.6 us)
Async XLA Ops:
  0.0 5.2 %copy-start = (bf16[288,1024]{1,0:T(8,128)(2,1)S(1)}, bf16[288,1024]{1,0:T(8,128)(2,1)}, u32[]{:S(2)}) copy-start(bf16[288,1024]{1,0:T(8,128)(2,1)} %param.6) | copy-start | bytes 1769476
  7.3 102.5 %copy-start.2 = (bf16[288]{0:T(512)(128)(2,1)S(1)}, bf16[288]{0:T(512)(128)(2,1)}, u32[]{:S(2)}) copy-start(bf16[288]{0:T(512)(128)(2,1)} %param.7) | copy-start | bytes 1732
  10.6 35.1 %all-to-all-start = ((bf16[32,10,1024]{2,1,0:T(8,128)(2,1)}), bf16[32,10,1024]{2,1,0:T(8,128)(2,1)S(1)}, u32[]{:S(2)}, u32[]{:S(2)}) async-start(bf16[32,10,1024]{2,1,0:T(8,128)(2,1)} %select_select_fusion), calls=%async_computation | async-start | bytes 2097152 | tf_op jit(solution)/shard_map/all_to_all | solution.py:119
  46.9 8.8 %collective-permute-start = (bf16[96,1024]{1,0:T(8,128)(2,1)S(1)}, bf16[96,1024]{1,0:T(8,128)(2,1)S(1)}, u32[]{:S(2)}, u32[]{:S(2)}) collective-permute-start(bf16[96,1024]{1,0:T(8,128)(2,1)S(1)} %get-tuple-element.6), channel_id=1, source_target_pairs={{0,1},{1,2},{2,3},{3,0},{4,5},{5,6},{6,7},{7,4},{8,9},{9,10},{10,1... | collective-permute-start | bytes 589832 | tf_op jit(solution)/shard_map/ppermute | solution.py:128
  48.8 8.8 %collective-permute-start.1 = (bf16[96,1024]{1,0:T(8,128)(2,1)S(1)}, bf16[96,1024]{1,0:T(8,128)(2,1)S(1)}, u32[]{:S(2)}, u32[]{:S(2)}) collective-permute-start(bf16[96,1024]{1,0:T(8,128)(2,1)S(1)} %get-tuple-element.6), channel_id=1, source_target_pairs={{0,3},{1,0},{2,1},{3,2},{4,7},{5,4},{6,5},{7,6},{8,11},{9,8},{10,9... | collective-permute-start | bytes 589832 | tf_op jit(solution)/shard_map/ppermute | solution.py:129
  55.7 8.5 %collective-permute-start.2 = (bf16[48,1024]{1,0:T(8,128)(2,1)S(1)}, bf16[48,1024]{1,0:T(8,128)(2,1)S(1)}, u32[]{:S(2)}, u32[]{:S(2)}) collective-permute-start(bf16[48,1024]{1,0:T(8,128)(2,1)S(1)} %slice.30), channel_id=1, source_target_pairs={{0,1},{1,2},{2,3},{3,0},{4,5},{5,6},{6,7},{7,4},{8,9},{9,10},{10,1... | collective-permute-start | bytes 294920 | tf_op jit(solution)/shard_map/ppermute | solution.py:130
  57.6 7.3 %collective-permute-start.3 = (bf16[48,1024]{1,0:T(8,128)(2,1)S(1)}, bf16[48,1024]{1,0:T(8,128)(2,1)S(1)}, u32[]{:S(2)}, u32[]{:S(2)}) collective-permute-start(bf16[48,1024]{1,0:T(8,128)(2,1)S(1)} %slice.31), channel_id=1, source_target_pairs={{0,3},{1,0},{2,1},{3,2},{4,7},{5,4},{6,5},{7,6},{8,11},{9,8},{10,9... | collective-permute-start | bytes 294920 | tf_op jit(solution)/shard_map/ppermute | solution.py:131
  65.6 19.5 %collective-permute-start.4 = (bf16[384,1024]{1,0:T(8,128)(2,1)S(1)}, bf16[384,1024]{1,0:T(8,128)(2,1)S(1)}, u32[]{:S(2)}, u32[]{:S(2)}) collective-permute-start(bf16[384,1024]{1,0:T(8,128)(2,1)S(1)} %get-tuple-element.11), channel_id=1, source_target_pairs={{0,4},{4,8},{8,12},{12,16},{16,20},{20,24},{24,28},{28,0},{1,5},{5... | collective-permute-start | bytes 2359304 | tf_op jit(solution)/shard_map/ppermute | solution.py:159
  70.2 19.1 %collective-permute-start.5 = (bf16[384,1024]{1,0:T(8,128)(2,1)S(1)}, bf16[384,1024]{1,0:T(8,128)(2,1)S(1)}, u32[]{:S(2)}, u32[]{:S(2)}) collective-permute-start(bf16[384,1024]{1,0:T(8,128)(2,1)S(1)} %get-tuple-element.11), channel_id=1, source_target_pairs={{0,28},{4,0},{8,4},{12,8},{16,12},{20,16},{24,20},{28,24},{1,29},{... | collective-permute-start | bytes 2359304 | tf_op jit(solution)/shard_map/ppermute | solution.py:160
  85.1 18.8 %collective-permute-start.6 = (bf16[384,1024]{1,0:T(8,128)(2,1)S(1)}, bf16[384,1024]{1,0:T(8,128)(2,1)}, u32[]{:S(2)}, u32[]{:S(2)}) collective-permute-start(bf16[384,1024]{1,0:T(8,128)(2,1)S(1)} %collective-permute-done.4), channel_id=1, source_target_pairs={{0,4},{4,8},{8,12},{12,16},{16,20},{20,24},{24,28},{28,0},{1,5},{5... | collective-permute-start | bytes 2359304 | tf_op jit(solution)/shard_map/ppermute | solution.py:159
  89.3 18.4 %copy-start.1 = (bf16[384,1024]{1,0:T(8,128)(2,1)}, bf16[384,1024]{1,0:T(8,128)(2,1)S(1)}, u32[]{:S(2)}) copy-start(bf16[384,1024]{1,0:T(8,128)(2,1)S(1)} %collective-permute-done.5) | copy-start | bytes 2359300
  89.3 18.4 %collective-permute-start.7 = (bf16[384,1024]{1,0:T(8,128)(2,1)S(1)}, bf16[384,1024]{1,0:T(8,128)(2,1)}, u32[]{:S(2)}, u32[]{:S(2)}) collective-permute-start(bf16[384,1024]{1,0:T(8,128)(2,1)S(1)} %collective-permute-done.5), channel_id=1, source_target_pairs={{0,28},{4,0},{8,4},{12,8},{16,12},{20,16},{24,20},{28,24},{1,29},{... | collective-permute-start | bytes 2359304 | tf_op jit(solution)/shard_map/ppermute | solution.py:160
  103.9 18.0 %collective-permute-start.8 = (bf16[384,1024]{1,0:T(8,128)(2,1)}, bf16[384,1024]{1,0:T(8,128)(2,1)S(1)}, u32[]{:S(2)}, u32[]{:S(2)}) collective-permute-start(bf16[384,1024]{1,0:T(8,128)(2,1)} %collective-permute-done.6), channel_id=1, source_target_pairs={{0,4},{4,8},{8,12},{12,16},{16,20},{20,24},{24,28},{28,0},{1,5},{5... | collective-permute-start | bytes 2359304 | tf_op jit(solution)/shard_map/ppermute | solution.py:159
  107.7 17.7 %collective-permute-start.9 = (bf16[384,1024]{1,0:T(8,128)(2,1)}, bf16[384,1024]{1,0:T(8,128)(2,1)S(1)}, u32[]{:S(2)}, u32[]{:S(2)}) collective-permute-start(bf16[384,1024]{1,0:T(8,128)(2,1)} %collective-permute-done.7), channel_id=1, source_target_pairs={{0,28},{4,0},{8,4},{12,8},{16,12},{20,16},{24,20},{28,24},{1,29},{... | collective-permute-start | bytes 2359304 | tf_op jit(solution)/shard_map/ppermute | solution.py:160
  122.0 9.9 %collective-permute-start.10 = (bf16[192,1024]{1,0:T(8,128)(2,1)S(1)}, bf16[192,1024]{1,0:T(8,128)(2,1)S(1)}, u32[]{:S(2)}, u32[]{:S(2)}) collective-permute-start(bf16[192,1024]{1,0:T(8,128)(2,1)S(1)} %slice.32), channel_id=1, source_target_pairs={{0,4},{4,8},{8,12},{12,16},{16,20},{20,24},{24,28},{28,0},{1,5},{5... | collective-permute-start | bytes 1179656 | tf_op jit(solution)/shard_map/ppermute | solution.py:163
  125.4 10.9 %collective-permute-start.11 = (bf16[192,1024]{1,0:T(8,128)(2,1)S(1)}, bf16[192,1024]{1,0:T(8,128)(2,1)S(1)}, u32[]{:S(2)}, u32[]{:S(2)}) collective-permute-start(bf16[192,1024]{1,0:T(8,128)(2,1)S(1)} %slice.33), channel_id=1, source_target_pairs={{0,28},{4,0},{8,4},{12,8},{16,12},{20,16},{24,20},{28,24},{1,29},{... | collective-permute-start | bytes 1179656 | tf_op jit(solution)/shard_map/ppermute | solution.py:164
